TPU v7x, 512 devices: a whole 4x4x16 slice. The times are simulated.
512 devices in a mesh: row: 32 (over z, core), col: 16 (over y, x).
Axes of the slice: x: 4, y: 4, z: 16, core: 2. Of those that a mesh axis runs over, the one named last changes fastest.
Arguments:
- block_input: bfloat16 [8192, 3072], P('row', 'col'), may hold values from -5 to 5
- conv_out: bfloat16 [8192, 3072], P('row', 'col'), may hold values from -100 to 100
- hidden_pre: bfloat16 [8192, 6144], P('row', 'col'), may hold values from -6 to 6
- cotangent: bfloat16 [8192, 3072], P('row', 'col'), may hold values from -16 to 16
- conv_kernel: float32 [49, 3072], P(None, ('col', 'row')), may hold values from -0.875 to 0.875
- norm_gain: float32 [3072], replicated, may hold values from 0.25 to 1.75
- norm_bias: float32 [3072], replicated, may hold values from -3 to 3
- layer_scale: float32 [3072], P('col'), may hold values from 0.3 to 3
- w_in: bfloat16 [3072, 6144], P('row', 'col'), may hold values from -0.109375 to 0.109375
- w_out: bfloat16 [3072, 6144], P('row', 'col'), may hold values from -0.078125 to 0.078125
Outputs:
- d_input: bfloat16 [8192, 3072], P('row', 'col')
- d_kernel: float32 [49, 3072], P(None, ('col', 'row'))
- d_gain: float32 [3072], P('col')
- d_bias: float32 [3072], P('col')
- d_w_in: bfloat16 [3072, 6144], P('row', 'col')
All inputs are finite; a program needn't handle non-finite values.
Results may differ from a plain program's by a relative error of at most 0.02.
Values may be sent and summed in bfloat16 or wider, within the bound.
No kernel may reach another device: no remote copies, remote signals or barrier semaphores. Data moves between devices by JAX's collectives and lax.ppermute only.
A program may use at most 64 MiB of HBM per device.

v0:
```python
import jax
import jax.numpy as jnp
from jax import lax
from jax.sharding import PartitionSpec as P

KS = 7
H = 64


def gelu_slope(values):
    cdf = 0.5 * (1.0 + lax.erf(values * 0.7071067811865476))
    density = jnp.exp(-0.5 * values * values) * 0.3989422804014327
    return cdf + values * density


def lane_taps(grads_flat, inputs_flat, kernel, count, few):
    lanes = H * few
    spread = ((0, 0), (3, 3), (3 * few, 3 * few))
    grads_pad = jnp.pad(grads_flat.astype(jnp.float32).reshape(count, H, lanes), spread)
    inputs_pad = jnp.pad(inputs_flat.astype(jnp.float32).reshape(count, H, lanes), spread)
    kernel_wide = jnp.tile(kernel, (1, H))
    centre = grads_pad[:, 3 : 3 + H, 3 * few : 3 * few + lanes]
    moved = jnp.zeros((count, H, lanes), jnp.float32)
    kernel_rows = []
    for tap in range(KS * KS):
        down = tap // KS
        across = tap % KS
        lead = (6 - across) * few
        moved = (
            moved + kernel_wide[tap] * grads_pad[:, 6 - down : 6 - down + H, lead : lead + lanes]
        )
        totals = jnp.sum(
            centre * inputs_pad[:, down : down + H, across * few : across * few + lanes],
            axis=(0, 1),
        )
        kernel_rows.append(jnp.sum(totals.reshape(H, few), axis=0))
    return (moved.reshape(count * H * H, few), jnp.stack(kernel_rows))


def body(
    block_input,
    conv_out,
    hidden_pre,
    cotangent,
    conv_kernel,
    norm_gain,
    norm_bias,
    layer_scale,
    w_in,
    w_out,
):
    channels = block_input.shape[1]
    width = norm_gain.shape[0]
    col_rank = lax.axis_index("col")
    scaled = (cotangent.astype(jnp.float32) * layer_scale).astype(jnp.bfloat16)
    scaled_full, inputs_full = (
        lax.all_gather(scaled, "col", axis=1, tiled=True),
        lax.all_gather(conv_out, "col", axis=1, tiled=True),
    )
    values = inputs_full.astype(jnp.float32)
    mean = jnp.mean(values, axis=1, keepdims=True)
    centred = values - mean
    rstd = lax.rsqrt(jnp.mean(centred * centred, axis=1, keepdims=True) + 1e-06)
    zhat_full = centred * rstd
    normed_full = (zhat_full * norm_gain + norm_bias).astype(jnp.bfloat16)
    zhat_own = lax.dynamic_slice_in_dim(zhat_full, col_rank * channels, channels, 1)
    gain_own = lax.dynamic_slice_in_dim(norm_gain, col_rank * channels, channels, 0)
    contract_last = (((1,), (1,)), ((), ()))
    columns = scaled_full
    grad_act = jnp.dot(
        columns,
        lax.all_gather(w_out, "row", axis=0, tiled=True),
        preferred_element_type=jnp.float32,
    )
    grad_pre = (grad_act * gelu_slope(hidden_pre.astype(jnp.float32))).astype(jnp.bfloat16)
    columns = normed_full
    d_w_in = lax.psum_scatter(
        lax.dot_general(
            columns, grad_pre, (((0,), (0,)), ((), ())), preferred_element_type=jnp.float32
        ).astype(jnp.bfloat16),
        "row",
        scatter_dimension=0,
        tiled=True,
    )
    partial_sum = lax.dot_general(
        grad_pre,
        lax.all_gather(w_in, "row", axis=0, tiled=True),
        contract_last,
        preferred_element_type=jnp.float32,
    )
    grad_norm = lax.psum_scatter(
        partial_sum.astype(jnp.bfloat16), "col", scatter_dimension=1, tiled=True
    ).astype(jnp.float32)
    dzhat = grad_norm * gain_own
    first_sum, second_sum = lax.psum(
        (jnp.sum(dzhat, axis=1), jnp.sum(dzhat * zhat_own, axis=1)), "col"
    )
    first = first_sum[:, None] / width
    second = second_sum[:, None] / width
    grad_conv = (rstd * (dzhat - first - zhat_own * second)).astype(jnp.bfloat16)
    d_gain, d_bias = lax.psum(
        (jnp.sum(grad_norm * zhat_own, axis=0), jnp.sum(grad_norm, axis=0)), "row"
    )
    images_grad, images_input = (
        lax.all_to_all(grad_conv, "row", split_axis=1, concat_axis=0, tiled=True),
        lax.all_to_all(block_input, "row", split_axis=1, concat_axis=0, tiled=True),
    )
    count = images_grad.shape[0] // (H * H)
    few = images_grad.shape[1]
    moved, d_kernel = lane_taps(images_grad, images_input, conv_kernel, count, few)
    back = lax.all_to_all(
        moved.astype(jnp.bfloat16), "row", split_axis=0, concat_axis=1, tiled=True
    ).astype(moved.dtype)
    d_input = (back + cotangent.astype(jnp.float32)).astype(jnp.bfloat16)
    return (d_input, d_kernel, d_gain, d_bias, d_w_in)


def solution(mesh):
    return jax.shard_map(
        body,
        mesh=mesh,
        in_specs=(
            P("row", "col"),
            P("row", "col"),
            P("row", "col"),
            P("row", "col"),
            P(None, ("col", "row")),
            P(),
            P(),
            P("col"),
            P("row", "col"),
            P("row", "col"),
        ),
        out_specs=(P("row", "col"), P(None, ("col", "row")), P("col"), P("col"), P("row", "col")),
        check_vma=False,
    )
```

profile of v0, /device:TPU:1, one launch (start us, length us, event | category | flops | bytes accessed | tf_op | source)
XLA Modules:
  0.0 540.3 jit_solution(10087494805711800408)
XLA Ops:
  7.2 1.6 fusion.16
  8.9 0.7 all-gather.9.cloned.1.call-update
  9.7 0.7 all-gather.11.cloned.1.call-update
  11.0 64.3 %all-gather.7.cloned.1.call-done = bf16[256,3072]{0,1:T(8,128)(2,1)} async-done(((bf16[256,192]{0,1:T(8,128)(2,1)}), bf16[256,3072]{0,1:T(8,128)(2,1)}) %all-gather.7.cloned.1.call-update) | async-done | bytes 1572880 | tf_op jit(solution)/shard_map/all_gather | solution.py:57
  75.2 75.3 %all-gather.9.cloned.1.call-done = bf16[3072,384]{1,0:T(8,128)(2,1)} async-done(((bf16[96,384]{1,0:T(8,128)(2,1)}), bf16[3072,384]{1,0:T(8,128)(2,1)}) %all-gather.9.cloned.1.call-update) | async-done | bytes 2359312 | tf_op jit(solution)/shard_map/all_gather | solution.py:72
  150.5 3.2 fusion.5
  153.7 68.2 %all-gather.11.cloned.1.call-done = bf16[3072,384]{1,0:T(8,128)(2,1)} async-done(((bf16[96,384]{1,0:T(8,128)(2,1)}), bf16[3072,384]{1,0:T(8,128)(2,1)}) %all-gather.11.cloned.1.call-update) | async-done | bytes 2359312 | tf_op jit(solution)/shard_map/all_gather | solution.py:87
  221.9 3.8 convolution_convert_fusion.1
  225.8 53.8 %all-gather.5.cloned.1.call-done = bf16[256,3072]{0,1:T(8,128)(2,1)} async-done(((bf16[256,192]{0,1:T(8,128)(2,1)}), bf16[256,3072]{0,1:T(8,128)(2,1)}) %all-gather.5.cloned.1.call-update) | async-done | bytes 1572880 | tf_op jit(solution)/shard_map/all_gather | solution.py:58
  279.6 1.9 convert_reduce_fusion
  281.6 1.9 fusion.2
  283.5 2.9 convolution_convert_fusion
  287.2 13.9 %all-to-all-start.2 = ((bf16[256,32,6]{0,2,1:T(8,128)(2,1)}), bf16[256,32,6]{0,2,1:T(8,128)(2,1)S(1)}, u32[]{:S(2)}, u32[]{:S(2)}) async-start(bf16[256,32,6]{0,2,1:T(8,128)(2,1)} %all_to_all.31), calls=%async_computation.3 | async-start | bytes 262144 | tf_op jit(solution)/shard_map/all_to_all | solution.py:106
  301.7 2.0 fusion
  303.7 67.8 %reduce-scatter.3.cloned.1.call-done = bf16[256,192]{0,1:T(8,128)(2,1)} async-done(((bf16[256,3072]{0,1:T(8,128)(2,1)}), bf16[256,192]{0,1:T(8,128)(2,1)}) %reduce-scatter.3.cloned.1.call-update) | async-done | bytes 98320 | tf_op jit(solution)/shard_map/reduce_scatter | solution.py:91
  371.4 1.2 fusion.22
  372.6 30.9 %all-reduce.3 = (f32[256]{0:T(256)S(1)}, f32[256]{0:T(256)S(1)}) all-reduce(f32[256]{0:T(256)S(1)} %get-tuple-element.16, f32[256]{0:T(256)S(1)} %get-tuple-element.66), channel_id=1, replica_groups=mesh['row'=32,'col'=16] {'col'}, use_global_device_ids=true, to_apply=%region_6.0 | all-reduce | flops 512 | bytes 4096 | tf_op jit(solution)/shard_map/psum | solution.py:95
  403.5 1.1 fusion.20
  404.6 0.7 all_to_all.13
  405.2 21.9 %all-to-all-start = ((bf16[256,32,6]{0,2,1:T(8,128)(2,1)}), bf16[256,32,6]{0,2,1:T(8,128)(2,1)S(1)}, u32[]{:S(2)}, u32[]{:S(2)}) async-start(bf16[256,32,6]{0,2,1:T(8,128)(2,1)} %all_to_all.13), calls=%async_computation.1 | async-start | bytes 262144 | tf_op jit(solution)/shard_map/all_to_all | solution.py:105
  435.4 2.7 copy.22
  438.1 4.0 reshape.498
  442.1 46.5 %all-reduce.2 = (f32[192]{0:T(256)}, f32[192]{0:T(256)}) all-reduce(f32[192]{0:T(256)S(1)} %get-tuple-element.15, f32[192]{0:T(256)S(1)} %get-tuple-element.67), channel_id=1, replica_groups=mesh['row'=32,'col'=16] {'row'}, use_global_device_ids=true, to_apply=%region_106.107 | all-reduce | flops 384 | bytes 3072 | tf_op jit(solution)/shard_map/psum | solution.py:101
  488.6 2.7 copy.20
  491.3 4.0 reshape.496
  495.2 2.3 fusion.116
  497.6 4.6 convert_element_type.85
  502.2 1.5 copy.21
  503.8 12.8 %all-to-all-start.1 = ((bf16[32,256,6]{1,2,0:T(8,128)(2,1)}), bf16[32,256,6]{1,2,0:T(8,128)(2,1)S(1)}, u32[]{:S(2)}, u32[]{:S(2)}) async-start(bf16[32,256,6]{1,2,0:T(8,128)(2,1)} %copy.21), calls=%async_computation.2 | async-start | bytes 262144 | tf_op jit(solution)/shard_map/all_to_all | solution.py:111
  520.6 0.9 fusion.179
  526.3 0.9 fusion.215
  532.0 0.7 stack.199
  (285 shorter events, 23.8 us)
Async XLA Ops:
  7.2 68.1 %all-gather.7.cloned.1.call-start = ((), (), s32[]{:S(2)}) async-start(), calls=%async_computation.6 | async-start | bytes 1671168 | tf_op jit(solution)/shard_map/all_gather | solution.py:57
  8.9 141.6 %all-gather.9.cloned.1.call-start = ((), (), s32[]{:S(2)}) async-start(), calls=%async_computation.7 | async-start | bytes 2433024 | tf_op jit(solution)/shard_map/all_gather | solution.py:72
  9.6 212.3 %all-gather.11.cloned.1.call-start = ((), (), s32[]{:S(2)}) async-start(), calls=%async_computation.8 | async-start | bytes 2433024 | tf_op jit(solution)/shard_map/all_gather | solution.py:87
  10.4 269.3 %all-gather.5.cloned.1.call-start = ((), (), s32[]{:S(2)}) async-start(), calls=%async_computation.5 | async-start | bytes 1671168 | tf_op jit(solution)/shard_map/all_gather | solution.py:58
  10.9 360.5 %reduce-scatter.3.cloned.1.call-start = ((), (), s32[]{:S(2)}) async-start(), calls=%async_computation.9 | async-start | bytes 1671168 | tf_op jit(solution)/shard_map/reduce_scatter | solution.py:91
  225.7 57.7 %copy-start.4 = (f32[3072]{0:T(1024)S(1)}, f32[3072]{0:T(1024)}, u32[]{:S(2)}) copy-start(f32[3072]{0:T(1024)} %param.15) | copy-start | bytes 36868
  225.7 57.7 %copy-start.5 = (f32[3072]{0:T(1024)S(1)}, f32[3072]{0:T(1024)}, u32[]{:S(2)}) copy-start(f32[3072]{0:T(1024)} %param.16) | copy-start | bytes 36868
  225.8 307.7 %reduce-scatter.5.cloned.1.call-start = ((), (), s32[]{:S(2)}) async-start(), calls=%async_computation.10 | async-start | bytes 2433024 | tf_op jit(solution)/shard_map/reduce_scatter | solution.py:77
  279.6 3.9 copy-start
  283.5 3.0 copy-start.3
  283.5 17.7 %copy-start.1 = (f32[49,6]{0,1:T(8,128)S(1)}, f32[49,6]{0,1:T(8,128)}, u32[]{:S(2)}) copy-start(f32[49,6]{0,1:T(8,128)} %param.14) | copy-start | bytes 3532
  287.2 118.1 %all-to-all-start.2 = ((bf16[256,32,6]{0,2,1:T(8,128)(2,1)}), bf16[256,32,6]{0,2,1:T(8,128)(2,1)S(1)}, u32[]{:S(2)}, u32[]{:S(2)}) async-start(bf16[256,32,6]{0,2,1:T(8,128)(2,1)} %all_to_all.31), calls=%async_computation.3 | async-start | bytes 262144 | tf_op jit(solution)/shard_map/all_to_all | solution.py:106
  405.2 83.3 %all-to-all-start = ((bf16[256,32,6]{0,2,1:T(8,128)(2,1)}), bf16[256,32,6]{0,2,1:T(8,128)(2,1)S(1)}, u32[]{:S(2)}, u32[]{:S(2)}) async-start(bf16[256,32,6]{0,2,1:T(8,128)(2,1)} %all_to_all.13), calls=%async_computation.1 | async-start | bytes 262144 | tf_op jit(solution)/shard_map/all_to_all | solution.py:105
  503.8 29.0 %copy-start.2 = (bf16[256,192]{0,1:T(8,128)(2,1)S(1)}, bf16[256,192]{0,1:T(8,128)(2,1)}, u32[]{:S(2)}) copy-start(bf16[256,192]{0,1:T(8,128)(2,1)} %param.13) | copy-start | bytes 294916
  503.8 28.9 %all-to-all-start.1 = ((bf16[32,256,6]{1,2,0:T(8,128)(2,1)}), bf16[32,256,6]{1,2,0:T(8,128)(2,1)S(1)}, u32[]{:S(2)}, u32[]{:S(2)}) async-start(bf16[32,256,6]{1,2,0:T(8,128)(2,1)} %copy.21), calls=%async_computation.2 | async-start | bytes 262144 | tf_op jit(solution)/shard_map/all_to_all | solution.py:111
Sparse Core Ops, SparseCore 0:
  11.6 63.5 all-gather.6
  77.3 73.1 all-gather.8
  152.6 69.2 all-gather.10
  224.8 54.8 all-gather.4
  283.6 87.8 reduce-scatter.2
  374.7 112.0 reduce-scatter.4
where the time goes:
time: 541 us; the launch traced here: 540 us
  waiting for transfers between devices  331 us (61%)
  blocking collectives  77.3 us (14%)
  starting transfers between devices  48.8 us (9%)
  local copies, waits for them, and re-layouts  41.2 us (8%)
  other arithmetic  16.5 us (3%)
  between operations  15.1 us (3%)
  matrix products  9.97 us (2%)
    all_gather x1, waiting for transfers between devices, body(): lax.all_gather(w_out, 'row', axis=0, tiled=True)  75.3 us
    all_gather x1, waiting for transfers between devices, body(): lax.all_gather(w_in, 'row', axis=0, tiled=True)  68.2 us
    reduce_scatter x1, waiting for transfers between devices, body(): lax.psum_scatter(partial_sum.astype(jnp.bfloat16), 'col', scatter_dimensi...  67.8 us
    all_gather x1, waiting for transfers between devices, body(): lax.all_gather(scaled, 'col', axis=1, tiled=True)  64.3 us
    all_gather x1, waiting for transfers between devices, body(): lax.all_gather(conv_out, 'col', axis=1, tiled=True)  53.8 us
    psum x1, blocking collectives, body(): lax.psum((jnp.sum(grad_norm * zhat_own, axis=0), jnp.sum(grad_norm, axis=...  46.5 us
    psum x1, blocking collectives, body(): lax.psum((jnp.sum(dzhat, axis=1), jnp.sum(dzhat * zhat_own, axis=1)), 'col')  30.9 us
    all_to_all x1, starting transfers between devices, body(): lax.all_to_all(grad_conv, 'row', split_axis=1, concat_axis=0, tiled=True)  21.9 us
  transfers between devices with their start and end apart: 9, of which 5 were waited for; matrix products, arithmetic and copies ran while one was open for 12% of the time, Pallas kernels for 0%

commit v1 on v0

v1 whole, which is shorter than its diff:
```python
import jax
import jax.numpy as jnp
from jax import lax
from jax.sharding import PartitionSpec as P

KS = 7
H = 64
HALO = KS // 2

WEIGHTS_VIA = "gather"
DWIN_VIA = "a2a"
ACTS_VIA = "a2a"


def gelu_slope(values):
    cdf = 0.5 * (1.0 + lax.erf(values * 0.7071067811865476))
    density = jnp.exp(-0.5 * values * values) * 0.3989422804014327
    return cdf + values * density


def gather_blocks(x, axis_name, size, via):
    if via == "a2a":
        wide = jnp.broadcast_to(x[None], (size,) + x.shape)
        return lax.all_to_all(wide, axis_name, 0, 0, tiled=True)
    return lax.all_gather(x, axis_name, axis=0, tiled=False)


def split_hi_lo(values):
    high = lax.reduce_precision(values, exponent_bits=8, mantissa_bits=7)
    low = values - high
    return high.astype(jnp.bfloat16), low.astype(jnp.bfloat16)


def body(
    block_input,
    conv_out,
    hidden_pre,
    cotangent,
    conv_kernel,
    norm_gain,
    norm_bias,
    layer_scale,
    w_in,
    w_out,
):
    tokens, channels = block_input.shape
    width = norm_gain.shape[0]
    hidden = hidden_pre.shape[1]
    n_col = width // channels
    n_row = width // w_in.shape[0]
    few = conv_kernel.shape[1]
    rows = tokens // H
    col_rank = lax.axis_index("col")
    row_rank = lax.axis_index("row")

    scaled = (cotangent.astype(jnp.float32) * layer_scale).astype(jnp.bfloat16)
    acts = gather_blocks(jnp.concatenate([scaled, conv_out], axis=1), "col", n_col, ACTS_VIA)
    weights = gather_blocks(jnp.concatenate([w_out, w_in], axis=1), "row", n_row, WEIGHTS_VIA)
    kernel_rows_full = lax.all_gather(conv_kernel, "row", axis=1, tiled=True)
    scaled_full = jnp.transpose(acts[:, :, :channels], (1, 0, 2)).reshape(tokens, width)
    inputs_full = jnp.transpose(acts[:, :, channels:], (1, 0, 2)).reshape(tokens, width)
    w_out_full = weights[:, :, :hidden].reshape(width, hidden)
    w_in_full = weights[:, :, hidden:].reshape(width, hidden)

    values = inputs_full.astype(jnp.float32)
    mean = jnp.mean(values, axis=1, keepdims=True)
    centred = values - mean
    rstd = lax.rsqrt(jnp.mean(centred * centred, axis=1, keepdims=True) + 1e-06)
    zhat_full = centred * rstd
    normed_full = (zhat_full * norm_gain + norm_bias).astype(jnp.bfloat16)
    zhat_own = lax.dynamic_slice_in_dim(zhat_full, col_rank * channels, channels, 1)
    gain_own = lax.dynamic_slice_in_dim(norm_gain, col_rank * channels, channels, 0)

    grad_act = jnp.dot(scaled_full, w_out_full, preferred_element_type=jnp.float32)
    grad_pre = (grad_act * gelu_slope(hidden_pre.astype(jnp.float32))).astype(jnp.bfloat16)

    block_w = lax.dot_general(
        normed_full, grad_pre, (((0,), (0,)), ((), ())), preferred_element_type=jnp.float32
    ).astype(jnp.bfloat16)
    if DWIN_VIA == "a2a":
        parts_w = lax.all_to_all(
            block_w.reshape(n_row, width // n_row, hidden), "row", 0, 0, tiled=True
        )
        d_w_in = jnp.sum(parts_w.astype(jnp.float32), axis=0).astype(jnp.bfloat16)
    else:
        d_w_in = lax.psum_scatter(block_w, "row", scatter_dimension=0, tiled=True)

    block_n = lax.dot_general(
        grad_pre, w_in_full, (((1,), (1,)), ((), ())), preferred_element_type=jnp.float32
    ).astype(jnp.bfloat16)
    weighted = block_n.astype(jnp.float32) * norm_gain
    first_part = jnp.sum(weighted, axis=1)
    second_part = jnp.sum(weighted * zhat_full, axis=1)
    f_hi, f_lo = split_hi_lo(first_part)
    s_hi, s_lo = split_hi_lo(second_part)
    sums = jnp.stack([f_hi, f_lo, s_hi, s_lo], axis=1)
    outgoing = jnp.concatenate(
        [
            jnp.transpose(block_n.reshape(tokens, n_col, channels), (1, 0, 2)),
            jnp.broadcast_to(sums[None], (n_col, tokens, 4)),
        ],
        axis=2,
    )
    incoming = lax.all_to_all(outgoing, "col", 0, 0, tiled=True).astype(jnp.float32)
    grad_norm = jnp.sum(incoming[:, :, :channels], axis=0)
    totals = jnp.sum(incoming[:, :, channels:], axis=0)
    first = (totals[:, 0] + totals[:, 1])[:, None] / width
    second = (totals[:, 2] + totals[:, 3])[:, None] / width
    dzhat = grad_norm * gain_own
    grad_conv = (rstd * (dzhat - first - zhat_own * second)).astype(jnp.bfloat16)
    gain_part = jnp.sum(grad_norm * zhat_own, axis=0)
    bias_part = jnp.sum(grad_norm, axis=0)

    per_image = H // rows
    grid = grad_conv.reshape(rows, H, channels)
    down_pairs = [(i, i + 1) for i in range(n_row) if (i + 1) % per_image != 0]
    up_pairs = [(i + 1, i) for i in range(n_row) if (i + 1) % per_image != 0]
    from_above = lax.ppermute(grid[rows - HALO :], "row", down_pairs)
    from_below = lax.ppermute(grid[:HALO], "row", up_pairs)
    tall = jnp.concatenate([from_above, grid, from_below], axis=0).astype(jnp.float32)
    padded = jnp.pad(tall, ((0, 0), (HALO, HALO), (0, 0)))
    inputs = block_input.astype(jnp.float32).reshape(rows, H, channels)
    kernel_full = kernel_rows_full
    moved = jnp.zeros((rows, H, channels), jnp.float32)
    kernel_rows = []
    for tap in range(KS * KS):
        down = tap // KS
        across = tap % KS
        window = padded[
            2 * HALO - down : 2 * HALO - down + rows, 2 * HALO - across : 2 * HALO - across + H
        ]
        moved = moved + kernel_full[tap] * window
        kernel_rows.append(jnp.sum(window * inputs, axis=(0, 1)))
    d_input = (moved.reshape(tokens, channels) + cotangent.astype(jnp.float32)).astype(jnp.bfloat16)

    kernel_part = jnp.stack(kernel_rows).reshape(KS * KS, n_row, few)
    kernel_part = jnp.transpose(kernel_part, (1, 0, 2)).reshape(n_row, KS * KS * few)
    norm_part = jnp.broadcast_to(jnp.concatenate([gain_part, bias_part])[None], (n_row, 2 * channels))
    reduced = jnp.sum(
        lax.all_to_all(jnp.concatenate([kernel_part, norm_part], axis=1), "row", 0, 0, tiled=True),
        axis=0,
    )
    d_kernel = reduced[: KS * KS * few].reshape(KS * KS, few)
    d_gain = reduced[KS * KS * few : KS * KS * few + channels]
    d_bias = reduced[KS * KS * few + channels :]
    return (d_input, d_kernel, d_gain, d_bias, d_w_in)


def solution(mesh):
    return jax.shard_map(
        body,
        mesh=mesh,
        in_specs=(
            P("row", "col"),
            P("row", "col"),
            P("row", "col"),
            P("row", "col"),
            P(None, ("col", "row")),
            P(),
            P(),
            P("col"),
            P("row", "col"),
            P("row", "col"),
        ),
        out_specs=(P("row", "col"), P(None, ("col", "row")), P("col"), P("col"), P("row", "col")),
        check_vma=False,
    )
```

time: 541 us -> 377 us (0.70)
  waiting for transfers between devices: 331 us -> 61.5 us
  blocking collectives: 77.3 us -> 174 us
  local copies, waits for them, and re-layouts: 41.2 us -> 73.4 us
  starting transfers between devices: 48.8 us -> 26.5 us
    all_gather x4 -> x1, waiting for transfers between devices: 262 us -> 25.3 us  [gather_blocks(): return lax.all_gather(x, axis_name, axis=0, tiled=False)]
    all_gather x0 -> x1, blocking collectives: none -> 128 us  [body(): kernel_rows_full = lax.all_gather(conv_kernel, 'row', axis=1, tiled=True)]
    psum x2 -> x0, blocking collectives: 77.3 us -> none  [the longest x1 46.5 us: body(): lax.psum((jnp.sum(grad_norm * zhat_own, axis=0), jnp.sum(grad_norm, axis=...]
    reduce_scatter x2 -> x0, waiting for transfers between devices: 67.8 us -> none  [the longest x1 67.8 us: body(): lax.psum_scatter(partial_sum.astype(jnp.bfloat16), 'col', scatter_dimensi...]
    all_to_all x0 -> x1, blocking collectives: none -> 46.5 us  [gather_blocks(): return lax.all_to_all(wide, axis_name, 0, 0, tiled=True)]
    another operation x148 -> x99, local copies, waits for them, and re-layouts: 12.2 us -> 50.6 us  [body(): kernel_part = jnp.stack(kernel_rows).reshape(KS * KS, n_row, few)]
    all_to_all x3, waiting for transfers between devices: 0.01 us -> 35.4 us  [the longest x1 25.4 us: body(): lax.all_to_all(outgoing, 'col', 0, 0, tiled=True).astype(jnp.float32)]
    all_to_all x3, starting transfers between devices: 48.6 us -> 20.2 us  [the longest x1 8.22 us: body(): lax.all_to_all(jnp.concatenate([kernel_part, norm_part], axis=1), 'row',...]
  transfers between devices with their start and end apart: 9 -> 6, of which waited for: 5 -> 4; matrix products, arithmetic and copies ran while one was open for 12% -> 6% of each run, Pallas kernels for 0% -> 0%
where the time goes in v1:
time: 377 us; the launch traced here: 376 us
  blocking collectives  174 us (46%)
  local copies, waits for them, and re-layouts  73.4 us (19%)
  waiting for transfers between devices  61.5 us (16%)
  starting transfers between devices  26.5 us (7%)
  other arithmetic  17.7 us (5%)
  between operations  14.6 us (4%)
  matrix products  7.84 us (2%)
    all_gather x1, blocking collectives, body(): kernel_rows_full = lax.all_gather(conv_kernel, 'row', axis=1, tiled=True)  128 us
    another operation x99, local copies, waits for them, and re-layouts, body(): kernel_part = jnp.stack(kernel_rows).reshape(KS * KS, n_row, few)  50.6 us
    all_to_all x1, blocking collectives, gather_blocks(): return lax.all_to_all(wide, axis_name, 0, 0, tiled=True)  46.5 us
    all_to_all x1, waiting for transfers between devices, body(): lax.all_to_all(outgoing, 'col', 0, 0, tiled=True).astype(jnp.float32)  25.4 us
    all_gather x1, waiting for transfers between devices, gather_blocks(): return lax.all_gather(x, axis_name, axis=0, tiled=False)  25.3 us
    all_to_all x1, waiting for transfers between devices, body(): lax.all_to_all(jnp.concatenate([kernel_part, norm_part], axis=1), 'row',...  10.1 us
    all_to_all x1, starting transfers between devices, body(): lax.all_to_all(jnp.concatenate([kernel_part, norm_part], axis=1), 'row',...  8.22 us
  transfers between devices with their start and end apart: 6, of which 4 were waited for; matrix products, arithmetic and copies ran while one was open for 6% of the time, Pallas kernels for 0%

profile of v1, /device:TPU:1, one launch (start us, length us, event | category | flops | bytes accessed | tf_op | source)
XLA Modules:
  0.0 376.0 jit_solution(20524008680382430)
XLA Ops:
  7.2 1.6 pad_maximum_fusion.2
  12.1 46.5 %all_to_all.24 = bf16[16,256,384]{1,2,0:T(8,128)(2,1)S(1)} all-to-all(bf16[16,256,384]{1,2,0:T(8,128)(2,1)S(1)} %broadcast_in_dim.6), channel_id=1, replica_groups=mesh['row'=32,'col'=16] {'col'}, dimensions={0} | all-to-all | bytes 6291456 | tf_op jit(solution)/shard_map/all_to_all | solution.py:24
  58.6 2.6 slice_convert_fusion
  61.2 3.6 copy.80
  65.6 25.3 %all-gather.4.cloned.1.call-done = bf16[3072,768]{1,0:T(8,128)(2,1)} async-done(((bf16[96,768]{1,0:T(8,128)(2,1)}), bf16[3072,768]{1,0:T(8,128)(2,1)}) %all-gather.4.cloned.1.call-update) | async-done | bytes 4718608 | tf_op jit(solution)/shard_map/all_gather | solution.py:25
  90.9 3.0 fusion.66
  93.9 1.1 fusion.4
  95.8 2.4 fusion
  98.2 3.7 copy.79
  101.9 2.7 pad_maximum_fusion
  104.7 6.7 %all-to-all-start.1 = ((bf16[16,256,196]{1,2,0:T(8,128)(2,1)}), bf16[16,256,196]{1,2,0:T(8,128)(2,1)}, u32[]{:S(2)}, u32[]{:S(2)}) async-start(bf16[16,256,196]{1,2,0:T(8,128)(2,1)} %pad_maximum_fusion), calls=%async_computation.1 | async-start | bytes 3276800 | tf_op jit(solution)/shard_map/all_to_all | solution.py:104
  111.5 25.4 %all-to-all-done.1 = bf16[16,256,196]{1,2,0:T(8,128)(2,1)} async-done(((bf16[16,256,196]{1,2,0:T(8,128)(2,1)}), bf16[16,256,196]{1,2,0:T(8,128)(2,1)}, u32[]{:S(2)}, u32[]{:S(2)}) %all-to-all-start.1) | async-done | bytes 1605664 | tf_op jit(solution)/shard_map/all_to_all | solution.py:104
  136.9 1.7 convert_element_type.110
  139.5 1.8 copy.81
  141.3 1.2 multiply_reduce_fusion.2
  142.5 3.3 collective-permute-start.1
  145.8 3.0 collective-permute-start
  171.4 1.7 copy.112
  173.1 1.7 copy.111
  174.8 1.7 copy.110
  176.5 1.7 copy.109
  178.2 1.7 copy.108
  179.8 1.7 copy.106
  199.3 3.8 %stack.207 = f32[49,32,6]{0,1,2:T(8,128)} concatenate(f32[1,32,6]{0,1,2:T(8,128)} %copy.83, f32[1,32,6]{0,1,2:T(8,128)S(1)} %copy.84, f32[1,32,6]{0,1,2:T(8,128)S(1)} %copy.85, f32[1,32,6]{0,1,2:T(8,128)} %copy.86, f32[1,32,6]{0,1,2:T(8,128)S(1)} %copy.87, f32[1,32,6]{0,1,2:T(8,128)S(1)} %copy.88, f32[1,32,6]{0,1,2:T(8,128)S(1)} %copy.89, f32[1,32,6]{0,1,2:T(8,128)S(1)} %copy.90, ...), dimensions={0} | concatenate | bytes 75264 | tf_op jit(solution)/shard_map/stack | solution.py:136
  205.0 8.2 %all-to-all-start.2 = ((f32[32,1,678]{2,1,0:T(1,128)}), f32[32,1,678]{2,1,0:T(1,128)S(1)}, u32[]{:S(2)}, u32[]{:S(2)}) async-start(f32[32,1,678]{2,1,0:T(1,128)} %all_to_all.17), calls=%async_computation.2 | async-start | bytes 196608 | tf_op jit(solution)/shard_map/all_to_all | solution.py:140
  213.2 4.4 %convolution_convert_fusion = bf16[3072,384]{1,0:T(8,128)(2,1)} fusion(bf16[256,384]{1,0:T(8,128)(2,1)S(1)} %copy-done.4, f32[256,3072]{1,0:T(8,128)} %copy-done, f32[3072]{0:T(1024)S(1)} %copy-done.9, f32[3072]{0:T(1024)S(1)} %copy-done.7), kind=kOutput, calls=%fused_computation | convolution fusion | flops 607518720 | bytes 5726208 | tf_op jit(solution)/shard_map/dot_general | solution.py:77
  217.6 10.1 %all-to-all-done.2 = f32[32,1,678]{2,1,0:T(1,128)S(1)} async-done(((f32[32,1,678]{2,1,0:T(1,128)}), f32[32,1,678]{2,1,0:T(1,128)S(1)}, u32[]{:S(2)}, u32[]{:S(2)}) %all-to-all-start.2) | async-done | bytes 86816 | tf_op jit(solution)/shard_map/all_to_all | solution.py:140
  227.7 5.3 %all-to-all-start.3 = ((bf16[32,96,384]{2,1,0:T(8,128)(2,1)}), bf16[32,96,384]{2,1,0:T(8,128)(2,1)S(1)}, u32[]{:S(2)}, u32[]{:S(2)}) async-start(bf16[32,96,384]{2,1,0:T(8,128)(2,1)} %bitcast.23), calls=%async_computation.3 | async-start | bytes 4718592 | tf_op jit(solution)/shard_map/all_to_all | solution.py:81
  233.0 127.9 %all-gather.1 = f32[32,6,49]{2,1,0:T(8,128)S(1)} all-gather(f32[1,6,49]{2,1,0:T(8,128)S(1)} %bitcast.102), channel_id=1, replica_groups=mesh['row'=32,'col'=16] {'row'}, dimensions={0}, use_global_device_ids=true | all-gather | bytes 38808 | tf_op jit(solution)/shard_map/all_gather | solution.py:59
  361.6 1.3 slice_reduce_fusion.49
  362.9 1.2 slice_reduce_fusion.50
  364.1 1.7 multiply_add_fusion
  (160 shorter events, 52.0 us)
Async XLA Ops:
  7.2 83.7 %all-gather.4.cloned.1.call-start = ((), (), s32[]{:S(2)}) async-start(), calls=%async_computation.4 | async-start | bytes 4866048 | tf_op jit(solution)/shard_map/all_gather | solution.py:25
  90.9 3.0 copy-start.2
  90.9 3.0 copy-start.11
  93.9 1.9 copy-start.1
  93.9 1.9 copy-start.6
  95.0 3.2 copy-start.3
  98.2 44.3 %copy-start = (f32[256,3072]{1,0:T(8,128)}, f32[256,3072]{1,0:T(8,128)S(1)}, u32[]{:S(2)}) copy-start(f32[256,3072]{1,0:T(8,128)S(1)} %get-tuple-element.117) | copy-start | bytes 9437188
  101.9 9.5 %copy-start.5 = (bf16[256,192]{0,1:T(8,128)(2,1)S(1)}, bf16[256,192]{0,1:T(8,128)(2,1)}, u32[]{:S(2)}) copy-start(bf16[256,192]{0,1:T(8,128)(2,1)} %param.10) | copy-start | bytes 294916
  104.7 32.3 %all-to-all-start.1 = ((bf16[16,256,196]{1,2,0:T(8,128)(2,1)}), bf16[16,256,196]{1,2,0:T(8,128)(2,1)}, u32[]{:S(2)}, u32[]{:S(2)}) async-start(bf16[16,256,196]{1,2,0:T(8,128)(2,1)} %pad_maximum_fusion), calls=%async_computation.1 | async-start | bytes 3276800 | tf_op jit(solution)/shard_map/all_to_all | solution.py:104
  142.5 7.0 %collective-permute-start.1 = (bf16[3,64,192]{2,1,0:T(8,128)(2,1)S(1)}, bf16[3,64,192]{2,1,0:T(8,128)(2,1)S(1)}, u32[]{:S(2)}, u32[]{:S(2)}) collective-permute-start(bf16[3,64,192]{2,1,0:T(8,128)(2,1)S(1)} %bitcast.97), channel_id=1, source_target_pairs={{16,0},{32,16},{48,32},{64,48},{80,64},{96,80},{112,96},{128,112},... | collective-permute-start | bytes 221192 | tf_op jit(solution)/shard_map/ppermute | solution.py:119
  145.8 4.5 %collective-permute-start = (bf16[3,64,192]{2,1,0:T(8,128)(2,1)S(1)}, bf16[3,64,192]{2,1,0:T(8,128)(2,1)S(1)}, u32[]{:S(2)}, u32[]{:S(2)}) collective-permute-start(bf16[3,64,192]{2,1,0:T(8,128)(2,1)S(1)} %bitcast.96), channel_id=1, source_target_pairs={{0,16},{16,32},{32,48},{48,64},{64,80},{80,96},{96,112},{112,128},... | collective-permute-start | bytes 221192 | tf_op jit(solution)/shard_map/ppermute | solution.py:118
  194.3 9.9 %copy-start.8 = (f32[678]{0:T(1024)S(1)}, f32[678]{0:T(1024)}, u32[]{:S(2)}) copy-start(f32[678]{0:T(1024)} %pad_maximum_fusion.4) | copy-start | bytes 8140
  199.3 13.9 %copy-start.4 = (bf16[256,384]{1,0:T(8,128)(2,1)S(1)}, bf16[256,384]{1,0:T(8,128)(2,1)}, u32[]{:S(2)}) copy-start(bf16[256,384]{1,0:T(8,128)(2,1)} %copy-done.3) | copy-start | bytes 589828
  199.3 14.0 %copy-start.7 = (f32[3072]{0:T(1024)S(1)}, f32[3072]{0:T(1024)}, u32[]{:S(2)}) copy-start(f32[3072]{0:T(1024)} %param.15) | copy-start | bytes 36868
  199.3 14.0 %copy-start.9 = (f32[3072]{0:T(1024)S(1)}, f32[3072]{0:T(1024)}, u32[]{:S(2)}) copy-start(f32[3072]{0:T(1024)} %param.16) | copy-start | bytes 36868
  205.0 22.7 %all-to-all-start.2 = ((f32[32,1,678]{2,1,0:T(1,128)}), f32[32,1,678]{2,1,0:T(1,128)S(1)}, u32[]{:S(2)}, u32[]{:S(2)}) async-start(f32[32,1,678]{2,1,0:T(1,128)} %all_to_all.17), calls=%async_computation.2 | async-start | bytes 196608 | tf_op jit(solution)/shard_map/all_to_all | solution.py:140
  217.6 15.4 %copy-start.10 = (f32[49,6]{0,1:T(8,128)S(1)}, f32[49,6]{0,1:T(8,128)}, u32[]{:S(2)}) copy-start(f32[49,6]{0,1:T(8,128)} %param.14) | copy-start | bytes 3532
  227.7 140.5 %all-to-all-start.3 = ((bf16[32,96,384]{2,1,0:T(8,128)(2,1)}), bf16[32,96,384]{2,1,0:T(8,128)(2,1)S(1)}, u32[]{:S(2)}, u32[]{:S(2)}) async-start(bf16[32,96,384]{2,1,0:T(8,128)(2,1)} %bitcast.23), calls=%async_computation.3 | async-start | bytes 4718592 | tf_op jit(solution)/shard_map/all_to_all | solution.py:81
Sparse Core Ops, SparseCore 0:
  10.1 80.7 all-gather.3

commit v2 on v1

--- a/solution.py
+++ b/solution.py
@@ -1,6 +1,8 @@
 import jax
 import jax.numpy as jnp
 from jax import lax
+from jax.experimental import pallas as pl
+from jax.experimental.pallas import tpu as pltpu
 from jax.sharding import PartitionSpec as P
 
 KS = 7
@@ -23,6 +25,44 @@
         wide = jnp.broadcast_to(x[None], (size,) + x.shape)
         return lax.all_to_all(wide, axis_name, 0, 0, tiled=True)
     return lax.all_gather(x, axis_name, axis=0, tiled=False)
+
+
+def split_three(values):
+    high = lax.reduce_precision(values, exponent_bits=8, mantissa_bits=7)
+    rest = values - high
+    middle = lax.reduce_precision(rest, exponent_bits=8, mantissa_bits=7)
+    low = rest - middle
+    return jnp.stack([high, middle, low]).astype(jnp.bfloat16)
+
+
+def conv_body(tall_ref, inputs_ref, cot_ref, kernel_ref, din_ref, dk_ref, pad_ref):
+    rows, span, channels = inputs_ref.shape
+    pad_ref[...] = tall_ref[...].astype(jnp.float32)
+    inputs = inputs_ref[...].astype(jnp.float32)
+    moved = jnp.zeros((rows, span, channels), jnp.float32)
+    for down in range(KS):
+        for across in range(KS):
+            tap = down * KS + across
+            window = pad_ref[
+                2 * HALO - down : 2 * HALO - down + rows,
+                2 * HALO - across : 2 * HALO - across + span,
+                :,
+            ]
+            moved = moved + kernel_ref[tap : tap + 1, :][None] * window
+            dk_ref[tap : tap + 1, :] = jnp.sum(window * inputs, axis=(0, 1))[None]
+    din_ref[...] = (moved + cot_ref[...].astype(jnp.float32)).astype(din_ref.dtype)
+
+
+def conv_call(padded, inputs, cot, kernel_full):
+    rows, span, channels = inputs.shape
+    return pl.pallas_call(
+        conv_body,
+        out_shape=(
+            jax.ShapeDtypeStruct((rows, span, channels), jnp.bfloat16),
+            jax.ShapeDtypeStruct((KS * KS, channels), jnp.float32),
+        ),
+        scratch_shapes=[pltpu.VMEM(padded.shape, jnp.float32)],
+    )(padded, inputs, cot, kernel_full)
 
 
 def split_hi_lo(values):
@@ -55,12 +95,23 @@
 
     scaled = (cotangent.astype(jnp.float32) * layer_scale).astype(jnp.bfloat16)
     acts = gather_blocks(jnp.concatenate([scaled, conv_out], axis=1), "col", n_col, ACTS_VIA)
-    weights = gather_blocks(jnp.concatenate([w_out, w_in], axis=1), "row", n_row, WEIGHTS_VIA)
-    kernel_rows_full = lax.all_gather(conv_kernel, "row", axis=1, tiled=True)
+    kernel_bits = split_three(conv_kernel).reshape(-1)
+    lanes_extra = -(-kernel_bits.shape[0] // w_in.shape[0])
+    kernel_bits = jnp.pad(kernel_bits, (0, lanes_extra * w_in.shape[0] - kernel_bits.shape[0]))
+    weights = gather_blocks(
+        jnp.concatenate([w_out, w_in, kernel_bits.reshape(w_in.shape[0], lanes_extra)], axis=1),
+        "row",
+        n_row,
+        WEIGHTS_VIA,
+    )
+    kernel_parts = weights[:, :, 2 * hidden :].reshape(n_row, -1)[:, : 3 * KS * KS * few]
+    kernel_parts = kernel_parts.reshape(n_row, 3, KS * KS, few).astype(jnp.float32)
+    kernel_sum = kernel_parts[:, 0] + kernel_parts[:, 1] + kernel_parts[:, 2]
+    kernel_rows_full = jnp.transpose(kernel_sum, (1, 0, 2)).reshape(KS * KS, n_row * few)
     scaled_full = jnp.transpose(acts[:, :, :channels], (1, 0, 2)).reshape(tokens, width)
     inputs_full = jnp.transpose(acts[:, :, channels:], (1, 0, 2)).reshape(tokens, width)
     w_out_full = weights[:, :, :hidden].reshape(width, hidden)
-    w_in_full = weights[:, :, hidden:].reshape(width, hidden)
+    w_in_full = weights[:, :, hidden : 2 * hidden].reshape(width, hidden)
 
     values = inputs_full.astype(jnp.float32)
     mean = jnp.mean(values, axis=1, keepdims=True)
@@ -117,23 +168,17 @@
     up_pairs = [(i + 1, i) for i in range(n_row) if (i + 1) % per_image != 0]
     from_above = lax.ppermute(grid[rows - HALO :], "row", down_pairs)
     from_below = lax.ppermute(grid[:HALO], "row", up_pairs)
-    tall = jnp.concatenate([from_above, grid, from_below], axis=0).astype(jnp.float32)
+    tall = jnp.concatenate([from_above, grid, from_below], axis=0)
     padded = jnp.pad(tall, ((0, 0), (HALO, HALO), (0, 0)))
-    inputs = block_input.astype(jnp.float32).reshape(rows, H, channels)
-    kernel_full = kernel_rows_full
-    moved = jnp.zeros((rows, H, channels), jnp.float32)
-    kernel_rows = []
-    for tap in range(KS * KS):
-        down = tap // KS
-        across = tap % KS
-        window = padded[
-            2 * HALO - down : 2 * HALO - down + rows, 2 * HALO - across : 2 * HALO - across + H
-        ]
-        moved = moved + kernel_full[tap] * window
-        kernel_rows.append(jnp.sum(window * inputs, axis=(0, 1)))
-    d_input = (moved.reshape(tokens, channels) + cotangent.astype(jnp.float32)).astype(jnp.bfloat16)
-
-    kernel_part = jnp.stack(kernel_rows).reshape(KS * KS, n_row, few)
+    d_input, kernel_sums = conv_call(
+        padded,
+        block_input.reshape(rows, H, channels),
+        cotangent.reshape(rows, H, channels),
+        kernel_rows_full,
+    )
+    d_input = d_input.reshape(tokens, channels)
+
+    kernel_part = kernel_sums.reshape(KS * KS, n_row, few)
     kernel_part = jnp.transpose(kernel_part, (1, 0, 2)).reshape(n_row, KS * KS * few)
     norm_part = jnp.broadcast_to(jnp.concatenate([gain_part, bias_part])[None], (n_row, 2 * channels))
     reduced = jnp.sum(

time: 377 us -> 310 us (0.82)
  blocking collectives: 174 us -> 46.5 us
  waiting for transfers between devices: 61.5 us -> 162 us
  local copies, waits for them, and re-layouts: 73.4 us -> 27 us
  Pallas kernels: 0 us -> 7 us
    all_gather x1 -> x0, blocking collectives: 128 us -> none  [body(): kernel_rows_full = lax.all_gather(conv_kernel, 'row', axis=1, tiled=True)]
    all_to_all x1, waiting for transfers between devices: 0.01 us -> 107 us  [body(): lax.all_to_all(block_w.reshape(n_row, width // n_row, hidden), 'row', 0,...]
    another operation x99 -> x1, local copies, waits for them, and re-layouts: 50.6 us -> 0.14 us  [split_three(): return jnp.stack([high, middle, low]).astype(jnp.bfloat16)]
    all_to_all x1, waiting for transfers between devices: 25.4 us -> 16.5 us  [body(): lax.all_to_all(outgoing, 'col', 0, 0, tiled=True).astype(jnp.float32)]
    pallas_call x0 -> x1, Pallas kernels: none -> 7 us  [conv_call(): pl.pallas_call(conv_body, out_shape=(jax.ShapeDtypeStruct((rows, span, ch...]
  transfers between devices with their start and end apart: 6 -> 6, of which waited for: 4 -> 5; matrix products, arithmetic and copies ran while one was open for 6% -> 8% of each run, Pallas kernels for 0% -> 0%
where the time goes in v2:
time: 310 us; the launch traced here: 308 us
  waiting for transfers between devices  162 us (52%)
  blocking collectives  46.5 us (15%)
  local copies, waits for them, and re-layouts  27 us (9%)
  starting transfers between devices  26.5 us (9%)
  other arithmetic  18.5 us (6%)
  between operations  14.3 us (5%)
  Pallas kernels  7 us (2%)
  matrix products  6.66 us (2%)
    all_to_all x1, waiting for transfers between devices, body(): lax.all_to_all(block_w.reshape(n_row, width // n_row, hidden), 'row', 0,...  107 us
    all_to_all x1, blocking collectives, gather_blocks(): return lax.all_to_all(wide, axis_name, 0, 0, tiled=True)  46.5 us
    all_gather x1, waiting for transfers between devices, gather_blocks(): return lax.all_gather(x, axis_name, axis=0, tiled=False)  26.1 us
    all_to_all x1, waiting for transfers between devices, body(): lax.all_to_all(outgoing, 'col', 0, 0, tiled=True).astype(jnp.float32)  16.5 us
    all_to_all x1, waiting for transfers between devices, body(): lax.all_to_all(jnp.concatenate([kernel_part, norm_part], axis=1), 'row',...  11.4 us
    all_to_all x1, starting transfers between devices, body(): lax.all_to_all(jnp.concatenate([kernel_part, norm_part], axis=1), 'row',...  8.37 us
    pallas_call x1, Pallas kernels, conv_call(): pl.pallas_call(conv_body, out_shape=(jax.ShapeDtypeStruct((rows, span, ch...  7 us
    all_to_all x1, starting transfers between devices, body(): lax.all_to_all(outgoing, 'col', 0, 0, tiled=True).astype(jnp.float32)  6.6 us
  transfers between devices with their start and end apart: 6, of which 5 were waited for; matrix products, arithmetic and copies ran while one was open for 8% of the time, Pallas kernels for 0%

profile of v2, /device:TPU:1, one launch (start us, length us, event | category | flops | bytes accessed | tf_op | source)
XLA Modules:
  0.0 308.0 jit_solution(13821947893903968847)
XLA Ops:
  8.4 1.6 pad_maximum_fusion.2
  10.0 1.0 multiply_convert_fusion.1
  12.2 46.5 %all_to_all.24 = bf16[16,256,384]{1,2,0:T(8,128)(2,1)S(1)} all-to-all(bf16[16,256,384]{1,2,0:T(8,128)(2,1)S(1)} %broadcast_in_dim.6), channel_id=1, replica_groups=mesh['row'=32,'col'=16] {'col'}, dimensions={0} | all-to-all | bytes 6291456 | tf_op jit(solution)/shard_map/all_to_all | solution.py:26
  58.7 2.6 slice_convert_fusion
  61.4 3.6 %copy.34 = f32[256,3072]{1,0:T(8,128)} copy(f32[256,3072]{0,1:T(8,128)} %bitcast.47) | data formatting | bytes 6291456 | tf_op jit(solution)/shard_map/convert_element_type | solution.py:116
  65.9 26.1 %all-gather.3.cloned.1.call-done = bf16[3072,778]{1,0:T(8,128)(2,1)} async-done(((bf16[96,778]{1,0:T(8,128)(2,1)}), bf16[3072,778]{1,0:T(8,128)(2,1)}) %all-gather.3.cloned.1.call-update) | async-done | bytes 4780048 | tf_op jit(solution)/shard_map/all_gather | solution.py:27
  92.0 3.0 fusion.26
  95.1 1.1 fusion.4
  97.0 2.4 fusion
  99.4 2.7 copy.33
  102.1 2.8 pad_maximum_fusion
  104.9 6.6 %all-to-all-start.1 = ((bf16[16,256,196]{1,2,0:T(8,128)(2,1)}), bf16[16,256,196]{1,2,0:T(8,128)(2,1)}, u32[]{:S(2)}, u32[]{:S(2)}) async-start(bf16[16,256,196]{1,2,0:T(8,128)(2,1)} %pad_maximum_fusion), calls=%async_computation.1 | async-start | bytes 3276800 | tf_op jit(solution)/shard_map/all_to_all | solution.py:155
  113.1 2.2 slice.108
  115.2 2.2 reshape.162
  118.5 1.2 fusion.17
  120.5 16.5 %all-to-all-done.1 = bf16[16,256,196]{1,2,0:T(8,128)(2,1)} async-done(((bf16[16,256,196]{1,2,0:T(8,128)(2,1)}), bf16[16,256,196]{1,2,0:T(8,128)(2,1)}, u32[]{:S(2)}, u32[]{:S(2)}) %all-to-all-start.1) | async-done | bytes 1605664 | tf_op jit(solution)/shard_map/all_to_all | solution.py:155
  137.0 1.7 convert_element_type.116
  138.8 0.9 slice_reduce_fusion
  139.7 1.1 copy.35
  141.0 3.4 %collective-permute-start.1 = (bf16[3,64,192]{2,1,0:T(8,128)(2,1)S(1)}, bf16[3,64,192]{2,1,0:T(8,128)(2,1)S(1)}, u32[]{:S(2)}, u32[]{:S(2)}) collective-permute-start(bf16[3,64,192]{2,1,0:T(8,128)(2,1)S(1)} %bitcast.61), channel_id=1, source_target_pairs={{16,0},{32,16},{48,32},{64,48},{80,64},{96,80},{112,96},{128,112},... | collective-permute-start | bytes 221192 | tf_op jit(solution)/shard_map/ppermute | solution.py:170
  144.4 2.9 collective-permute-start
  147.4 1.3 pad_maximum_fusion.5
  149.6 7.0 %shard_map.137 = (bf16[4,64,192]{2,1,0:T(8,128)(2,1)}, f32[49,192]{1,0:T(8,128)}) custom-call(bf16[10,70,192]{2,1,0:T(8,128)(2,1)} %fusion.16.tall_ref, bf16[4,64,192]{2,1,0:T(8,128)(2,1)} %bitcast.57, bf16[4,64,192]{2,1,0:T(8,128)(2,1)} %bitcast.56, f32[49,192]{1,0:T(8,128)} %copy.40.kernel_ref), custom_call_target="tpu_custom_call" | custom-call | tf_op jit(solution)/shard_map/pallas_call | solution.py:58
  156.6 0.9 copy.41
  158.2 1.1 copy.42
  160.0 1.0 copy.44
  162.4 8.4 %all-to-all-start.2 = ((f32[32,1,678]{2,1,0:T(1,128)}), f32[32,1,678]{2,1,0:T(1,128)S(1)}, u32[]{:S(2)}, u32[]{:S(2)}) async-start(f32[32,1,678]{2,1,0:T(1,128)} %all_to_all.17), calls=%async_computation.2 | async-start | bytes 196608 | tf_op jit(solution)/shard_map/all_to_all | solution.py:185
  170.8 3.2 %convolution_convert_fusion = bf16[3072,384]{1,0:T(8,128)(2,1)} fusion(bf16[256,384]{1,0:T(8,128)(2,1)S(1)} %copy-done.3, f32[256,3072]{1,0:T(8,128)S(1)} %get-tuple-element.28, f32[3072]{0:T(1024)} %param.16, f32[3072]{0:T(1024)S(1)} %copy-done.7), kind=kOutput, calls=%fused_computation | convolution fusion | flops 607518720 | bytes 5726208 | tf_op jit(solution)/shard_map/dot_general | solution.py:128
  173.9 11.4 %all-to-all-done.2 = f32[32,1,678]{2,1,0:T(1,128)S(1)} async-done(((f32[32,1,678]{2,1,0:T(1,128)}), f32[32,1,678]{2,1,0:T(1,128)S(1)}, u32[]{:S(2)}, u32[]{:S(2)}) %all-to-all-start.2) | async-done | bytes 86816 | tf_op jit(solution)/shard_map/all_to_all | solution.py:185
  185.4 5.2 %all-to-all-start.3 = ((bf16[32,96,384]{2,1,0:T(8,128)(2,1)}), bf16[32,96,384]{2,1,0:T(8,128)(2,1)S(1)}, u32[]{:S(2)}, u32[]{:S(2)}) async-start(bf16[32,96,384]{2,1,0:T(8,128)(2,1)} %bitcast.48), calls=%async_computation.3 | async-start | bytes 4718592 | tf_op jit(solution)/shard_map/all_to_all | solution.py:132
  192.8 107.4 %all-to-all-done.3 = bf16[32,96,384]{2,1,0:T(8,128)(2,1)S(1)} async-done(((bf16[32,96,384]{2,1,0:T(8,128)(2,1)}), bf16[32,96,384]{2,1,0:T(8,128)(2,1)S(1)}, u32[]{:S(2)}, u32[]{:S(2)}) %all-to-all-start.3) | async-done | bytes 2359328 | tf_op jit(solution)/shard_map/all_to_all | solution.py:132
  300.2 1.0 reduce_sum.108
  (61 shorter events, 13.9 us)
Async XLA Ops:
  7.2 84.8 %all-gather.3.cloned.1.call-start = ((), (), s32[]{:S(2)}) async-start(), calls=%async_computation.4 | async-start | bytes 5677056 | tf_op jit(solution)/shard_map/all_gather | solution.py:27
  92.0 3.1 %copy-start.1 = (bf16[16,256,192]{1,2,0:T(8,128)(2,1)S(1)}, bf16[16,256,192]{1,2,0:T(8,128)(2,1)}, u32[]{:S(2)}) copy-start(bf16[16,256,192]{1,2,0:T(8,128)(2,1)} %get-tuple-element.34) | copy-start | bytes 4718596
  92.0 3.1 %copy-start.8 = (bf16[256,384]{1,0:T(8,128)(2,1)S(1)}, bf16[256,384]{1,0:T(8,128)(2,1)}, u32[]{:S(2)}) copy-start(bf16[256,384]{1,0:T(8,128)(2,1)} %param.12) | copy-start | bytes 589828
  95.1 1.9 copy-start
  95.1 1.9 copy-start.7
  96.2 3.2 %copy-start.2 = (bf16[256,384]{1,0:T(8,128)(2,1)}, bf16[256,384]{1,0:T(8,128)(2,1)S(1)}, u32[]{:S(2)}) copy-start(bf16[256,384]{1,0:T(8,128)(2,1)S(1)} %fusion.4) | copy-start | bytes 589828
  102.1 9.4 %copy-start.4 = (bf16[256,192]{0,1:T(8,128)(2,1)S(1)}, bf16[256,192]{0,1:T(8,128)(2,1)}, u32[]{:S(2)}) copy-start(bf16[256,192]{0,1:T(8,128)(2,1)} %param.13) | copy-start | bytes 294916
  102.1 10.2 %copy-start.6 = (bf16[256,192]{0,1:T(8,128)(2,1)S(1)}, bf16[256,192]{0,1:T(8,128)(2,1)}, u32[]{:S(2)}) copy-start(bf16[256,192]{0,1:T(8,128)(2,1)} %param.10) | copy-start | bytes 294916
  104.9 32.2 %all-to-all-start.1 = ((bf16[16,256,196]{1,2,0:T(8,128)(2,1)}), bf16[16,256,196]{1,2,0:T(8,128)(2,1)}, u32[]{:S(2)}, u32[]{:S(2)}) async-start(bf16[16,256,196]{1,2,0:T(8,128)(2,1)} %pad_maximum_fusion), calls=%async_computation.1 | async-start | bytes 3276800 | tf_op jit(solution)/shard_map/all_to_all | solution.py:155
  141.0 29.8 %copy-start.3 = (bf16[256,384]{1,0:T(8,128)(2,1)S(1)}, bf16[256,384]{1,0:T(8,128)(2,1)}, u32[]{:S(2)}) copy-start(bf16[256,384]{1,0:T(8,128)(2,1)} %copy-done.2) | copy-start | bytes 589828
  141.0 7.7 %collective-permute-start.1 = (bf16[3,64,192]{2,1,0:T(8,128)(2,1)S(1)}, bf16[3,64,192]{2,1,0:T(8,128)(2,1)S(1)}, u32[]{:S(2)}, u32[]{:S(2)}) collective-permute-start(bf16[3,64,192]{2,1,0:T(8,128)(2,1)S(1)} %bitcast.61), channel_id=1, source_target_pairs={{16,0},{32,16},{48,32},{64,48},{80,64},{96,80},{112,96},{128,112},... | collective-permute-start | bytes 221192 | tf_op jit(solution)/shard_map/ppermute | solution.py:170
  144.4 4.4 %collective-permute-start = (bf16[3,64,192]{2,1,0:T(8,128)(2,1)S(1)}, bf16[3,64,192]{2,1,0:T(8,128)(2,1)S(1)}, u32[]{:S(2)}, u32[]{:S(2)}) collective-permute-start(bf16[3,64,192]{2,1,0:T(8,128)(2,1)S(1)} %bitcast.60), channel_id=1, source_target_pairs={{0,16},{16,32},{32,48},{48,64},{64,80},{80,96},{96,112},{112,128},... | collective-permute-start | bytes 221192 | tf_op jit(solution)/shard_map/ppermute | solution.py:169
  162.4 23.0 %all-to-all-start.2 = ((f32[32,1,678]{2,1,0:T(1,128)}), f32[32,1,678]{2,1,0:T(1,128)S(1)}, u32[]{:S(2)}, u32[]{:S(2)}) async-start(f32[32,1,678]{2,1,0:T(1,128)} %all_to_all.17), calls=%async_computation.2 | async-start | bytes 196608 | tf_op jit(solution)/shard_map/all_to_all | solution.py:185
  173.9 16.6 %copy-start.5 = (bf16[4,64,192]{2,1,0:T(8,128)(2,1)S(1)}, bf16[4,64,192]{2,1,0:T(8,128)(2,1)}, u32[]{:S(2)}) copy-start(bf16[4,64,192]{2,1,0:T(8,128)(2,1)} %get-tuple-element.7) | copy-start | bytes 294916
  185.4 114.8 %all-to-all-start.3 = ((bf16[32,96,384]{2,1,0:T(8,128)(2,1)}), bf16[32,96,384]{2,1,0:T(8,128)(2,1)S(1)}, u32[]{:S(2)}, u32[]{:S(2)}) async-start(bf16[32,96,384]{2,1,0:T(8,128)(2,1)} %bitcast.48), calls=%async_computation.3 | async-start | bytes 4718592 | tf_op jit(solution)/shard_map/all_to_all | solution.py:132
Sparse Core Ops, SparseCore 0:
  10.1 81.8 all-gather.2

commit v3 on v2

--- a/solution.py
+++ b/solution.py
@@ -10,7 +10,7 @@
 HALO = KS // 2
 
 WEIGHTS_VIA = "gather"
-DWIN_VIA = "a2a"
+DWIN_VIA = "rs"
 ACTS_VIA = "a2a"
 
 

time: 310 us -> 218 us (0.70)
  waiting for transfers between devices: 162 us -> 76.9 us
  starting transfers between devices: 26.5 us -> 21.4 us
    all_to_all x1 -> x0, waiting for transfers between devices: 107 us -> none  [body(): lax.all_to_all(block_w.reshape(n_row, width // n_row, hidden), 'row', 0,...]
    reduce_scatter x0 -> x1, waiting for transfers between devices: none -> 20.9 us  [body(): d_w_in = lax.psum_scatter(block_w, 'row', scatter_dimension=0, tiled=True)]
    all_to_all x1 -> x0, starting transfers between devices: 5.16 us -> none  [body(): lax.all_to_all(block_w.reshape(n_row, width // n_row, hidden), 'row', 0,...]
    unnamed x23 -> x21, local copies, waits for them, and re-layouts: 3.9 us -> 6.46 us
  transfers between devices with their start and end apart: 6 -> 6, of which waited for: 5 -> 6; matrix products, arithmetic and copies ran while one was open for 8% -> 16% of each run, Pallas kernels for 0% -> 3%
where the time goes in v3:
time: 218 us; the launch traced here: 215 us
  waiting for transfers between devices  76.9 us (35%)
  blocking collectives  46.5 us (21%)
  local copies, waits for them, and re-layouts  26.3 us (12%)
  starting transfers between devices  21.4 us (10%)
  other arithmetic  16.5 us (8%)
  between operations  14.3 us (7%)
  Pallas kernels  7 us (3%)
  matrix products  6.01 us (3%)
    all_to_all x1, blocking collectives, gather_blocks(): return lax.all_to_all(wide, axis_name, 0, 0, tiled=True)  46.5 us
    all_gather x1, waiting for transfers between devices, gather_blocks(): return lax.all_gather(x, axis_name, axis=0, tiled=False)  26.1 us
    reduce_scatter x1, waiting for transfers between devices, body(): d_w_in = lax.psum_scatter(block_w, 'row', scatter_dimension=0, tiled=True)  20.9 us
    all_to_all x1, waiting for transfers between devices, body(): lax.all_to_all(outgoing, 'col', 0, 0, tiled=True).astype(jnp.float32)  16.6 us
    all_to_all x1, waiting for transfers between devices, body(): lax.all_to_all(jnp.concatenate([kernel_part, norm_part], axis=1), 'row',...  11.8 us
    all_to_all x1, starting transfers between devices, body(): lax.all_to_all(jnp.concatenate([kernel_part, norm_part], axis=1), 'row',...  8.51 us
    pallas_call x1, Pallas kernels, conv_call(): pl.pallas_call(conv_body, out_shape=(jax.ShapeDtypeStruct((rows, span, ch...  7 us
    all_to_all x1, starting transfers between devices, body(): lax.all_to_all(outgoing, 'col', 0, 0, tiled=True).astype(jnp.float32)  6.59 us
  transfers between devices with their start and end apart: 6, of which 6 were waited for; matrix products, arithmetic and copies ran while one was open for 16% of the time, Pallas kernels for 3%

profile of v3, /device:TPU:1, one launch (start us, length us, event | category | flops | bytes accessed | tf_op | source)
XLA Modules:
  0.0 214.8 jit_solution(10390446048740563420)
XLA Ops:
  8.4 1.6 pad_maximum_fusion.2
  10.1 1.0 multiply_convert_fusion.1
  11.1 0.9 pad_maximum_fusion.1
  12.3 46.5 %all_to_all.19 = bf16[16,256,384]{1,2,0:T(8,128)(2,1)S(1)} all-to-all(bf16[16,256,384]{1,2,0:T(8,128)(2,1)S(1)} %broadcast_in_dim.6), channel_id=1, replica_groups=mesh['row'=32,'col'=16] {'col'}, dimensions={0} | all-to-all | bytes 6291456 | tf_op jit(solution)/shard_map/all_to_all | solution.py:26
  58.8 2.7 %slice_convert_fusion = (f32[16,256,192]{1,2,0:T(8,128)}, bf16[16,256,192]{1,2,0:T(8,128)(2,1)}) fusion(bf16[16,256,384]{1,2,0:T(8,128)(2,1)S(1)} %all_to_all.19), kind=kLoop, calls=%fused_computation.11 | loop fusion | flops 786432 | bytes 7864320 | tf_op jit(solution)/shard_map/convert_element_type | solution.py:116
  61.4 3.6 %copy.34 = f32[256,3072]{1,0:T(8,128)} copy(f32[256,3072]{0,1:T(8,128)} %bitcast.46) | data formatting | bytes 6291456 | tf_op jit(solution)/shard_map/convert_element_type | solution.py:116
  65.9 26.1 %all-gather.3.cloned.1.call-done = bf16[3072,778]{1,0:T(8,128)(2,1)} async-done(((bf16[96,778]{1,0:T(8,128)(2,1)}), bf16[3072,778]{1,0:T(8,128)(2,1)}) %all-gather.3.cloned.1.call-update) | async-done | bytes 4780048 | tf_op jit(solution)/shard_map/all_gather | solution.py:27
  92.0 3.0 %fusion.26 = (bf16[32,96,384]{2,1,0:T(8,128)(2,1)S(1)}, bf16[32,96,384]{2,1,0:T(8,128)(2,1)S(1)}) fusion(bf16[32,96,778]{2,1,0:T(8,128)(2,1)} %bitcast.49), kind=kLoop, calls=%fused_computation.68 | loop fusion | bytes 9437184 | tf_op jit(solution)/shard_map/slice | solution.py:114
  95.0 1.1 fusion.4
  96.9 2.5 %fusion = (f32[256]{0:T(256)S(1)}, f32[256]{0:T(256)S(1)}, f32[256,3072]{1,0:T(8,128)S(1)}, bf16[256,3072]{1,0:T(8,128)(2,1)}) fusion(f32[3072]{0:T(1024)S(1)} %copy-done.5, f32[256]{0:T(256)S(1)} %add_rsqrt_fusion, f32[256,3072]{1,0:T(8,128)S(1)} %copy-done.1, f32[256]{0:T(256)S(1)} %broadcast_multiply_fusion, bf16[256,384]{1,0:T(8,128)(2,1)S(1)} %fusion.4, ...), kind=kOutput, calls=%fused_computation.6 | convolution fusion | flops 610270720 | bytes 10436608 | tf_op jit(solution)/shard_map/dot_general | solution.py:139
  99.4 2.5 %convolution_convert_fusion = bf16[3072,384]{1,0:T(8,128)(2,1)} fusion(bf16[256,384]{1,0:T(8,128)(2,1)S(1)} %fusion.4, f32[256,3072]{1,0:T(8,128)S(1)} %get-tuple-element.28, f32[3072]{0:T(1024)S(1)} %copy-done.6, f32[3072]{0:T(1024)S(1)} %copy-done.5), kind=kOutput, calls=%fused_computation | convolution fusion | flops 607518720 | bytes 5726208 | tf_op jit(solution)/shard_map/dot_general | solution.py:128
  101.9 2.6 %copy.33 = bf16[256,3072]{0,1:T(8,128)(2,1)} copy(bf16[256,3072]{1,0:T(8,128)(2,1)} %get-tuple-element.48) | data formatting | bytes 3145728 | tf_op jit(solution)/shard_map/convert_element_type | solution.py:141
  104.5 2.8 %pad_maximum_fusion = bf16[16,256,196]{1,2,0:T(8,128)(2,1)} fusion(bf16[16,256,4]{1,2,0:T(4,128)(2,1)S(1)} %broadcast_in_dim.7, bf16[16,256,192]{1,2,0:T(8,128)(2,1)} %bitcast.48), kind=kLoop, calls=%fused_computation.10 | loop fusion | flops 3211264 | bytes 3211264 | tf_op jit(solution)/shard_map/concatenate | solution.py:148
  107.4 6.6 %all-to-all-start.1 = ((bf16[16,256,196]{1,2,0:T(8,128)(2,1)}), bf16[16,256,196]{1,2,0:T(8,128)(2,1)}, u32[]{:S(2)}, u32[]{:S(2)}) async-start(bf16[16,256,196]{1,2,0:T(8,128)(2,1)} %pad_maximum_fusion), calls=%async_computation.1 | async-start | bytes 3276800 | tf_op jit(solution)/shard_map/all_to_all | solution.py:155
  115.5 2.1 slice.108
  117.6 2.2 %reshape.158 = bf16[32,960]{1,0:T(8,128)(2,1)S(1)} reshape(bf16[32,96,10]{2,1,0:T(8,128)(2,1)} %slice.108) | data formatting | bytes 122880 | tf_op jit(solution)/shard_map/reshape | solution.py:107
  120.0 0.9 reshape.156
  120.9 1.2 fusion.17
  122.9 16.6 %all-to-all-done.1 = bf16[16,256,196]{1,2,0:T(8,128)(2,1)} async-done(((bf16[16,256,196]{1,2,0:T(8,128)(2,1)}), bf16[16,256,196]{1,2,0:T(8,128)(2,1)}, u32[]{:S(2)}, u32[]{:S(2)}) %all-to-all-start.1) | async-done | bytes 1605664 | tf_op jit(solution)/shard_map/all_to_all | solution.py:155
  139.5 1.7 convert_element_type.114
  141.2 1.7 copy-done
  143.7 1.1 copy.35
  144.8 0.9 slice_reduce_fusion.2
  146.0 3.3 %collective-permute-start.1 = (bf16[3,64,192]{2,1,0:T(8,128)(2,1)S(1)}, bf16[3,64,192]{2,1,0:T(8,128)(2,1)S(1)}, u32[]{:S(2)}, u32[]{:S(2)}) collective-permute-start(bf16[3,64,192]{2,1,0:T(8,128)(2,1)S(1)} %bitcast.59), channel_id=1, source_target_pairs={{16,0},{32,16},{48,32},{64,48},{80,64},{96,80},{112,96},{128,112},... | collective-permute-start | bytes 221192 | tf_op jit(solution)/shard_map/ppermute | solution.py:170
  149.3 2.9 %collective-permute-start = (bf16[3,64,192]{2,1,0:T(8,128)(2,1)S(1)}, bf16[3,64,192]{2,1,0:T(8,128)(2,1)S(1)}, u32[]{:S(2)}, u32[]{:S(2)}) collective-permute-start(bf16[3,64,192]{2,1,0:T(8,128)(2,1)S(1)} %bitcast.58), channel_id=1, source_target_pairs={{0,16},{16,32},{32,48},{48,64},{64,80},{80,96},{96,112},{112,128},... | collective-permute-start | bytes 221192 | tf_op jit(solution)/shard_map/ppermute | solution.py:169
  152.6 1.1 collective-permute-done
  154.6 7.0 %shard_map.137 = (bf16[4,64,192]{2,1,0:T(8,128)(2,1)}, f32[49,192]{1,0:T(8,128)}) custom-call(bf16[10,70,192]{2,1,0:T(8,128)(2,1)} %fusion.16.tall_ref, bf16[4,64,192]{2,1,0:T(8,128)(2,1)} %bitcast.55, bf16[4,64,192]{2,1,0:T(8,128)(2,1)} %bitcast.54, f32[49,192]{1,0:T(8,128)} %copy.40.kernel_ref), custom_call_target="tpu_custom_call" | custom-call | tf_op jit(solution)/shard_map/pallas_call | solution.py:58
  161.6 0.9 copy.41
  163.6 8.5 %all-to-all-start.2 = ((f32[32,1,678]{2,1,0:T(1,128)}), f32[32,1,678]{2,1,0:T(1,128)S(1)}, u32[]{:S(2)}, u32[]{:S(2)}) async-start(f32[32,1,678]{2,1,0:T(1,128)} %all_to_all.14), calls=%async_computation.2 | async-start | bytes 196608 | tf_op jit(solution)/shard_map/all_to_all | solution.py:185
  172.1 1.6 copy.45
  173.7 11.8 %all-to-all-done.2 = f32[32,1,678]{2,1,0:T(1,128)S(1)} async-done(((f32[32,1,678]{2,1,0:T(1,128)}), f32[32,1,678]{2,1,0:T(1,128)S(1)}, u32[]{:S(2)}, u32[]{:S(2)}) %all-to-all-start.2) | async-done | bytes 86816 | tf_op jit(solution)/shard_map/all_to_all | solution.py:185
  187.0 20.9 %reduce-scatter.2.cloned.1.call-done = bf16[96,384]{1,0:T(8,128)(2,1)} async-done(((bf16[3072,384]{1,0:T(8,128)(2,1)}), bf16[96,384]{1,0:T(8,128)(2,1)}) %reduce-scatter.2.cloned.1.call-update) | async-done | bytes 73744 | tf_op jit(solution)/shard_map/reduce_scatter | solution.py:137
  (59 shorter events, 10.9 us)
Async XLA Ops:
  7.2 84.8 %all-gather.3.cloned.1.call-start = ((), (), s32[]{:S(2)}) async-start(), calls=%async_computation.5 | async-start | bytes 5677056 | tf_op jit(solution)/shard_map/all_gather | solution.py:27
  10.0 197.9 %reduce-scatter.2.cloned.1.call-start = ((), (), s32[]{:S(2)}) async-start(), calls=%async_computation.4 | async-start | bytes 2433024 | tf_op jit(solution)/shard_map/reduce_scatter | solution.py:137
  92.0 3.0 %copy-start.2 = (bf16[16,256,192]{1,2,0:T(8,128)(2,1)S(1)}, bf16[16,256,192]{1,2,0:T(8,128)(2,1)}, u32[]{:S(2)}) copy-start(bf16[16,256,192]{1,2,0:T(8,128)(2,1)} %get-tuple-element.34) | copy-start | bytes 4718596
  92.0 3.0 %copy-start.7 = (bf16[256,384]{1,0:T(8,128)(2,1)S(1)}, bf16[256,384]{1,0:T(8,128)(2,1)}, u32[]{:S(2)}) copy-start(bf16[256,384]{1,0:T(8,128)(2,1)} %param.12) | copy-start | bytes 589828
  95.0 1.9 copy-start.1
  95.0 1.9 copy-start.5
  96.9 2.5 %copy-start.6 = (f32[3072]{0:T(1024)S(1)}, f32[3072]{0:T(1024)}, u32[]{:S(2)}) copy-start(f32[3072]{0:T(1024)} %param.16) | copy-start | bytes 36868
  104.5 9.4 %copy-start.3 = (bf16[256,192]{0,1:T(8,128)(2,1)S(1)}, bf16[256,192]{0,1:T(8,128)(2,1)}, u32[]{:S(2)}) copy-start(bf16[256,192]{0,1:T(8,128)(2,1)} %param.13) | copy-start | bytes 294916
  104.5 10.3 %copy-start.4 = (bf16[256,192]{0,1:T(8,128)(2,1)S(1)}, bf16[256,192]{0,1:T(8,128)(2,1)}, u32[]{:S(2)}) copy-start(bf16[256,192]{0,1:T(8,128)(2,1)} %param.10) | copy-start | bytes 294916
  107.4 32.2 %all-to-all-start.1 = ((bf16[16,256,196]{1,2,0:T(8,128)(2,1)}), bf16[16,256,196]{1,2,0:T(8,128)(2,1)}, u32[]{:S(2)}, u32[]{:S(2)}) async-start(bf16[16,256,196]{1,2,0:T(8,128)(2,1)} %pad_maximum_fusion), calls=%async_computation.1 | async-start | bytes 3276800 | tf_op jit(solution)/shard_map/all_to_all | solution.py:155
  141.2 1.7 copy-start
  146.0 6.6 %collective-permute-start.1 = (bf16[3,64,192]{2,1,0:T(8,128)(2,1)S(1)}, bf16[3,64,192]{2,1,0:T(8,128)(2,1)S(1)}, u32[]{:S(2)}, u32[]{:S(2)}) collective-permute-start(bf16[3,64,192]{2,1,0:T(8,128)(2,1)S(1)} %bitcast.59), channel_id=1, source_target_pairs={{16,0},{32,16},{48,32},{64,48},{80,64},{96,80},{112,96},{128,112},... | collective-permute-start | bytes 221192 | tf_op jit(solution)/shard_map/ppermute | solution.py:170
  149.3 4.5 %collective-permute-start = (bf16[3,64,192]{2,1,0:T(8,128)(2,1)S(1)}, bf16[3,64,192]{2,1,0:T(8,128)(2,1)S(1)}, u32[]{:S(2)}, u32[]{:S(2)}) collective-permute-start(bf16[3,64,192]{2,1,0:T(8,128)(2,1)S(1)} %bitcast.58), channel_id=1, source_target_pairs={{0,16},{16,32},{32,48},{48,64},{64,80},{80,96},{96,112},{112,128},... | collective-permute-start | bytes 221192 | tf_op jit(solution)/shard_map/ppermute | solution.py:169
  163.6 22.0 %all-to-all-start.2 = ((f32[32,1,678]{2,1,0:T(1,128)}), f32[32,1,678]{2,1,0:T(1,128)S(1)}, u32[]{:S(2)}, u32[]{:S(2)}) async-start(f32[32,1,678]{2,1,0:T(1,128)} %all_to_all.14), calls=%async_computation.2 | async-start | bytes 196608 | tf_op jit(solution)/shard_map/all_to_all | solution.py:185
Sparse Core Ops, SparseCore 0:
  10.1 81.8 all-gather.2
  102.0 105.9 reduce-scatter.1

commit v4 on v3

--- a/solution.py
+++ b/solution.py
@@ -3,14 +3,16 @@
 from jax import lax
 from jax.experimental import pallas as pl
 from jax.experimental.pallas import tpu as pltpu
-from jax.sharding import PartitionSpec as P
+from jax.sharding import Mesh, PartitionSpec as P
 
 KS = 7
 H = 64
 HALO = KS // 2
 
 WEIGHTS_VIA = "gather"
-DWIN_VIA = "rs"
+DWIN_VIA = "two_level"
+ROW = ("z", "core")
+SWAP = [(0, 1), (1, 0)]
 ACTS_VIA = "a2a"
 
 
@@ -91,7 +93,7 @@
     few = conv_kernel.shape[1]
     rows = tokens // H
     col_rank = lax.axis_index("col")
-    row_rank = lax.axis_index("row")
+    row_rank = lax.axis_index(ROW)
 
     scaled = (cotangent.astype(jnp.float32) * layer_scale).astype(jnp.bfloat16)
     acts = gather_blocks(jnp.concatenate([scaled, conv_out], axis=1), "col", n_col, ACTS_VIA)
@@ -100,7 +102,7 @@
     kernel_bits = jnp.pad(kernel_bits, (0, lanes_extra * w_in.shape[0] - kernel_bits.shape[0]))
     weights = gather_blocks(
         jnp.concatenate([w_out, w_in, kernel_bits.reshape(w_in.shape[0], lanes_extra)], axis=1),
-        "row",
+        ROW,
         n_row,
         WEIGHTS_VIA,
     )
@@ -130,11 +132,26 @@
     ).astype(jnp.bfloat16)
     if DWIN_VIA == "a2a":
         parts_w = lax.all_to_all(
-            block_w.reshape(n_row, width // n_row, hidden), "row", 0, 0, tiled=True
+            block_w.reshape(n_row, width // n_row, hidden), ROW, 0, 0, tiled=True
         )
         d_w_in = jnp.sum(parts_w.astype(jnp.float32), axis=0).astype(jnp.bfloat16)
+    elif DWIN_VIA == "two_level":
+        core = lax.axis_index("core")
+        halves = block_w.reshape(width, 2, hidden // 2)
+        kept = lax.dynamic_index_in_dim(halves, core, axis=1, keepdims=False)
+        given = lax.dynamic_index_in_dim(halves, 1 - core, axis=1, keepdims=False)
+        chip_sum = (kept.astype(jnp.float32) + lax.ppermute(given, "core", SWAP).astype(jnp.float32))
+        chip_rows = lax.psum_scatter(chip_sum.astype(jnp.bfloat16), "z", scatter_dimension=0, tiled=True)
+        chip_rows = chip_rows.reshape(2, width // n_row, hidden // 2)
+        own = lax.dynamic_index_in_dim(chip_rows, core, axis=0, keepdims=False)
+        other = lax.ppermute(
+            lax.dynamic_index_in_dim(chip_rows, 1 - core, axis=0, keepdims=False), "core", SWAP
+        )
+        d_w_in = jnp.where(
+            core == 0, jnp.concatenate([own, other], axis=1), jnp.concatenate([other, own], axis=1)
+        )
     else:
-        d_w_in = lax.psum_scatter(block_w, "row", scatter_dimension=0, tiled=True)
+        d_w_in = lax.psum_scatter(block_w, ROW, scatter_dimension=0, tiled=True)
 
     block_n = lax.dot_general(
         grad_pre, w_in_full, (((1,), (1,)), ((), ())), preferred_element_type=jnp.float32
@@ -166,8 +183,8 @@
     grid = grad_conv.reshape(rows, H, channels)
     down_pairs = [(i, i + 1) for i in range(n_row) if (i + 1) % per_image != 0]
     up_pairs = [(i + 1, i) for i in range(n_row) if (i + 1) % per_image != 0]
-    from_above = lax.ppermute(grid[rows - HALO :], "row", down_pairs)
-    from_below = lax.ppermute(grid[:HALO], "row", up_pairs)
+    from_above = lax.ppermute(grid[rows - HALO :], ROW, down_pairs)
+    from_below = lax.ppermute(grid[:HALO], ROW, up_pairs)
     tall = jnp.concatenate([from_above, grid, from_below], axis=0)
     padded = jnp.pad(tall, ((0, 0), (HALO, HALO), (0, 0)))
     d_input, kernel_sums = conv_call(
@@ -182,7 +199,7 @@
     kernel_part = jnp.transpose(kernel_part, (1, 0, 2)).reshape(n_row, KS * KS * few)
     norm_part = jnp.broadcast_to(jnp.concatenate([gain_part, bias_part])[None], (n_row, 2 * channels))
     reduced = jnp.sum(
-        lax.all_to_all(jnp.concatenate([kernel_part, norm_part], axis=1), "row", 0, 0, tiled=True),
+        lax.all_to_all(jnp.concatenate([kernel_part, norm_part], axis=1), ROW, 0, 0, tiled=True),
         axis=0,
     )
     d_kernel = reduced[: KS * KS * few].reshape(KS * KS, few)
@@ -192,21 +209,23 @@
 
 
 def solution(mesh):
+    devices = mesh.devices
+    split = Mesh(devices.reshape(devices.shape[0] // 2, 2, devices.shape[1]), ROW + ("col",))
     return jax.shard_map(
         body,
-        mesh=mesh,
+        mesh=split,
         in_specs=(
-            P("row", "col"),
-            P("row", "col"),
-            P("row", "col"),
-            P("row", "col"),
-            P(None, ("col", "row")),
+            P(ROW, "col"),
+            P(ROW, "col"),
+            P(ROW, "col"),
+            P(ROW, "col"),
+            P(None, ("col",) + ROW),
             P(),
             P(),
             P("col"),
-            P("row", "col"),
-            P("row", "col"),
+            P(ROW, "col"),
+            P(ROW, "col"),
         ),
-        out_specs=(P("row", "col"), P(None, ("col", "row")), P("col"), P("col"), P("row", "col")),
+        out_specs=(P(ROW, "col"), P(None, ("col",) + ROW), P("col"), P("col"), P(ROW, "col")),
         check_vma=False,
     )

time: 218 us -> 207 us (0.950)
  blocking collectives: 46.5 us -> 0 us
  starting transfers between devices: 21.4 us -> 38 us
  waiting for transfers between devices: 76.9 us -> 87.8 us
  local copies, waits for them, and re-layouts: 26.3 us -> 33.9 us
  other arithmetic: 16.5 us -> 20.4 us
    all_to_all x1 -> x0, blocking collectives: 46.5 us -> none  [gather_blocks(): return lax.all_to_all(wide, axis_name, 0, 0, tiled=True)]
    all_to_all x1 -> x2, waiting for transfers between devices: 11.8 us -> 51.2 us  [the longest x1 39.7 us: gather_blocks(): return lax.all_to_all(wide, axis_name, 0, 0, tiled=True)]
    reduce_scatter x1 -> x0, waiting for transfers between devices: 20.9 us -> none  [body(): d_w_in = lax.psum_scatter(block_w, 'row', scatter_dimension=0, tiled=True)]
    ppermute x2 -> x4, starting transfers between devices: 6.19 us -> 15.7 us  [the longest x1 7.29 us: body(): lax.ppermute(lax.dynamic_index_in_dim(chip_rows, 1 - core, axis=0, keepdi...]
    all_to_all x1 -> x2, starting transfers between devices: 8.51 us -> 15.6 us  [the longest x1 7.97 us: body(): lax.all_to_all(jnp.concatenate([kernel_part, norm_part], axis=1), ROW, 0,...]
    all_to_all x1, waiting for transfers between devices: 16.6 us -> 10.9 us  [body(): lax.all_to_all(outgoing, 'col', 0, 0, tiled=True).astype(jnp.float32)]
    unnamed x21 -> x24, local copies, waits for them, and re-layouts: 6.46 us -> 10.4 us
    convert_element_type x0 -> x1, other arithmetic: none -> 3.13 us  [body(): chip_sum.astype(jnp.bfloat16)]
  transfers between devices with their start and end apart: 6 -> 9, of which waited for: 6 -> 6; matrix products, arithmetic and copies ran while one was open for 16% -> 20% of each run, Pallas kernels for 3% -> 3%
where the time goes in v4:
time: 207 us; the launch traced here: 206 us
  waiting for transfers between devices  87.8 us (42%)
  starting transfers between devices  38 us (18%)
  local copies, waits for them, and re-layouts  33.9 us (16%)
  other arithmetic  20.4 us (10%)
  between operations  14.3 us (7%)
  Pallas kernels  7.01 us (3%)
  matrix products  4.4 us (2%)
    all_to_all x1, waiting for transfers between devices, gather_blocks(): return lax.all_to_all(wide, axis_name, 0, 0, tiled=True)  39.7 us
    all_gather x1, waiting for transfers between devices, gather_blocks(): return lax.all_gather(x, axis_name, axis=0, tiled=False)  23.5 us
    all_to_all x1, waiting for transfers between devices, body(): lax.all_to_all(jnp.concatenate([kernel_part, norm_part], axis=1), ROW, 0,...  11.5 us
    all_to_all x1, waiting for transfers between devices, body(): lax.all_to_all(outgoing, 'col', 0, 0, tiled=True).astype(jnp.float32)  10.9 us
    unnamed x24, local copies, waits for them, and re-layouts  10.4 us
    all_to_all x1, starting transfers between devices, body(): lax.all_to_all(jnp.concatenate([kernel_part, norm_part], axis=1), ROW, 0,...  7.97 us
    all_to_all x1, starting transfers between devices, gather_blocks(): return lax.all_to_all(wide, axis_name, 0, 0, tiled=True)  7.58 us
    ppermute x1, starting transfers between devices, body(): lax.ppermute(lax.dynamic_index_in_dim(chip_rows, 1 - core, axis=0, keepdi...  7.29 us
  transfers between devices with their start and end apart: 9, of which 6 were waited for; matrix products, arithmetic and copies ran while one was open for 20% of the time, Pallas kernels for 3%

profile of v4, /device:TPU:1, one launch (start us, length us, event | category | flops | bytes accessed | tf_op | source)
XLA Modules:
  0.0 205.8 jit_solution(12056448876618093933)
XLA Ops:
  8.4 1.6 pad_maximum_fusion.2
  11.9 2.0 broadcast_in_dim.6
  13.9 7.6 %all-to-all-start = ((bf16[16,256,384]{1,2,0:T(8,128)(2,1)}), bf16[16,256,384]{1,2,0:T(8,128)(2,1)S(1)}, u32[]{:S(2)}, u32[]{:S(2)}) async-start(bf16[16,256,384]{1,2,0:T(8,128)(2,1)} %broadcast_in_dim.6), calls=%async_computation | async-start | bytes 6291456 | tf_op jit(solution)/shard_map/all_to_all | solution.py:28
  21.5 39.7 %all-to-all-done = bf16[16,256,384]{1,2,0:T(8,128)(2,1)S(1)} async-done(((bf16[16,256,384]{1,2,0:T(8,128)(2,1)}), bf16[16,256,384]{1,2,0:T(8,128)(2,1)S(1)}, u32[]{:S(2)}, u32[]{:S(2)}) %all-to-all-start) | async-done | bytes 3145760 | tf_op jit(solution)/shard_map/all_to_all | solution.py:28
  61.3 2.7 %slice_convert_fusion = (f32[16,256,192]{1,2,0:T(8,128)}, bf16[16,256,192]{1,2,0:T(8,128)(2,1)}) fusion(bf16[16,256,384]{1,2,0:T(8,128)(2,1)S(1)} %all-to-all-done), kind=kLoop, calls=%fused_computation.13 | loop fusion | flops 786432 | bytes 7864320 | tf_op jit(solution)/shard_map/convert_element_type | solution.py:118
  63.9 3.6 %copy.38 = f32[256,3072]{1,0:T(8,128)} copy(f32[256,3072]{0,1:T(8,128)} %bitcast.58) | data formatting | bytes 6291456 | tf_op jit(solution)/shard_map/convert_element_type | solution.py:118
  68.5 23.5 %all-gather.3.cloned.1.call-done = bf16[3072,778]{1,0:T(8,128)(2,1)} async-done(((bf16[96,778]{1,0:T(8,128)(2,1)}), bf16[3072,778]{1,0:T(8,128)(2,1)}) %all-gather.3.cloned.1.call-update) | async-done | bytes 4780048 | tf_op jit(solution)/shard_map/all_gather | solution.py:29
  92.0 3.0 %fusion.27 = (bf16[32,96,384]{2,1,0:T(8,128)(2,1)S(1)}, bf16[32,96,384]{2,1,0:T(8,128)(2,1)S(1)}) fusion(bf16[32,96,778]{2,1,0:T(8,128)(2,1)} %bitcast.63), kind=kLoop, calls=%fused_computation.74 | loop fusion | bytes 9437184 | tf_op jit(solution)/shard_map/slice | solution.py:116
  95.0 1.1 fusion.5
  96.9 2.5 %fusion = (f32[256]{0:T(256)S(1)}, f32[256]{0:T(256)S(1)}, f32[256,3072]{1,0:T(8,128)S(1)}, bf16[256,3072]{1,0:T(8,128)(2,1)}) fusion(f32[3072]{0:T(1024)S(1)} %copy-done.6, f32[256]{0:T(256)S(1)} %add_rsqrt_fusion, f32[256,3072]{1,0:T(8,128)S(1)} %copy-done.1, f32[256]{0:T(256)S(1)} %broadcast_multiply_fusion, bf16[256,384]{1,0:T(8,128)(2,1)S(1)} %fusion.5, ...), kind=kOutput, calls=%fused_computation.6 | convolution fusion | flops 610270720 | bytes 10436608 | tf_op jit(solution)/shard_map/dot_general | solution.py:156
  100.3 1.4 copy-done.2
  101.6 1.2 dynamic-slice_bitcast_fusion
  102.8 2.2 %collective-permute-start.2 = (bf16[3072,192]{0,1:T(8,128)(2,1)}, bf16[3072,192]{0,1:T(8,128)(2,1)}, u32[]{:S(2)}, u32[]{:S(2)}) collective-permute-start(bf16[3072,192]{0,1:T(8,128)(2,1)} %dynamic-slice_bitcast_fusion), channel_id=1, source_target_pairs={{0,16},{16,0},{1,17},{17,1},{2,18},{18,2},{3,19},{19,3},{4,20},{20... | collective-permute-start | bytes 3538952 | tf_op jit(solution)/shard_map/ppermute | solution.py:143
  105.0 2.6 %copy.37 = bf16[256,3072]{0,1:T(8,128)(2,1)} copy(bf16[256,3072]{1,0:T(8,128)(2,1)} %get-tuple-element.50) | data formatting | bytes 3145728 | tf_op jit(solution)/shard_map/convert_element_type | solution.py:158
  107.6 2.8 %pad_maximum_fusion = bf16[16,256,196]{1,2,0:T(8,128)(2,1)} fusion(bf16[16,256,4]{1,2,0:T(4,128)(2,1)S(1)} %broadcast_in_dim.7, bf16[16,256,192]{1,2,0:T(8,128)(2,1)} %bitcast.62), kind=kLoop, calls=%fused_computation.12 | loop fusion | flops 3211264 | bytes 3211264 | tf_op jit(solution)/shard_map/concatenate | solution.py:165
  110.4 6.7 %all-to-all-start.1 = ((bf16[16,256,196]{1,2,0:T(8,128)(2,1)}), bf16[16,256,196]{1,2,0:T(8,128)(2,1)}, u32[]{:S(2)}, u32[]{:S(2)}) async-start(bf16[16,256,196]{1,2,0:T(8,128)(2,1)} %pad_maximum_fusion), calls=%async_computation.1 | async-start | bytes 3276800 | tf_op jit(solution)/shard_map/all_to_all | solution.py:172
  117.1 3.1 %fusion.1 = bf16[3072,192]{0,1:T(8,128)(2,1)} fusion(bf16[3072,192]{0,1:T(8,128)(2,1)} %collective-permute-done.2, bf16[3072,2,192]{0,2,1:T(8,128)(2,1)} %bitcast.60, s32[]{:T(128)S(6)} %select_n.24), kind=kLoop, calls=%fused_computation.11 | loop fusion | flops 2359296 | bytes 3538948 | tf_op jit(solution)/shard_map/convert_element_type | solution.py:144
  120.3 2.5 %copy.53 = bf16[3072,192]{1,0:T(8,128)(2,1)} copy(bf16[3072,192]{0,1:T(8,128)(2,1)} %fusion.1) | data formatting | bytes 2359296
  124.4 2.1 slice.108
  126.5 2.2 %reshape.171 = bf16[32,960]{1,0:T(8,128)(2,1)S(1)} reshape(bf16[32,96,10]{2,1,0:T(8,128)(2,1)} %slice.108) | data formatting | bytes 122880 | tf_op jit(solution)/shard_map/reshape | solution.py:109
  129.7 1.2 fusion.18
  131.8 10.9 %all-to-all-done.1 = bf16[16,256,196]{1,2,0:T(8,128)(2,1)} async-done(((bf16[16,256,196]{1,2,0:T(8,128)(2,1)}), bf16[16,256,196]{1,2,0:T(8,128)(2,1)}, u32[]{:S(2)}, u32[]{:S(2)}) %all-to-all-start.1) | async-done | bytes 1605664 | tf_op jit(solution)/shard_map/all_to_all | solution.py:172
  142.7 1.7 convert_element_type.126
  144.4 1.7 copy-done
  149.2 3.3 %collective-permute-start.1 = (bf16[3,64,192]{2,1,0:T(8,128)(2,1)S(1)}, bf16[3,64,192]{2,1,0:T(8,128)(2,1)S(1)}, u32[]{:S(2)}, u32[]{:S(2)}) collective-permute-start(bf16[3,64,192]{2,1,0:T(8,128)(2,1)S(1)} %bitcast.74), channel_id=1, source_target_pairs={{16,0},{32,16},{48,32},{64,48},{80,64},{96,80},{112,96},{128,112},... | collective-permute-start | bytes 221192 | tf_op jit(solution)/shard_map/ppermute | solution.py:187
  152.5 3.0 %collective-permute-start = (bf16[3,64,192]{2,1,0:T(8,128)(2,1)S(1)}, bf16[3,64,192]{2,1,0:T(8,128)(2,1)S(1)}, u32[]{:S(2)}, u32[]{:S(2)}) collective-permute-start(bf16[3,64,192]{2,1,0:T(8,128)(2,1)S(1)} %bitcast.73), channel_id=1, source_target_pairs={{0,16},{16,32},{32,48},{48,64},{64,80},{80,96},{96,112},{112,128},... | collective-permute-start | bytes 221192 | tf_op jit(solution)/shard_map/ppermute | solution.py:186
  156.0 1.6 collective-permute-done
  158.5 7.0 %shard_map.137 = (bf16[4,64,192]{2,1,0:T(8,128)(2,1)}, f32[49,192]{1,0:T(8,128)}) custom-call(bf16[10,70,192]{2,1,0:T(8,128)(2,1)} %fusion.17.tall_ref, bf16[4,64,192]{2,1,0:T(8,128)(2,1)} %bitcast.69, bf16[4,64,192]{2,1,0:T(8,128)(2,1)} %bitcast.68, f32[49,192]{1,0:T(8,128)} %copy.44.kernel_ref), custom_call_target="tpu_custom_call" | custom-call | tf_op jit(solution)/shard_map/pallas_call | solution.py:60
  167.4 8.0 %all-to-all-start.2 = ((f32[32,1,678]{2,1,0:T(1,128)}), f32[32,1,678]{2,1,0:T(1,128)S(1)}, u32[]{:S(2)}, u32[]{:S(2)}) async-start(f32[32,1,678]{2,1,0:T(1,128)} %all_to_all.14), calls=%async_computation.2 | async-start | bytes 196608 | tf_op jit(solution)/shard_map/all_to_all | solution.py:202
  175.4 1.7 copy.51
  177.1 11.5 %all-to-all-done.2 = f32[32,1,678]{2,1,0:T(1,128)S(1)} async-done(((f32[32,1,678]{2,1,0:T(1,128)}), f32[32,1,678]{2,1,0:T(1,128)S(1)}, u32[]{:S(2)}, u32[]{:S(2)}) %all-to-all-start.2) | async-done | bytes 86816 | tf_op jit(solution)/shard_map/all_to_all | solution.py:202
  189.5 7.3 %collective-permute-start.3 = (bf16[96,192]{1,0:T(8,128)(2,1)S(1)}, bf16[96,192]{1,0:T(8,128)(2,1)S(1)}, u32[]{:S(2)}, u32[]{:S(2)}) collective-permute-start(bf16[96,192]{1,0:T(8,128)(2,1)S(1)} %get-tuple-element.38), channel_id=1, source_target_pairs={{0,16},{16,0},{1,17},{17,1},{2,18},{18,2},{3,19},{19,3},{4,20},{20... | collective-permute-start | bytes 110600 | tf_op jit(solution)/shard_map/ppermute | solution.py:147
  (71 shorter events, 18.9 us)
Async XLA Ops:
  7.2 84.8 %all-gather.3.cloned.1.call-start = ((), (), s32[]{:S(2)}) async-start(), calls=%async_computation.4 | async-start | bytes 5677056 | tf_op jit(solution)/shard_map/all_gather | solution.py:29
  13.9 47.3 %all-to-all-start = ((bf16[16,256,384]{1,2,0:T(8,128)(2,1)}), bf16[16,256,384]{1,2,0:T(8,128)(2,1)S(1)}, u32[]{:S(2)}, u32[]{:S(2)}) async-start(bf16[16,256,384]{1,2,0:T(8,128)(2,1)} %broadcast_in_dim.6), calls=%async_computation | async-start | bytes 6291456 | tf_op jit(solution)/shard_map/all_to_all | solution.py:28
  92.0 3.0 %copy-start.3 = (bf16[16,256,192]{1,2,0:T(8,128)(2,1)S(1)}, bf16[16,256,192]{1,2,0:T(8,128)(2,1)}, u32[]{:S(2)}) copy-start(bf16[16,256,192]{1,2,0:T(8,128)(2,1)} %get-tuple-element.34) | copy-start | bytes 4718596
  92.0 3.0 %copy-start.8 = (bf16[256,384]{1,0:T(8,128)(2,1)S(1)}, bf16[256,384]{1,0:T(8,128)(2,1)}, u32[]{:S(2)}) copy-start(bf16[256,384]{1,0:T(8,128)(2,1)} %param.12) | copy-start | bytes 589828
  95.0 1.9 copy-start.1
  95.0 1.9 copy-start.6
  96.9 2.5 %copy-start.7 = (f32[3072]{0:T(1024)S(1)}, f32[3072]{0:T(1024)}, u32[]{:S(2)}) copy-start(f32[3072]{0:T(1024)} %param.16) | copy-start | bytes 36868
  100.2 1.4 copy-start.2
  102.8 14.3 %collective-permute-start.2 = (bf16[3072,192]{0,1:T(8,128)(2,1)}, bf16[3072,192]{0,1:T(8,128)(2,1)}, u32[]{:S(2)}, u32[]{:S(2)}) collective-permute-start(bf16[3072,192]{0,1:T(8,128)(2,1)} %dynamic-slice_bitcast_fusion), channel_id=1, source_target_pairs={{0,16},{16,0},{1,17},{17,1},{2,18},{18,2},{3,19},{19,3},{4,20},{20... | collective-permute-start | bytes 3538952 | tf_op jit(solution)/shard_map/ppermute | solution.py:143
  110.4 32.3 %all-to-all-start.1 = ((bf16[16,256,196]{1,2,0:T(8,128)(2,1)}), bf16[16,256,196]{1,2,0:T(8,128)(2,1)}, u32[]{:S(2)}, u32[]{:S(2)}) async-start(bf16[16,256,196]{1,2,0:T(8,128)(2,1)} %pad_maximum_fusion), calls=%async_computation.1 | async-start | bytes 3276800 | tf_op jit(solution)/shard_map/all_to_all | solution.py:172
  117.1 71.6 %reduce-scatter.4.cloned.1.call-start = ((), (), s32[]{:S(2)}) async-start(), calls=%async_computation.5 | async-start | bytes 1671168
  120.3 2.6 %copy-start.4 = (bf16[256,192]{0,1:T(8,128)(2,1)S(1)}, bf16[256,192]{0,1:T(8,128)(2,1)}, u32[]{:S(2)}) copy-start(bf16[256,192]{0,1:T(8,128)(2,1)} %param.13) | copy-start | bytes 294916
  120.3 3.4 %copy-start.5 = (bf16[256,192]{0,1:T(8,128)(2,1)S(1)}, bf16[256,192]{0,1:T(8,128)(2,1)}, u32[]{:S(2)}) copy-start(bf16[256,192]{0,1:T(8,128)(2,1)} %param.10) | copy-start | bytes 294916
  144.4 1.7 copy-start
  149.2 6.8 %collective-permute-start.1 = (bf16[3,64,192]{2,1,0:T(8,128)(2,1)S(1)}, bf16[3,64,192]{2,1,0:T(8,128)(2,1)S(1)}, u32[]{:S(2)}, u32[]{:S(2)}) collective-permute-start(bf16[3,64,192]{2,1,0:T(8,128)(2,1)S(1)} %bitcast.74), channel_id=1, source_target_pairs={{16,0},{32,16},{48,32},{64,48},{80,64},{96,80},{112,96},{128,112},... | collective-permute-start | bytes 221192 | tf_op jit(solution)/shard_map/ppermute | solution.py:187
  152.5 5.1 %collective-permute-start = (bf16[3,64,192]{2,1,0:T(8,128)(2,1)S(1)}, bf16[3,64,192]{2,1,0:T(8,128)(2,1)S(1)}, u32[]{:S(2)}, u32[]{:S(2)}) collective-permute-start(bf16[3,64,192]{2,1,0:T(8,128)(2,1)S(1)} %bitcast.73), channel_id=1, source_target_pairs={{0,16},{16,32},{32,48},{48,64},{64,80},{80,96},{96,112},{112,128},... | collective-permute-start | bytes 221192 | tf_op jit(solution)/shard_map/ppermute | solution.py:186
  167.4 21.1 %all-to-all-start.2 = ((f32[32,1,678]{2,1,0:T(1,128)}), f32[32,1,678]{2,1,0:T(1,128)S(1)}, u32[]{:S(2)}, u32[]{:S(2)}) async-start(f32[32,1,678]{2,1,0:T(1,128)} %all_to_all.14), calls=%async_computation.2 | async-start | bytes 196608 | tf_op jit(solution)/shard_map/all_to_all | solution.py:202
  189.5 8.7 %collective-permute-start.3 = (bf16[96,192]{1,0:T(8,128)(2,1)S(1)}, bf16[96,192]{1,0:T(8,128)(2,1)S(1)}, u32[]{:S(2)}, u32[]{:S(2)}) collective-permute-start(bf16[96,192]{1,0:T(8,128)(2,1)S(1)} %get-tuple-element.38), channel_id=1, source_target_pairs={{0,16},{16,0},{1,17},{17,1},{2,18},{18,2},{3,19},{19,3},{4,20},{20... | collective-permute-start | bytes 110600 | tf_op jit(solution)/shard_map/ppermute | solution.py:147
Sparse Core Ops, SparseCore 0:
  10.1 81.8 all-gather.2
  123.0 60.3 reduce-scatter.3

commit v5 on v4

--- a/solution.py
+++ b/solution.py
@@ -10,7 +10,6 @@
 HALO = KS // 2
 
 WEIGHTS_VIA = "gather"
-DWIN_VIA = "two_level"
 ROW = ("z", "core")
 SWAP = [(0, 1), (1, 0)]
 ACTS_VIA = "a2a"
@@ -127,31 +126,24 @@
     grad_act = jnp.dot(scaled_full, w_out_full, preferred_element_type=jnp.float32)
     grad_pre = (grad_act * gelu_slope(hidden_pre.astype(jnp.float32))).astype(jnp.bfloat16)
 
-    block_w = lax.dot_general(
-        normed_full, grad_pre, (((0,), (0,)), ((), ())), preferred_element_type=jnp.float32
-    ).astype(jnp.bfloat16)
-    if DWIN_VIA == "a2a":
-        parts_w = lax.all_to_all(
-            block_w.reshape(n_row, width // n_row, hidden), ROW, 0, 0, tiled=True
-        )
-        d_w_in = jnp.sum(parts_w.astype(jnp.float32), axis=0).astype(jnp.bfloat16)
-    elif DWIN_VIA == "two_level":
-        core = lax.axis_index("core")
-        halves = block_w.reshape(width, 2, hidden // 2)
-        kept = lax.dynamic_index_in_dim(halves, core, axis=1, keepdims=False)
-        given = lax.dynamic_index_in_dim(halves, 1 - core, axis=1, keepdims=False)
-        chip_sum = (kept.astype(jnp.float32) + lax.ppermute(given, "core", SWAP).astype(jnp.float32))
-        chip_rows = lax.psum_scatter(chip_sum.astype(jnp.bfloat16), "z", scatter_dimension=0, tiled=True)
-        chip_rows = chip_rows.reshape(2, width // n_row, hidden // 2)
-        own = lax.dynamic_index_in_dim(chip_rows, core, axis=0, keepdims=False)
-        other = lax.ppermute(
-            lax.dynamic_index_in_dim(chip_rows, 1 - core, axis=0, keepdims=False), "core", SWAP
-        )
-        d_w_in = jnp.where(
-            core == 0, jnp.concatenate([own, other], axis=1), jnp.concatenate([other, own], axis=1)
-        )
-    else:
-        d_w_in = lax.psum_scatter(block_w, ROW, scatter_dimension=0, tiled=True)
+    core = lax.axis_index("core")
+    normed_pair = jnp.concatenate([normed_full, lax.ppermute(normed_full, "core", SWAP)], axis=0)
+    grad_halves = grad_pre.reshape(tokens, 2, hidden // 2)
+    kept = lax.dynamic_index_in_dim(grad_halves, core, axis=1, keepdims=False)
+    given = lax.dynamic_index_in_dim(grad_halves, 1 - core, axis=1, keepdims=False)
+    grad_pair = jnp.concatenate([kept, lax.ppermute(given, "core", SWAP)], axis=0)
+    chip_sum = lax.dot_general(
+        normed_pair, grad_pair, (((0,), (0,)), ((), ())), preferred_element_type=jnp.float32
+    )
+    chip_rows = lax.psum_scatter(chip_sum.astype(jnp.bfloat16), "z", scatter_dimension=0, tiled=True)
+    chip_rows = chip_rows.reshape(2, width // n_row, hidden // 2)
+    own = lax.dynamic_index_in_dim(chip_rows, core, axis=0, keepdims=False)
+    other = lax.ppermute(
+        lax.dynamic_index_in_dim(chip_rows, 1 - core, axis=0, keepdims=False), "core", SWAP
+    )
+    d_w_in = jnp.where(
+        core == 0, jnp.concatenate([own, other], axis=1), jnp.concatenate([other, own], axis=1)
+    )
 
     block_n = lax.dot_general(
         grad_pre, w_in_full, (((1,), (1,)), ((), ())), preferred_element_type=jnp.float32

time: 207 us -> 203 us (0.981)
  blocking collectives: 0 us -> 46.5 us
  waiting for transfers between devices: 87.8 us -> 44.7 us
  local copies, waits for them, and re-layouts: 33.9 us -> 27.6 us
  starting transfers between devices: 38 us -> 33 us
  matrix products: 4.4 us -> 7.51 us
    all_to_all x0 -> x1, blocking collectives: none -> 46.5 us  [gather_blocks(): return lax.all_to_all(wide, axis_name, 0, 0, tiled=True)]
    all_to_all x1 -> x0, waiting for transfers between devices: 39.7 us -> none  [gather_blocks(): return lax.all_to_all(wide, axis_name, 0, 0, tiled=True)]
    all_to_all x1 -> x0, starting transfers between devices: 7.58 us -> none  [gather_blocks(): return lax.all_to_all(wide, axis_name, 0, 0, tiled=True)]
    all_gather x1, waiting for transfers between devices: 23.5 us -> 18.7 us  [gather_blocks(): return lax.all_gather(x, axis_name, axis=0, tiled=False)]
    ppermute x1 -> x2, starting transfers between devices: 2.16 us -> 6.86 us  [the longest x1 4.4 us: body(): lax.ppermute(normed_full, 'core', SWAP)]
    unnamed x24 -> x21, local copies, waits for them, and re-layouts: 10.4 us -> 6.7 us
    all_to_all x1, waiting for transfers between devices: 11.5 us -> 14.8 us  [body(): lax.all_to_all(jnp.concatenate([kernel_part, norm_part], axis=1), ROW, 0,...]
    dot_general x1, matrix products: 0.84 us -> 4.11 us  [body(): lax.dot_general(normed_pair, grad_pair, (((0,), (0,)), ((), ())), preferr...]
  transfers between devices with their start and end apart: 9 -> 9, of which waited for: 6 -> 5; matrix products, arithmetic and copies ran while one was open for 20% -> 23% of each run, Pallas kernels for 3% -> 4%
where the time goes in v5:
time: 203 us; the launch traced here: 200 us
  blocking collectives  46.5 us (23%)
  waiting for transfers between devices  44.7 us (22%)
  starting transfers between devices  33 us (16%)
  local copies, waits for them, and re-layouts  27.6 us (14%)
  other arithmetic  19.2 us (9%)
  between operations  14.3 us (7%)
  matrix products  7.51 us (4%)
  Pallas kernels  7.01 us (3%)
    all_to_all x1, blocking collectives, gather_blocks(): return lax.all_to_all(wide, axis_name, 0, 0, tiled=True)  46.5 us
    all_gather x1, waiting for transfers between devices, gather_blocks(): return lax.all_gather(x, axis_name, axis=0, tiled=False)  18.7 us
    all_to_all x1, waiting for transfers between devices, body(): lax.all_to_all(jnp.concatenate([kernel_part, norm_part], axis=1), ROW, 0,...  14.8 us
    all_to_all x1, waiting for transfers between devices, body(): lax.all_to_all(outgoing, 'col', 0, 0, tiled=True).astype(jnp.float32)  8.83 us
    all_to_all x1, starting transfers between devices, body(): lax.all_to_all(jnp.concatenate([kernel_part, norm_part], axis=1), ROW, 0,...  8.63 us
    pallas_call x1, Pallas kernels, conv_call(): pl.pallas_call(conv_body, out_shape=(jax.ShapeDtypeStruct((rows, span, ch...  7.01 us
    unnamed x21, local copies, waits for them, and re-layouts  6.7 us
    all_to_all x1, starting transfers between devices, body(): lax.all_to_all(outgoing, 'col', 0, 0, tiled=True).astype(jnp.float32)  6.59 us
  transfers between devices with their start and end apart: 9, of which 5 were waited for; matrix products, arithmetic and copies ran while one was open for 23% of the time, Pallas kernels for 4%

profile of v5, /device:TPU:1, one launch (start us, length us, event | category | flops | bytes accessed | tf_op | source)
XLA Modules:
  0.0 199.8 jit_solution(14400293369215576520)
XLA Ops:
  8.4 1.6 pad_maximum_fusion.2
  10.0 1.0 multiply_convert_fusion.1
  12.2 46.5 %all_to_all.19 = bf16[16,256,384]{1,2,0:T(8,128)(2,1)S(1)} all-to-all(bf16[16,256,384]{1,2,0:T(8,128)(2,1)S(1)} %broadcast_in_dim.6), channel_id=1, replica_groups=mesh['z'=16,'core'=2,'col'=16] {'col'}, dimensions={0} | all-to-all | bytes 6291456 | tf_op jit(solution)/shard_map/all_to_all | solution.py:27
  58.7 2.6 %slice_convert_fusion = (f32[16,256,192]{1,2,0:T(8,128)}, bf16[16,256,192]{1,2,0:T(8,128)(2,1)}) fusion(bf16[16,256,384]{1,2,0:T(8,128)(2,1)S(1)} %all_to_all.19), kind=kLoop, calls=%fused_computation.14 | loop fusion | flops 786432 | bytes 7864320 | tf_op jit(solution)/shard_map/convert_element_type | solution.py:117
  61.3 3.7 %copy.35 = f32[256,3072]{1,0:T(8,128)} copy(f32[256,3072]{0,1:T(8,128)} %bitcast.55) | data formatting | bytes 6291456 | tf_op jit(solution)/shard_map/convert_element_type | solution.py:117
  65.9 1.0 copy-done.1
  66.9 2.0 add_convert_fusion
  68.9 4.4 %collective-permute-start.2 = (bf16[256,3072]{1,0:T(8,128)(2,1)}, bf16[256,3072]{1,0:T(8,128)(2,1)}, u32[]{:S(2)}, u32[]{:S(2)}) collective-permute-start(bf16[256,3072]{1,0:T(8,128)(2,1)} %get-tuple-element.28), channel_id=1, source_target_pairs={{0,16},{16,0},{1,17},{17,1},{2,18},{18,2},{3,19},{19,3},{4,20},{20... | collective-permute-start | bytes 4718600 | tf_op jit(solution)/shard_map/ppermute | solution.py:130
  73.3 18.7 %all-gather.3.cloned.1.call-done = bf16[3072,778]{1,0:T(8,128)(2,1)} async-done(((bf16[96,778]{1,0:T(8,128)(2,1)}), bf16[3072,778]{1,0:T(8,128)(2,1)}) %all-gather.3.cloned.1.call-update) | async-done | bytes 4780048 | tf_op jit(solution)/shard_map/all_gather | solution.py:28
  92.0 3.0 %fusion.31 = (bf16[32,96,384]{2,1,0:T(8,128)(2,1)S(1)}, bf16[32,96,384]{2,1,0:T(8,128)(2,1)S(1)}) fusion(bf16[32,96,778]{2,1,0:T(8,128)(2,1)} %bitcast.58), kind=kLoop, calls=%fused_computation.78 | loop fusion | bytes 9437184 | tf_op jit(solution)/shard_map/slice | solution.py:115
  95.0 1.1 fusion.5
  96.1 2.3 %fusion.3 = (f32[256]{0:T(256)S(1)}, f32[256]{0:T(256)S(1)}, bf16[256,3072]{1,0:T(8,128)(2,1)}) fusion(f32[3072]{0:T(1024)S(1)} %copy-done.5, f32[256,3072]{1,0:T(8,128)S(1)} %get-tuple-element.29, bf16[256,384]{1,0:T(8,128)(2,1)S(1)} %fusion.5, bf16[3072,384]{1,0:T(8,128)(2,1)S(1)} %bitcast.56), kind=kOutput, calls=%fused_computation.9 | convolution fusion | flops 608697856 | bytes 7288832 | tf_op jit(solution)/shard_map/dot_general | solution.py:148
  98.4 2.6 %copy.34 = bf16[256,3072]{0,1:T(8,128)(2,1)} copy(bf16[256,3072]{1,0:T(8,128)(2,1)} %get-tuple-element.53) | data formatting | bytes 3145728 | tf_op jit(solution)/shard_map/convert_element_type | solution.py:150
  101.1 2.8 %pad_maximum_fusion = bf16[16,256,196]{1,2,0:T(8,128)(2,1)} fusion(bf16[16,256,4]{1,2,0:T(4,128)(2,1)S(1)} %broadcast_in_dim.7, bf16[16,256,192]{1,2,0:T(8,128)(2,1)} %bitcast.57), kind=kLoop, calls=%fused_computation.13 | loop fusion | flops 3211264 | bytes 3211264 | tf_op jit(solution)/shard_map/concatenate | solution.py:157
  103.8 6.6 %all-to-all-start.1 = ((bf16[16,256,196]{1,2,0:T(8,128)(2,1)}), bf16[16,256,196]{1,2,0:T(8,128)(2,1)}, u32[]{:S(2)}, u32[]{:S(2)}) async-start(bf16[16,256,196]{1,2,0:T(8,128)(2,1)} %pad_maximum_fusion), calls=%async_computation.1 | async-start | bytes 3276800 | tf_op jit(solution)/shard_map/all_to_all | solution.py:164
  110.7 2.5 %collective-permute-start.3 = (bf16[256,192]{0,1:T(8,128)(2,1)S(1)}, bf16[256,192]{0,1:T(8,128)(2,1)S(1)}, u32[]{:S(2)}, u32[]{:S(2)}) collective-permute-start(bf16[256,192]{0,1:T(8,128)(2,1)S(1)} %get-tuple-element.37), channel_id=1, source_target_pairs={{0,16},{16,0},{1,17},{17,1},{2,18},{18,2},{3,19},{19,3},{4,20},{20... | collective-permute-start | bytes 294920 | tf_op jit(solution)/shard_map/ppermute | solution.py:134
  114.1 4.1 %convolution_convert_fusion = bf16[3072,192]{1,0:T(8,128)(2,1)} fusion(bf16[256,3072]{1,0:T(8,128)(2,1)} %collective-permute-done.2, bf16[256,3072]{1,0:T(8,128)(2,1)} %get-tuple-element.28, bf16[256,192]{0,1:T(8,128)(2,1)S(1)} %collective-permute-done.3, bf16[256,192]{0,1:T(8,128)(2,1)S(1)} %get-tuple-element.36), kind=kOutput, calls=%fused_computation | convolution fusion | flops 611254272 | bytes 4521984 | tf_op jit(solution)/shard_map/dot_general | solution.py:135
  119.8 2.1 %slice.108 = bf16[32,96,10]{2,1,0:T(8,128)(2,1)} slice(bf16[32,96,778]{2,1,0:T(8,128)(2,1)} %bitcast.59), slice={[0:32], [0:96], [768:778]} | slice | bytes 122880 | tf_op jit(solution)/shard_map/slice | solution.py:108
  121.9 2.2 %reshape.166 = bf16[32,960]{1,0:T(8,128)(2,1)S(1)} reshape(bf16[32,96,10]{2,1,0:T(8,128)(2,1)} %slice.108) | data formatting | bytes 122880 | tf_op jit(solution)/shard_map/reshape | solution.py:108
  125.1 1.2 fusion.18
  127.2 8.8 %all-to-all-done.1 = bf16[16,256,196]{1,2,0:T(8,128)(2,1)} async-done(((bf16[16,256,196]{1,2,0:T(8,128)(2,1)}), bf16[16,256,196]{1,2,0:T(8,128)(2,1)}, u32[]{:S(2)}, u32[]{:S(2)}) %all-to-all-start.1) | async-done | bytes 1605664 | tf_op jit(solution)/shard_map/all_to_all | solution.py:164
  136.0 1.7 convert_element_type.114
  137.7 1.7 copy-done
  140.2 1.1 copy.36
  142.5 3.3 %collective-permute-start.1 = (bf16[3,64,192]{2,1,0:T(8,128)(2,1)S(1)}, bf16[3,64,192]{2,1,0:T(8,128)(2,1)S(1)}, u32[]{:S(2)}, u32[]{:S(2)}) collective-permute-start(bf16[3,64,192]{2,1,0:T(8,128)(2,1)S(1)} %bitcast.70), channel_id=1, source_target_pairs={{16,0},{32,16},{48,32},{64,48},{80,64},{96,80},{112,96},{128,112},... | collective-permute-start | bytes 221192 | tf_op jit(solution)/shard_map/ppermute | solution.py:179
  145.8 2.9 %collective-permute-start = (bf16[3,64,192]{2,1,0:T(8,128)(2,1)S(1)}, bf16[3,64,192]{2,1,0:T(8,128)(2,1)S(1)}, u32[]{:S(2)}, u32[]{:S(2)}) collective-permute-start(bf16[3,64,192]{2,1,0:T(8,128)(2,1)S(1)} %bitcast.69), channel_id=1, source_target_pairs={{0,16},{16,32},{32,48},{48,64},{64,80},{80,96},{96,112},{112,128},... | collective-permute-start | bytes 221192 | tf_op jit(solution)/shard_map/ppermute | solution.py:178
  148.8 1.4 collective-permute-done.1
  151.1 7.0 %shard_map.137 = (bf16[4,64,192]{2,1,0:T(8,128)(2,1)}, f32[49,192]{1,0:T(8,128)}) custom-call(bf16[10,70,192]{2,1,0:T(8,128)(2,1)} %fusion.17.tall_ref, bf16[4,64,192]{2,1,0:T(8,128)(2,1)} %bitcast.65, bf16[4,64,192]{2,1,0:T(8,128)(2,1)} %bitcast.64, f32[49,192]{1,0:T(8,128)} %copy.41.kernel_ref), custom_call_target="tpu_custom_call" | custom-call | tf_op jit(solution)/shard_map/pallas_call | solution.py:59
  160.0 8.6 %all-to-all-start.2 = ((f32[32,1,678]{2,1,0:T(1,128)}), f32[32,1,678]{2,1,0:T(1,128)S(1)}, u32[]{:S(2)}, u32[]{:S(2)}) async-start(f32[32,1,678]{2,1,0:T(1,128)} %all_to_all.14), calls=%async_computation.2 | async-start | bytes 196608 | tf_op jit(solution)/shard_map/all_to_all | solution.py:194
  168.7 1.7 copy.47
  170.3 14.8 %all-to-all-done.2 = f32[32,1,678]{2,1,0:T(1,128)S(1)} async-done(((f32[32,1,678]{2,1,0:T(1,128)}), f32[32,1,678]{2,1,0:T(1,128)S(1)}, u32[]{:S(2)}, u32[]{:S(2)}) %all-to-all-start.2) | async-done | bytes 86816 | tf_op jit(solution)/shard_map/all_to_all | solution.py:194
  186.1 4.7 %collective-permute-start.4 = (bf16[96,192]{1,0:T(8,128)(2,1)S(1)}, bf16[96,192]{1,0:T(8,128)(2,1)S(1)}, u32[]{:S(2)}, u32[]{:S(2)}) collective-permute-start(bf16[96,192]{1,0:T(8,128)(2,1)S(1)} %get-tuple-element.41), channel_id=1, source_target_pairs={{0,16},{16,0},{1,17},{17,1},{2,18},{18,2},{3,19},{19,3},{4,20},{20... | collective-permute-start | bytes 110600 | tf_op jit(solution)/shard_map/ppermute | solution.py:141
  (70 shorter events, 16.1 us)
Async XLA Ops:
  7.2 84.8 %all-gather.3.cloned.1.call-start = ((), (), s32[]{:S(2)}) async-start(), calls=%async_computation.5 | async-start | bytes 5677056 | tf_op jit(solution)/shard_map/all_gather | solution.py:28
  61.3 4.6 %copy-start.5 = (f32[3072]{0:T(1024)S(1)}, f32[3072]{0:T(1024)}, u32[]{:S(2)}) copy-start(f32[3072]{0:T(1024)} %param.15) | copy-start | bytes 36868
  61.3 4.6 %copy-start.6 = (f32[3072]{0:T(1024)S(1)}, f32[3072]{0:T(1024)}, u32[]{:S(2)}) copy-start(f32[3072]{0:T(1024)} %param.16) | copy-start | bytes 36868
  65.0 1.9 copy-start.1
  68.9 44.2 %collective-permute-start.2 = (bf16[256,3072]{1,0:T(8,128)(2,1)}, bf16[256,3072]{1,0:T(8,128)(2,1)}, u32[]{:S(2)}, u32[]{:S(2)}) collective-permute-start(bf16[256,3072]{1,0:T(8,128)(2,1)} %get-tuple-element.28), channel_id=1, source_target_pairs={{0,16},{16,0},{1,17},{17,1},{2,18},{18,2},{3,19},{19,3},{4,20},{20... | collective-permute-start | bytes 4718600 | tf_op jit(solution)/shard_map/ppermute | solution.py:130
  92.0 3.0 %copy-start.2 = (bf16[16,256,192]{1,2,0:T(8,128)(2,1)S(1)}, bf16[16,256,192]{1,2,0:T(8,128)(2,1)}, u32[]{:S(2)}) copy-start(bf16[16,256,192]{1,2,0:T(8,128)(2,1)} %get-tuple-element.35) | copy-start | bytes 4718596
  92.0 3.0 %copy-start.7 = (bf16[256,384]{1,0:T(8,128)(2,1)S(1)}, bf16[256,384]{1,0:T(8,128)(2,1)}, u32[]{:S(2)}) copy-start(bf16[256,384]{1,0:T(8,128)(2,1)} %param.12) | copy-start | bytes 589828
  103.8 32.2 %all-to-all-start.1 = ((bf16[16,256,196]{1,2,0:T(8,128)(2,1)}), bf16[16,256,196]{1,2,0:T(8,128)(2,1)}, u32[]{:S(2)}, u32[]{:S(2)}) async-start(bf16[16,256,196]{1,2,0:T(8,128)(2,1)} %pad_maximum_fusion), calls=%async_computation.1 | async-start | bytes 3276800 | tf_op jit(solution)/shard_map/all_to_all | solution.py:164
  110.4 74.8 %reduce-scatter.2.cloned.1.call-start = ((), (), s32[]{:S(2)}) async-start(), calls=%async_computation.4 | async-start | bytes 1671168 | tf_op jit(solution)/shard_map/reduce_scatter | solution.py:138
  110.7 3.4 %collective-permute-start.3 = (bf16[256,192]{0,1:T(8,128)(2,1)S(1)}, bf16[256,192]{0,1:T(8,128)(2,1)S(1)}, u32[]{:S(2)}, u32[]{:S(2)}) collective-permute-start(bf16[256,192]{0,1:T(8,128)(2,1)S(1)} %get-tuple-element.37), channel_id=1, source_target_pairs={{0,16},{16,0},{1,17},{17,1},{2,18},{18,2},{3,19},{19,3},{4,20},{20... | collective-permute-start | bytes 294920 | tf_op jit(solution)/shard_map/ppermute | solution.py:134
  114.1 4.1 %copy-start.3 = (bf16[256,192]{0,1:T(8,128)(2,1)S(1)}, bf16[256,192]{0,1:T(8,128)(2,1)}, u32[]{:S(2)}) copy-start(bf16[256,192]{0,1:T(8,128)(2,1)} %param.13) | copy-start | bytes 294916
  114.1 5.0 %copy-start.4 = (bf16[256,192]{0,1:T(8,128)(2,1)S(1)}, bf16[256,192]{0,1:T(8,128)(2,1)}, u32[]{:S(2)}) copy-start(bf16[256,192]{0,1:T(8,128)(2,1)} %param.10) | copy-start | bytes 294916
  137.7 1.7 copy-start
  142.5 7.7 %collective-permute-start.1 = (bf16[3,64,192]{2,1,0:T(8,128)(2,1)S(1)}, bf16[3,64,192]{2,1,0:T(8,128)(2,1)S(1)}, u32[]{:S(2)}, u32[]{:S(2)}) collective-permute-start(bf16[3,64,192]{2,1,0:T(8,128)(2,1)S(1)} %bitcast.70), channel_id=1, source_target_pairs={{16,0},{32,16},{48,32},{64,48},{80,64},{96,80},{112,96},{128,112},... | collective-permute-start | bytes 221192 | tf_op jit(solution)/shard_map/ppermute | solution.py:179
  145.8 4.4 %collective-permute-start = (bf16[3,64,192]{2,1,0:T(8,128)(2,1)S(1)}, bf16[3,64,192]{2,1,0:T(8,128)(2,1)S(1)}, u32[]{:S(2)}, u32[]{:S(2)}) collective-permute-start(bf16[3,64,192]{2,1,0:T(8,128)(2,1)S(1)} %bitcast.69), channel_id=1, source_target_pairs={{0,16},{16,32},{32,48},{48,64},{64,80},{80,96},{96,112},{112,128},... | collective-permute-start | bytes 221192 | tf_op jit(solution)/shard_map/ppermute | solution.py:178
  160.0 25.1 %all-to-all-start.2 = ((f32[32,1,678]{2,1,0:T(1,128)}), f32[32,1,678]{2,1,0:T(1,128)S(1)}, u32[]{:S(2)}, u32[]{:S(2)}) async-start(f32[32,1,678]{2,1,0:T(1,128)} %all_to_all.14), calls=%async_computation.2 | async-start | bytes 196608 | tf_op jit(solution)/shard_map/all_to_all | solution.py:194
  186.1 6.2 %collective-permute-start.4 = (bf16[96,192]{1,0:T(8,128)(2,1)S(1)}, bf16[96,192]{1,0:T(8,128)(2,1)S(1)}, u32[]{:S(2)}, u32[]{:S(2)}) collective-permute-start(bf16[96,192]{1,0:T(8,128)(2,1)S(1)} %get-tuple-element.41), channel_id=1, source_target_pairs={{0,16},{16,0},{1,17},{17,1},{2,18},{18,2},{3,19},{19,3},{4,20},{20... | collective-permute-start | bytes 110600 | tf_op jit(solution)/shard_map/ppermute | solution.py:141
Sparse Core Ops, SparseCore 0:
  10.1 81.8 all-gather.2
  118.3 59.8 reduce-scatter.1

commit v6 on v5

--- a/solution.py
+++ b/solution.py
@@ -41,29 +41,28 @@
     pad_ref[...] = tall_ref[...].astype(jnp.float32)
     inputs = inputs_ref[...].astype(jnp.float32)
     moved = jnp.zeros((rows, span, channels), jnp.float32)
-    for down in range(KS):
-        for across in range(KS):
+    for across in range(KS):
+        slab = pad_ref[:, 2 * HALO - across : 2 * HALO - across + span, :]
+        for down in range(KS):
             tap = down * KS + across
-            window = pad_ref[
-                2 * HALO - down : 2 * HALO - down + rows,
-                2 * HALO - across : 2 * HALO - across + span,
-                :,
-            ]
+            window = slab[2 * HALO - down : 2 * HALO - down + rows]
             moved = moved + kernel_ref[tap : tap + 1, :][None] * window
-            dk_ref[tap : tap + 1, :] = jnp.sum(window * inputs, axis=(0, 1))[None]
+            part = jnp.sum(window * inputs, axis=0).reshape(span // 8, 8, channels)
+            dk_ref[tap] = jnp.sum(part, axis=0)
     din_ref[...] = (moved + cot_ref[...].astype(jnp.float32)).astype(din_ref.dtype)
 
 
 def conv_call(padded, inputs, cot, kernel_full):
     rows, span, channels = inputs.shape
-    return pl.pallas_call(
+    din, dk = pl.pallas_call(
         conv_body,
         out_shape=(
             jax.ShapeDtypeStruct((rows, span, channels), jnp.bfloat16),
-            jax.ShapeDtypeStruct((KS * KS, channels), jnp.float32),
+            jax.ShapeDtypeStruct((KS * KS, 8, channels), jnp.float32),
         ),
         scratch_shapes=[pltpu.VMEM(padded.shape, jnp.float32)],
     )(padded, inputs, cot, kernel_full)
+    return din, jnp.sum(dk, axis=1)
 
 
 def split_hi_lo(values):
@@ -135,7 +134,8 @@
     chip_sum = lax.dot_general(
         normed_pair, grad_pair, (((0,), (0,)), ((), ())), preferred_element_type=jnp.float32
     )
-    chip_rows = lax.psum_scatter(chip_sum.astype(jnp.bfloat16), "z", scatter_dimension=0, tiled=True)
+    chip_ready = chip_sum.astype(jnp.bfloat16)
+    chip_rows = lax.psum_scatter(chip_ready, "z", scatter_dimension=0, tiled=True)
     chip_rows = chip_rows.reshape(2, width // n_row, hidden // 2)
     own = lax.dynamic_index_in_dim(chip_rows, core, axis=0, keepdims=False)
     other = lax.ppermute(
@@ -161,6 +161,7 @@
         ],
         axis=2,
     )
+    chip_ready, outgoing = lax.optimization_barrier((chip_ready, outgoing))
     incoming = lax.all_to_all(outgoing, "col", 0, 0, tiled=True).astype(jnp.float32)
     grad_norm = jnp.sum(incoming[:, :, :channels], axis=0)
     totals = jnp.sum(incoming[:, :, channels:], axis=0)

time: 203 us -> 211 us (1.039)
  waiting for transfers between devices: 44.7 us -> 55.5 us
  starting transfers between devices: 33 us -> 29.4 us
    all_gather x1, waiting for transfers between devices: 18.7 us -> 26.1 us  [gather_blocks(): return lax.all_gather(x, axis_name, axis=0, tiled=False)]
    all_to_all x1, waiting for transfers between devices: 8.83 us -> 14 us  [body(): lax.all_to_all(outgoing, 'col', 0, 0, tiled=True).astype(jnp.float32)]
    unnamed x21 -> x22, local copies, waits for them, and re-layouts: 6.7 us -> 8.99 us
    ppermute x1, starting transfers between devices: 4.4 us -> 2.16 us  [body(): lax.ppermute(normed_full, 'core', SWAP)]
  transfers between devices with their start and end apart: 9 -> 9, of which waited for: 5 -> 5; matrix products, arithmetic and copies ran while one was open for 23% -> 18% of each run, Pallas kernels for 4% -> 3%
where the time goes in v6:
time: 211 us; the launch traced here: 210 us
  waiting for transfers between devices  55.5 us (26%)
  blocking collectives  46.5 us (22%)
  starting transfers between devices  29.4 us (14%)
  local copies, waits for them, and re-layouts  29 us (14%)
  other arithmetic  20.5 us (10%)
  between operations  14.3 us (7%)
  matrix products  7.75 us (4%)
  Pallas kernels  6.61 us (3%)
    all_to_all x1, blocking collectives, gather_blocks(): return lax.all_to_all(wide, axis_name, 0, 0, tiled=True)  46.5 us
    all_gather x1, waiting for transfers between devices, gather_blocks(): return lax.all_gather(x, axis_name, axis=0, tiled=False)  26.1 us
    all_to_all x1, waiting for transfers between devices, body(): lax.all_to_all(outgoing, 'col', 0, 0, tiled=True).astype(jnp.float32)  14 us
    all_to_all x1, waiting for transfers between devices, body(): lax.all_to_all(jnp.concatenate([kernel_part, norm_part], axis=1), ROW, 0,...  13.7 us
    all_to_all x1, starting transfers between devices, body(): lax.all_to_all(jnp.concatenate([kernel_part, norm_part], axis=1), ROW, 0,...  9.05 us
    unnamed x22, local copies, waits for them, and re-layouts  8.99 us
    all_to_all x1, starting transfers between devices, body(): lax.all_to_all(outgoing, 'col', 0, 0, tiled=True).astype(jnp.float32)  6.73 us
    pallas_call x1, Pallas kernels, conv_call(): pl.pallas_call(conv_body, out_shape=(jax.ShapeDtypeStruct((rows, span, ch...  6.61 us
  transfers between devices with their start and end apart: 9, of which 5 were waited for; matrix products, arithmetic and copies ran while one was open for 18% of the time, Pallas kernels for 3%

profile of v6, /device:TPU:1, one launch (start us, length us, event | category | flops | bytes accessed | tf_op | source)
XLA Modules:
  0.0 209.7 jit_solution(12473305665830783825)
XLA Ops:
  8.4 1.6 pad_maximum_fusion.2
  12.2 46.5 %all_to_all.19 = bf16[16,256,384]{1,2,0:T(8,128)(2,1)S(1)} all-to-all(bf16[16,256,384]{1,2,0:T(8,128)(2,1)S(1)} %broadcast_in_dim.6), channel_id=1, replica_groups=mesh['z'=16,'core'=2,'col'=16] {'col'}, dimensions={0} | all-to-all | bytes 6291456 | tf_op jit(solution)/shard_map/all_to_all | solution.py:27
  58.7 2.7 %slice_convert_fusion = (f32[16,256,192]{1,2,0:T(8,128)}, bf16[16,256,192]{1,2,0:T(8,128)(2,1)}) fusion(bf16[16,256,384]{1,2,0:T(8,128)(2,1)S(1)} %all_to_all.19), kind=kLoop, calls=%fused_computation.14 | loop fusion | flops 786432 | bytes 7864320 | tf_op jit(solution)/shard_map/convert_element_type | solution.py:116
  61.4 3.6 %copy.36 = f32[256,3072]{1,0:T(8,128)} copy(f32[256,3072]{0,1:T(8,128)} %bitcast.56) | data formatting | bytes 6291456 | tf_op jit(solution)/shard_map/convert_element_type | solution.py:116
  65.9 26.1 %all-gather.3.cloned.1.call-done = bf16[3072,778]{1,0:T(8,128)(2,1)} async-done(((bf16[96,778]{1,0:T(8,128)(2,1)}), bf16[3072,778]{1,0:T(8,128)(2,1)}) %all-gather.3.cloned.1.call-update) | async-done | bytes 4780048 | tf_op jit(solution)/shard_map/all_gather | solution.py:28
  92.0 3.0 %fusion.31 = (bf16[32,96,384]{2,1,0:T(8,128)(2,1)S(1)}, bf16[32,96,384]{2,1,0:T(8,128)(2,1)S(1)}) fusion(bf16[32,96,778]{2,1,0:T(8,128)(2,1)} %bitcast.59), kind=kLoop, calls=%fused_computation.78 | loop fusion | bytes 9437184 | tf_op jit(solution)/shard_map/slice | solution.py:114
  95.0 1.1 fusion.5
  96.9 3.0 %fusion.3 = (f32[256]{0:T(256)}, f32[256]{0:T(256)}, f32[256,3072]{1,0:T(8,128)S(1)}, bf16[256,3072]{1,0:T(8,128)(2,1)}) fusion(f32[3072]{0:T(1024)S(1)} %copy-done.5, f32[256]{0:T(256)S(1)} %add_rsqrt_fusion, f32[256,3072]{1,0:T(8,128)S(1)} %copy-done.1, f32[256]{0:T(256)S(1)} %broadcast_multiply_fusion, bf16[256,384]{1,0:T(8,128)(2,1)S(1)} %fusion.5, ...), kind=kOutput, calls=%fused_computation.7 | convolution fusion | flops 610270720 | bytes 10436608 | tf_op jit(solution)/shard_map/dot_general | solution.py:148
  99.9 1.6 add_convert_fusion
  101.5 2.2 %collective-permute-start = (bf16[256,3072]{1,0:T(8,128)(2,1)}, bf16[256,3072]{1,0:T(8,128)(2,1)}, u32[]{:S(2)}, u32[]{:S(2)}) collective-permute-start(bf16[256,3072]{1,0:T(8,128)(2,1)} %add_convert_fusion), channel_id=1, source_target_pairs={{0,16},{16,0},{1,17},{17,1},{2,18},{18,2},{3,19},{19,3},{4,20},{20... | collective-permute-start | bytes 4718600 | tf_op jit(solution)/shard_map/ppermute | solution.py:129
  103.8 2.2 %collective-permute-start.1 = (bf16[256,192]{0,1:T(8,128)(2,1)S(1)}, bf16[256,192]{0,1:T(8,128)(2,1)S(1)}, u32[]{:S(2)}, u32[]{:S(2)}) collective-permute-start(bf16[256,192]{0,1:T(8,128)(2,1)S(1)} %get-tuple-element.38), channel_id=1, source_target_pairs={{0,16},{16,0},{1,17},{17,1},{2,18},{18,2},{3,19},{19,3},{4,20},{20... | collective-permute-start | bytes 294920 | tf_op jit(solution)/shard_map/ppermute | solution.py:133
  106.0 2.6 %copy.39 = bf16[256,3072]{0,1:T(8,128)(2,1)} copy(bf16[256,3072]{1,0:T(8,128)(2,1)} %get-tuple-element.54) | data formatting | bytes 3145728 | tf_op jit(solution)/shard_map/convert_element_type | solution.py:150
  109.3 2.7 %pad_maximum_fusion = bf16[16,256,196]{1,2,0:T(8,128)(2,1)} fusion(bf16[16,256,4]{1,2,0:T(4,128)(2,1)S(1)} %broadcast_in_dim.7, bf16[16,256,192]{1,2,0:T(8,128)(2,1)} %bitcast.58), kind=kLoop, calls=%fused_computation.13 | loop fusion | flops 3211264 | bytes 3211264 | tf_op jit(solution)/shard_map/concatenate | solution.py:157
  112.0 3.7 %convolution_convert_fusion.1 = bf16[3072,192]{0,1:T(8,128)(2,1)} fusion(bf16[256,3072]{1,0:T(8,128)(2,1)} %collective-permute-done, bf16[256,3072]{1,0:T(8,128)(2,1)} %add_convert_fusion, bf16[256,192]{0,1:T(8,128)(2,1)S(1)} %collective-permute-done.1, bf16[256,192]{0,1:T(8,128)(2,1)S(1)} %get-tuple-element.37), kind=kOutput, calls=%fused_computation.1 | convolution fusion | flops 611254272 | bytes 4521984 | tf_op jit(solution)/shard_map/dot_general | solution.py:134
  115.7 6.7 %all-to-all-start.1 = ((bf16[16,256,196]{1,2,0:T(8,128)(2,1)}), bf16[16,256,196]{1,2,0:T(8,128)(2,1)}, u32[]{:S(2)}, u32[]{:S(2)}) async-start(bf16[16,256,196]{1,2,0:T(8,128)(2,1)} %pad_maximum_fusion), calls=%async_computation.1 | async-start | bytes 3276800 | tf_op jit(solution)/shard_map/all_to_all | solution.py:165
  122.5 2.5 %copy.54 = bf16[3072,192]{1,0:T(8,128)(2,1)} copy(bf16[3072,192]{0,1:T(8,128)(2,1)} %convolution_convert_fusion.1) | data formatting | bytes 2359296
  126.7 2.1 slice.108
  128.7 2.2 %reshape.168 = bf16[32,960]{1,0:T(8,128)(2,1)S(1)} reshape(bf16[32,96,10]{2,1,0:T(8,128)(2,1)} %slice.108) | data formatting | bytes 122880 | tf_op jit(solution)/shard_map/reshape | solution.py:107
  132.0 1.2 fusion.18
  134.0 14.0 %all-to-all-done.1 = bf16[16,256,196]{1,2,0:T(8,128)(2,1)} async-done(((bf16[16,256,196]{1,2,0:T(8,128)(2,1)}), bf16[16,256,196]{1,2,0:T(8,128)(2,1)}, u32[]{:S(2)}, u32[]{:S(2)}) %all-to-all-start.1) | async-done | bytes 1605664 | tf_op jit(solution)/shard_map/all_to_all | solution.py:165
  148.0 1.7 convert_element_type.116
  149.7 1.7 copy-done
  152.2 1.1 copy.40
  154.5 3.3 %collective-permute-start.3 = (bf16[3,64,192]{2,1,0:T(8,128)(2,1)S(1)}, bf16[3,64,192]{2,1,0:T(8,128)(2,1)S(1)}, u32[]{:S(2)}, u32[]{:S(2)}) collective-permute-start(bf16[3,64,192]{2,1,0:T(8,128)(2,1)S(1)} %bitcast.71), channel_id=1, source_target_pairs={{16,0},{32,16},{48,32},{64,48},{80,64},{96,80},{112,96},{128,112},... | collective-permute-start | bytes 221192 | tf_op jit(solution)/shard_map/ppermute | solution.py:180
  157.8 2.9 %collective-permute-start.2 = (bf16[3,64,192]{2,1,0:T(8,128)(2,1)S(1)}, bf16[3,64,192]{2,1,0:T(8,128)(2,1)S(1)}, u32[]{:S(2)}, u32[]{:S(2)}) collective-permute-start(bf16[3,64,192]{2,1,0:T(8,128)(2,1)S(1)} %bitcast.70), channel_id=1, source_target_pairs={{0,16},{16,32},{32,48},{48,64},{64,80},{80,96},{96,112},{112,128},... | collective-permute-start | bytes 221192 | tf_op jit(solution)/shard_map/ppermute | solution.py:179
  160.8 1.1 collective-permute-done.3
  163.3 6.6 %shard_map.137 = (bf16[4,64,192]{2,1,0:T(8,128)(2,1)}, f32[49,8,192]{2,1,0:T(8,128)}) custom-call(bf16[10,70,192]{2,1,0:T(8,128)(2,1)} %fusion.17.tall_ref, bf16[4,64,192]{2,1,0:T(8,128)(2,1)} %bitcast.66, bf16[4,64,192]{2,1,0:T(8,128)(2,1)} %bitcast.65, f32[49,192]{1,0:T(8,128)} %copy.45.kernel_ref), custom_call_target="tpu_custom_call" | custom-call | tf_op jit(solution)/shard_map/pallas_call | solution.py:57
  169.9 1.1 reduce_sum.102
  172.2 9.1 %all-to-all-start.2 = ((f32[32,1,678]{2,1,0:T(1,128)}), f32[32,1,678]{2,1,0:T(1,128)S(1)}, u32[]{:S(2)}, u32[]{:S(2)}) async-start(f32[32,1,678]{2,1,0:T(1,128)} %all_to_all.14), calls=%async_computation.2 | async-start | bytes 196608 | tf_op jit(solution)/shard_map/all_to_all | solution.py:195
  181.3 1.7 copy.52
  182.9 13.7 %all-to-all-done.2 = f32[32,1,678]{2,1,0:T(1,128)S(1)} async-done(((f32[32,1,678]{2,1,0:T(1,128)}), f32[32,1,678]{2,1,0:T(1,128)S(1)}, u32[]{:S(2)}, u32[]{:S(2)}) %all-to-all-start.2) | async-done | bytes 86816 | tf_op jit(solution)/shard_map/all_to_all | solution.py:195
  197.6 3.1 %collective-permute-start.4 = (bf16[96,192]{1,0:T(8,128)(2,1)S(1)}, bf16[96,192]{1,0:T(8,128)(2,1)S(1)}, u32[]{:S(2)}, u32[]{:S(2)}) collective-permute-start(bf16[96,192]{1,0:T(8,128)(2,1)S(1)} %get-tuple-element.42), channel_id=1, source_target_pairs={{0,16},{16,0},{1,17},{17,1},{2,18},{18,2},{3,19},{19,3},{4,20},{20... | collective-permute-start | bytes 110600 | tf_op jit(solution)/shard_map/ppermute | solution.py:141
  (72 shorter events, 17.3 us)
Async XLA Ops:
  7.2 84.8 %all-gather.3.cloned.1.call-start = ((), (), s32[]{:S(2)}) async-start(), calls=%async_computation.4 | async-start | bytes 5677056 | tf_op jit(solution)/shard_map/all_gather | solution.py:28
  92.0 3.0 %copy-start.2 = (bf16[16,256,192]{1,2,0:T(8,128)(2,1)S(1)}, bf16[16,256,192]{1,2,0:T(8,128)(2,1)}, u32[]{:S(2)}) copy-start(bf16[16,256,192]{1,2,0:T(8,128)(2,1)} %get-tuple-element.36) | copy-start | bytes 4718596
  92.0 3.0 %copy-start.7 = (bf16[256,384]{1,0:T(8,128)(2,1)S(1)}, bf16[256,384]{1,0:T(8,128)(2,1)}, u32[]{:S(2)}) copy-start(bf16[256,384]{1,0:T(8,128)(2,1)} %param.12) | copy-start | bytes 589828
  95.0 1.9 copy-start.1
  95.0 1.9 copy-start.5
  96.9 3.0 %copy-start.6 = (f32[3072]{0:T(1024)S(1)}, f32[3072]{0:T(1024)}, u32[]{:S(2)}) copy-start(f32[3072]{0:T(1024)} %param.16) | copy-start | bytes 36868
  101.5 10.6 %collective-permute-start = (bf16[256,3072]{1,0:T(8,128)(2,1)}, bf16[256,3072]{1,0:T(8,128)(2,1)}, u32[]{:S(2)}, u32[]{:S(2)}) collective-permute-start(bf16[256,3072]{1,0:T(8,128)(2,1)} %add_convert_fusion), channel_id=1, source_target_pairs={{0,16},{16,0},{1,17},{17,1},{2,18},{18,2},{3,19},{19,3},{4,20},{20... | collective-permute-start | bytes 4718600 | tf_op jit(solution)/shard_map/ppermute | solution.py:129
  103.8 8.2 %collective-permute-start.1 = (bf16[256,192]{0,1:T(8,128)(2,1)S(1)}, bf16[256,192]{0,1:T(8,128)(2,1)S(1)}, u32[]{:S(2)}, u32[]{:S(2)}) collective-permute-start(bf16[256,192]{0,1:T(8,128)(2,1)S(1)} %get-tuple-element.38), channel_id=1, source_target_pairs={{0,16},{16,0},{1,17},{17,1},{2,18},{18,2},{3,19},{19,3},{4,20},{20... | collective-permute-start | bytes 294920 | tf_op jit(solution)/shard_map/ppermute | solution.py:133
  115.7 9.4 %copy-start.3 = (bf16[256,192]{0,1:T(8,128)(2,1)S(1)}, bf16[256,192]{0,1:T(8,128)(2,1)}, u32[]{:S(2)}) copy-start(bf16[256,192]{0,1:T(8,128)(2,1)} %param.13) | copy-start | bytes 294916
  115.7 10.2 %copy-start.4 = (bf16[256,192]{0,1:T(8,128)(2,1)S(1)}, bf16[256,192]{0,1:T(8,128)(2,1)}, u32[]{:S(2)}) copy-start(bf16[256,192]{0,1:T(8,128)(2,1)} %param.10) | copy-start | bytes 294916
  115.7 32.3 %all-to-all-start.1 = ((bf16[16,256,196]{1,2,0:T(8,128)(2,1)}), bf16[16,256,196]{1,2,0:T(8,128)(2,1)}, u32[]{:S(2)}, u32[]{:S(2)}) async-start(bf16[16,256,196]{1,2,0:T(8,128)(2,1)} %pad_maximum_fusion), calls=%async_computation.1 | async-start | bytes 3276800 | tf_op jit(solution)/shard_map/all_to_all | solution.py:165
  122.5 74.2 %reduce-scatter.4.cloned.1.call-start = ((), (), s32[]{:S(2)}) async-start(), calls=%async_computation.5 | async-start | bytes 1671168
  149.7 1.7 copy-start
  154.5 7.4 %collective-permute-start.3 = (bf16[3,64,192]{2,1,0:T(8,128)(2,1)S(1)}, bf16[3,64,192]{2,1,0:T(8,128)(2,1)S(1)}, u32[]{:S(2)}, u32[]{:S(2)}) collective-permute-start(bf16[3,64,192]{2,1,0:T(8,128)(2,1)S(1)} %bitcast.71), channel_id=1, source_target_pairs={{16,0},{32,16},{48,32},{64,48},{80,64},{96,80},{112,96},{128,112},... | collective-permute-start | bytes 221192 | tf_op jit(solution)/shard_map/ppermute | solution.py:180
  157.8 4.7 %collective-permute-start.2 = (bf16[3,64,192]{2,1,0:T(8,128)(2,1)S(1)}, bf16[3,64,192]{2,1,0:T(8,128)(2,1)S(1)}, u32[]{:S(2)}, u32[]{:S(2)}) collective-permute-start(bf16[3,64,192]{2,1,0:T(8,128)(2,1)S(1)} %bitcast.70), channel_id=1, source_target_pairs={{0,16},{16,32},{32,48},{48,64},{64,80},{80,96},{96,112},{112,128},... | collective-permute-start | bytes 221192 | tf_op jit(solution)/shard_map/ppermute | solution.py:179
  172.2 24.4 %all-to-all-start.2 = ((f32[32,1,678]{2,1,0:T(1,128)}), f32[32,1,678]{2,1,0:T(1,128)S(1)}, u32[]{:S(2)}, u32[]{:S(2)}) async-start(f32[32,1,678]{2,1,0:T(1,128)} %all_to_all.14), calls=%async_computation.2 | async-start | bytes 196608 | tf_op jit(solution)/shard_map/all_to_all | solution.py:195
  197.6 4.5 %collective-permute-start.4 = (bf16[96,192]{1,0:T(8,128)(2,1)S(1)}, bf16[96,192]{1,0:T(8,128)(2,1)S(1)}, u32[]{:S(2)}, u32[]{:S(2)}) collective-permute-start(bf16[96,192]{1,0:T(8,128)(2,1)S(1)} %get-tuple-element.42), channel_id=1, source_target_pairs={{0,16},{16,0},{1,17},{17,1},{2,18},{18,2},{3,19},{19,3},{4,20},{20... | collective-permute-start | bytes 110600 | tf_op jit(solution)/shard_map/ppermute | solution.py:141
Sparse Core Ops, SparseCore 0:
  10.1 81.8 all-gather.2
  126.1 58.1 reduce-scatter.3

commit v7 on v6

--- a/solution.py
+++ b/solution.py
@@ -161,7 +161,6 @@
         ],
         axis=2,
     )
-    chip_ready, outgoing = lax.optimization_barrier((chip_ready, outgoing))
     incoming = lax.all_to_all(outgoing, "col", 0, 0, tiled=True).astype(jnp.float32)
     grad_norm = jnp.sum(incoming[:, :, :channels], axis=0)
     totals = jnp.sum(incoming[:, :, channels:], axis=0)
@@ -188,11 +187,15 @@
     )
     d_input = d_input.reshape(tokens, channels)
 
-    kernel_part = kernel_sums.reshape(KS * KS, n_row, few)
-    kernel_part = jnp.transpose(kernel_part, (1, 0, 2)).reshape(n_row, KS * KS * few)
-    norm_part = jnp.broadcast_to(jnp.concatenate([gain_part, bias_part])[None], (n_row, 2 * channels))
+    n_chip = n_row // 2
+    partials = jnp.concatenate([kernel_sums.reshape(-1), gain_part, bias_part])
+    partials = partials + lax.ppermute(partials, "core", SWAP)
+    kernel_chip = partials[: KS * KS * channels].reshape(KS * KS, n_chip, 2, few)
+    kernel_chip = lax.dynamic_index_in_dim(kernel_chip, core, axis=2, keepdims=False)
+    kernel_chip = jnp.transpose(kernel_chip, (1, 0, 2)).reshape(n_chip, KS * KS * few)
+    norm_chip = jnp.broadcast_to(partials[None, KS * KS * channels :], (n_chip, 2 * channels))
     reduced = jnp.sum(
-        lax.all_to_all(jnp.concatenate([kernel_part, norm_part], axis=1), ROW, 0, 0, tiled=True),
+        lax.all_to_all(jnp.concatenate([kernel_chip, norm_chip], axis=1), "z", 0, 0, tiled=True),
         axis=0,
     )
     d_kernel = reduced[: KS * KS * few].reshape(KS * KS, few)

time: 211 us -> 200 us (0.948)
  waiting for transfers between devices: 55.5 us -> 41.9 us
  starting transfers between devices: 29.4 us -> 33.2 us
    all_gather x1, waiting for transfers between devices: 26.1 us -> 18.7 us  [gather_blocks(): return lax.all_gather(x, axis_name, axis=0, tiled=False)]
    all_to_all x1, waiting for transfers between devices: 14 us -> 10.3 us  [body(): lax.all_to_all(outgoing, 'col', 0, 0, tiled=True).astype(jnp.float32)]
    unnamed x22 -> x25, local copies, waits for them, and re-layouts: 8.99 us -> 5.85 us
    all_to_all x1, waiting for transfers between devices: 13.7 us -> 10.8 us  [body(): lax.all_to_all(jnp.concatenate([kernel_chip, norm_chip], axis=1), 'z', 0,...]
    ppermute x1, starting transfers between devices: 2.16 us -> 4.4 us  [body(): lax.ppermute(normed_full, 'core', SWAP)]
  transfers between devices with their start and end apart: 9 -> 10, of which waited for: 5 -> 5; matrix products, arithmetic and copies ran while one was open for 18% -> 25% of each run, Pallas kernels for 3% -> 3%
where the time goes in v7:
time: 200 us
  blocking collectives  46.5 us (23%)
  waiting for transfers between devices  41.9 us (21%)
  starting transfers between devices  33.2 us (17%)
  local copies, waits for them, and re-layouts  29.2 us (15%)
  other arithmetic  20.2 us (10%)
  between operations  14.4 us (7%)
  matrix products  7.51 us (4%)
  Pallas kernels  6.64 us (3%)
    all_to_all x1, blocking collectives, gather_blocks(): return lax.all_to_all(wide, axis_name, 0, 0, tiled=True)  46.5 us
    all_gather x1, waiting for transfers between devices, gather_blocks(): return lax.all_gather(x, axis_name, axis=0, tiled=False)  18.7 us
    all_to_all x1, waiting for transfers between devices, body(): lax.all_to_all(jnp.concatenate([kernel_chip, norm_chip], axis=1), 'z', 0,...  10.8 us
    all_to_all x1, waiting for transfers between devices, body(): lax.all_to_all(outgoing, 'col', 0, 0, tiled=True).astype(jnp.float32)  10.3 us
    all_to_all x1, starting transfers between devices, body(): lax.all_to_all(jnp.concatenate([kernel_chip, norm_chip], axis=1), 'z', 0,...  7.37 us
    pallas_call x1, Pallas kernels, conv_call(): pl.pallas_call(conv_body, out_shape=(jax.ShapeDtypeStruct((rows, span, ch...  6.64 us
    all_to_all x1, starting transfers between devices, body(): lax.all_to_all(outgoing, 'col', 0, 0, tiled=True).astype(jnp.float32)  6.59 us
    unnamed x25, local copies, waits for them, and re-layouts  5.85 us
  transfers between devices with their start and end apart: 10, of which 5 were waited for; matrix products, arithmetic and copies ran while one was open for 25% of the time, Pallas kernels for 3%

profile of v7, /device:TPU:1, one launch (start us, length us, event | category | flops | bytes accessed | tf_op | source)
XLA Modules:
  0.0 199.6 jit_solution(3943950515646733702)
XLA Ops:
  8.4 1.6 pad_maximum_fusion.2
  12.2 46.5 %all_to_all.19 = bf16[16,256,384]{1,2,0:T(8,128)(2,1)S(1)} all-to-all(bf16[16,256,384]{1,2,0:T(8,128)(2,1)S(1)} %broadcast_in_dim.6), channel_id=1, replica_groups=mesh['z'=16,'core'=2,'col'=16] {'col'}, dimensions={0} | all-to-all | bytes 6291456 | tf_op jit(solution)/shard_map/all_to_all | solution.py:27
  58.7 2.6 %slice_convert_fusion = (f32[16,256,192]{1,2,0:T(8,128)}, bf16[16,256,192]{1,2,0:T(8,128)(2,1)}) fusion(bf16[16,256,384]{1,2,0:T(8,128)(2,1)S(1)} %all_to_all.19), kind=kLoop, calls=%fused_computation.14 | loop fusion | flops 786432 | bytes 7864320 | tf_op jit(solution)/shard_map/convert_element_type | solution.py:116
  61.3 3.7 %copy.47 = f32[256,3072]{1,0:T(8,128)} copy(f32[256,3072]{0,1:T(8,128)} %bitcast.56) | data formatting | bytes 6291456 | tf_op jit(solution)/shard_map/convert_element_type | solution.py:116
  66.9 2.0 add_convert_fusion
  68.9 4.4 %collective-permute-start.3 = (bf16[256,3072]{1,0:T(8,128)(2,1)}, bf16[256,3072]{1,0:T(8,128)(2,1)}, u32[]{:S(2)}, u32[]{:S(2)}) collective-permute-start(bf16[256,3072]{1,0:T(8,128)(2,1)} %get-tuple-element.33), channel_id=1, source_target_pairs={{0,16},{16,0},{1,17},{17,1},{2,18},{18,2},{3,19},{19,3},{4,20},{20... | collective-permute-start | bytes 4718600 | tf_op jit(solution)/shard_map/ppermute | solution.py:129
  73.3 18.7 %all-gather.3.cloned.1.call-done = bf16[3072,778]{1,0:T(8,128)(2,1)} async-done(((bf16[96,778]{1,0:T(8,128)(2,1)}), bf16[3072,778]{1,0:T(8,128)(2,1)}) %all-gather.3.cloned.1.call-update) | async-done | bytes 4780048 | tf_op jit(solution)/shard_map/all_gather | solution.py:28
  92.0 3.0 %fusion.31 = (bf16[32,96,384]{2,1,0:T(8,128)(2,1)S(1)}, bf16[32,96,384]{2,1,0:T(8,128)(2,1)S(1)}) fusion(bf16[32,96,778]{2,1,0:T(8,128)(2,1)} %bitcast.59), kind=kLoop, calls=%fused_computation.78 | loop fusion | bytes 9437184 | tf_op jit(solution)/shard_map/slice | solution.py:114
  95.0 1.1 fusion.5
  96.1 2.3 %fusion.3 = (f32[256]{0:T(256)S(1)}, f32[256]{0:T(256)S(1)}, bf16[256,3072]{1,0:T(8,128)(2,1)}) fusion(f32[3072]{0:T(1024)S(1)} %copy-done.6, f32[256,3072]{1,0:T(8,128)S(1)} %get-tuple-element.34, bf16[256,384]{1,0:T(8,128)(2,1)S(1)} %fusion.5, bf16[3072,384]{1,0:T(8,128)(2,1)S(1)} %bitcast.57), kind=kOutput, calls=%fused_computation.9 | convolution fusion | flops 608697856 | bytes 7288832 | tf_op jit(solution)/shard_map/dot_general | solution.py:148
  98.4 2.6 %copy.46 = bf16[256,3072]{0,1:T(8,128)(2,1)} copy(bf16[256,3072]{1,0:T(8,128)(2,1)} %get-tuple-element.58) | data formatting | bytes 3145728 | tf_op jit(solution)/shard_map/convert_element_type | solution.py:150
  101.1 2.8 %pad_maximum_fusion = bf16[16,256,196]{1,2,0:T(8,128)(2,1)} fusion(bf16[16,256,4]{1,2,0:T(4,128)(2,1)S(1)} %broadcast_in_dim.7, bf16[16,256,192]{1,2,0:T(8,128)(2,1)} %bitcast.58), kind=kLoop, calls=%fused_computation.13 | loop fusion | flops 3211264 | bytes 3211264 | tf_op jit(solution)/shard_map/concatenate | solution.py:157
  103.8 6.6 %all-to-all-start.1 = ((bf16[16,256,196]{1,2,0:T(8,128)(2,1)}), bf16[16,256,196]{1,2,0:T(8,128)(2,1)}, u32[]{:S(2)}, u32[]{:S(2)}) async-start(bf16[16,256,196]{1,2,0:T(8,128)(2,1)} %pad_maximum_fusion), calls=%async_computation.1 | async-start | bytes 3276800 | tf_op jit(solution)/shard_map/all_to_all | solution.py:164
  110.7 2.5 %collective-permute-start.4 = (bf16[256,192]{0,1:T(8,128)(2,1)S(1)}, bf16[256,192]{0,1:T(8,128)(2,1)S(1)}, u32[]{:S(2)}, u32[]{:S(2)}) collective-permute-start(bf16[256,192]{0,1:T(8,128)(2,1)S(1)} %get-tuple-element.42), channel_id=1, source_target_pairs={{0,16},{16,0},{1,17},{17,1},{2,18},{18,2},{3,19},{19,3},{4,20},{20... | collective-permute-start | bytes 294920 | tf_op jit(solution)/shard_map/ppermute | solution.py:133
  114.1 4.1 %convolution_convert_fusion = bf16[3072,192]{1,0:T(8,128)(2,1)} fusion(bf16[256,3072]{1,0:T(8,128)(2,1)} %collective-permute-done.3, bf16[256,3072]{1,0:T(8,128)(2,1)} %get-tuple-element.33, bf16[256,192]{0,1:T(8,128)(2,1)S(1)} %collective-permute-done.4, bf16[256,192]{0,1:T(8,128)(2,1)S(1)} %get-tuple-element.41), kind=kOutput, calls=%fused_computation | convolution fusion | flops 611254272 | bytes 4521984 | tf_op jit(solution)/shard_map/dot_general | solution.py:134
  120.4 2.1 %slice.127 = bf16[32,96,10]{2,1,0:T(8,128)(2,1)} slice(bf16[32,96,778]{2,1,0:T(8,128)(2,1)} %bitcast.60), slice={[0:32], [0:96], [768:778]} | slice | bytes 122880 | tf_op jit(solution)/shard_map/slice | solution.py:107
  122.4 2.2 %reshape.175 = bf16[32,960]{1,0:T(8,128)(2,1)S(1)} reshape(bf16[32,96,10]{2,1,0:T(8,128)(2,1)} %slice.127) | data formatting | bytes 122880 | tf_op jit(solution)/shard_map/reshape | solution.py:107
  125.7 10.3 %all-to-all-done.1 = bf16[16,256,196]{1,2,0:T(8,128)(2,1)} async-done(((bf16[16,256,196]{1,2,0:T(8,128)(2,1)}), bf16[16,256,196]{1,2,0:T(8,128)(2,1)}, u32[]{:S(2)}, u32[]{:S(2)}) %all-to-all-start.1) | async-done | bytes 1605664 | tf_op jit(solution)/shard_map/all_to_all | solution.py:164
  136.0 1.7 convert_element_type.114
  137.7 1.7 copy-done
  142.6 3.3 %collective-permute-start.1 = (bf16[3,64,192]{2,1,0:T(8,128)(2,1)S(1)}, bf16[3,64,192]{2,1,0:T(8,128)(2,1)S(1)}, u32[]{:S(2)}, u32[]{:S(2)}) collective-permute-start(bf16[3,64,192]{2,1,0:T(8,128)(2,1)S(1)} %bitcast.72), channel_id=1, source_target_pairs={{16,0},{32,16},{48,32},{64,48},{80,64},{96,80},{112,96},{128,112},... | collective-permute-start | bytes 221192 | tf_op jit(solution)/shard_map/ppermute | solution.py:179
  145.8 2.9 %collective-permute-start = (bf16[3,64,192]{2,1,0:T(8,128)(2,1)S(1)}, bf16[3,64,192]{2,1,0:T(8,128)(2,1)S(1)}, u32[]{:S(2)}, u32[]{:S(2)}) collective-permute-start(bf16[3,64,192]{2,1,0:T(8,128)(2,1)S(1)} %bitcast.71), channel_id=1, source_target_pairs={{0,16},{16,32},{32,48},{48,64},{64,80},{80,96},{96,112},{112,128},... | collective-permute-start | bytes 221192 | tf_op jit(solution)/shard_map/ppermute | solution.py:178
  148.8 1.2 fusion.18
  151.7 6.6 %shard_map.137 = (bf16[4,64,192]{2,1,0:T(8,128)(2,1)}, f32[49,8,192]{2,1,0:T(8,128)}) custom-call(bf16[10,70,192]{2,1,0:T(8,128)(2,1)} %fusion.17.tall_ref, bf16[4,64,192]{2,1,0:T(8,128)(2,1)} %bitcast.67, bf16[4,64,192]{2,1,0:T(8,128)(2,1)} %bitcast.66, f32[49,192]{1,0:T(8,128)} %copy.53.kernel_ref), custom_call_target="tpu_custom_call" | custom-call | tf_op jit(solution)/shard_map/pallas_call | solution.py:57
  158.3 1.1 reduce_sum.102
  159.7 1.9 collective-permute-start.2
  161.6 1.2 collective-permute-done.2
  162.8 1.2 slice.110
  164.5 1.2 copy.61
  166.5 7.4 %all-to-all-start.2 = ((f32[16,1,678]{2,1,0:T(1,128)}), f32[16,1,678]{2,1,0:T(1,128)S(1)}, u32[]{:S(2)}, u32[]{:S(2)}) async-start(f32[16,1,678]{2,1,0:T(1,128)} %all_to_all.14), calls=%async_computation.2 | async-start | bytes 98304 | tf_op jit(solution)/shard_map/all_to_all | solution.py:198
  174.7 10.8 %all-to-all-done.2 = f32[16,1,678]{2,1,0:T(1,128)S(1)} async-done(((f32[16,1,678]{2,1,0:T(1,128)}), f32[16,1,678]{2,1,0:T(1,128)S(1)}, u32[]{:S(2)}, u32[]{:S(2)}) %all-to-all-start.2) | async-done | bytes 43424 | tf_op jit(solution)/shard_map/all_to_all | solution.py:198
  186.3 4.2 %collective-permute-start.5 = (bf16[96,192]{1,0:T(8,128)(2,1)S(1)}, bf16[96,192]{1,0:T(8,128)(2,1)S(1)}, u32[]{:S(2)}, u32[]{:S(2)}) collective-permute-start(bf16[96,192]{1,0:T(8,128)(2,1)S(1)} %get-tuple-element.46), channel_id=1, source_target_pairs={{0,16},{16,0},{1,17},{17,1},{2,18},{18,2},{3,19},{19,3},{4,20},{20... | collective-permute-start | bytes 110600 | tf_op jit(solution)/shard_map/ppermute | solution.py:141
  (81 shorter events, 19.9 us)
Async XLA Ops:
  7.2 84.8 %all-gather.3.cloned.1.call-start = ((), (), s32[]{:S(2)}) async-start(), calls=%async_computation.5 | async-start | bytes 5677056 | tf_op jit(solution)/shard_map/all_gather | solution.py:28
  61.3 4.6 %copy-start.6 = (f32[3072]{0:T(1024)S(1)}, f32[3072]{0:T(1024)}, u32[]{:S(2)}) copy-start(f32[3072]{0:T(1024)} %param.15) | copy-start | bytes 36868
  61.3 4.6 %copy-start.7 = (f32[3072]{0:T(1024)S(1)}, f32[3072]{0:T(1024)}, u32[]{:S(2)}) copy-start(f32[3072]{0:T(1024)} %param.16) | copy-start | bytes 36868
  65.0 1.9 copy-start.1
  68.9 44.2 %collective-permute-start.3 = (bf16[256,3072]{1,0:T(8,128)(2,1)}, bf16[256,3072]{1,0:T(8,128)(2,1)}, u32[]{:S(2)}, u32[]{:S(2)}) collective-permute-start(bf16[256,3072]{1,0:T(8,128)(2,1)} %get-tuple-element.33), channel_id=1, source_target_pairs={{0,16},{16,0},{1,17},{17,1},{2,18},{18,2},{3,19},{19,3},{4,20},{20... | collective-permute-start | bytes 4718600 | tf_op jit(solution)/shard_map/ppermute | solution.py:129
  92.0 3.0 %copy-start.2 = (bf16[16,256,192]{1,2,0:T(8,128)(2,1)S(1)}, bf16[16,256,192]{1,2,0:T(8,128)(2,1)}, u32[]{:S(2)}) copy-start(bf16[16,256,192]{1,2,0:T(8,128)(2,1)} %get-tuple-element.40) | copy-start | bytes 4718596
  92.0 3.0 %copy-start.9 = (bf16[256,384]{1,0:T(8,128)(2,1)S(1)}, bf16[256,384]{1,0:T(8,128)(2,1)}, u32[]{:S(2)}) copy-start(bf16[256,384]{1,0:T(8,128)(2,1)} %param.12) | copy-start | bytes 589828
  103.8 32.2 %all-to-all-start.1 = ((bf16[16,256,196]{1,2,0:T(8,128)(2,1)}), bf16[16,256,196]{1,2,0:T(8,128)(2,1)}, u32[]{:S(2)}, u32[]{:S(2)}) async-start(bf16[16,256,196]{1,2,0:T(8,128)(2,1)} %pad_maximum_fusion), calls=%async_computation.1 | async-start | bytes 3276800 | tf_op jit(solution)/shard_map/all_to_all | solution.py:164
  110.4 75.1 %reduce-scatter.2.cloned.1.call-start = ((), (), s32[]{:S(2)}) async-start(), calls=%async_computation.4 | async-start | bytes 1671168 | tf_op jit(solution)/shard_map/reduce_scatter | solution.py:138
  110.7 3.4 %collective-permute-start.4 = (bf16[256,192]{0,1:T(8,128)(2,1)S(1)}, bf16[256,192]{0,1:T(8,128)(2,1)S(1)}, u32[]{:S(2)}, u32[]{:S(2)}) collective-permute-start(bf16[256,192]{0,1:T(8,128)(2,1)S(1)} %get-tuple-element.42), channel_id=1, source_target_pairs={{0,16},{16,0},{1,17},{17,1},{2,18},{18,2},{3,19},{19,3},{4,20},{20... | collective-permute-start | bytes 294920 | tf_op jit(solution)/shard_map/ppermute | solution.py:133
  114.1 4.1 %copy-start.3 = (bf16[256,192]{0,1:T(8,128)(2,1)S(1)}, bf16[256,192]{0,1:T(8,128)(2,1)}, u32[]{:S(2)}) copy-start(bf16[256,192]{0,1:T(8,128)(2,1)} %param.13) | copy-start | bytes 294916
  114.1 5.5 %copy-start.5 = (bf16[256,192]{0,1:T(8,128)(2,1)S(1)}, bf16[256,192]{0,1:T(8,128)(2,1)}, u32[]{:S(2)}) copy-start(bf16[256,192]{0,1:T(8,128)(2,1)} %param.10) | copy-start | bytes 294916
  137.7 1.7 copy-start
  139.4 2.8 %copy-start.8 = (f32[192]{0:T(256)S(1)}, f32[192]{0:T(256)}, u32[]{:S(2)}) copy-start(f32[192]{0:T(256)} %dynamic_slice.24) | copy-start | bytes 2308
  142.6 8.3 %collective-permute-start.1 = (bf16[3,64,192]{2,1,0:T(8,128)(2,1)S(1)}, bf16[3,64,192]{2,1,0:T(8,128)(2,1)S(1)}, u32[]{:S(2)}, u32[]{:S(2)}) collective-permute-start(bf16[3,64,192]{2,1,0:T(8,128)(2,1)S(1)} %bitcast.72), channel_id=1, source_target_pairs={{16,0},{32,16},{48,32},{64,48},{80,64},{96,80},{112,96},{128,112},... | collective-permute-start | bytes 221192 | tf_op jit(solution)/shard_map/ppermute | solution.py:179
  145.8 5.0 %collective-permute-start = (bf16[3,64,192]{2,1,0:T(8,128)(2,1)S(1)}, bf16[3,64,192]{2,1,0:T(8,128)(2,1)S(1)}, u32[]{:S(2)}, u32[]{:S(2)}) collective-permute-start(bf16[3,64,192]{2,1,0:T(8,128)(2,1)S(1)} %bitcast.71), channel_id=1, source_target_pairs={{0,16},{16,32},{32,48},{48,64},{64,80},{80,96},{96,112},{112,128},... | collective-permute-start | bytes 221192 | tf_op jit(solution)/shard_map/ppermute | solution.py:178
  158.3 15.6 %copy-start.4 = (bf16[4,64,192]{2,1,0:T(8,128)(2,1)S(1)}, bf16[4,64,192]{2,1,0:T(8,128)(2,1)}, u32[]{:S(2)}) copy-start(bf16[4,64,192]{2,1,0:T(8,128)(2,1)} %get-tuple-element.7) | copy-start | bytes 294916
  159.7 3.1 %collective-permute-start.2 = (f32[9792]{0:T(1024)S(1)}, f32[9792]{0:T(1024)S(1)}, u32[]{:S(2)}, u32[]{:S(2)}) collective-permute-start(f32[9792]{0:T(1024)S(1)} %concatenate.34), channel_id=1, source_target_pairs={{0,16},{16,0},{1,17},{17,1},{2,18},{18,2},{3,19},{19,3},{4,20},{20... | collective-permute-start | bytes 117512 | tf_op jit(solution)/shard_map/ppermute | solution.py:192
  166.5 18.9 %all-to-all-start.2 = ((f32[16,1,678]{2,1,0:T(1,128)}), f32[16,1,678]{2,1,0:T(1,128)S(1)}, u32[]{:S(2)}, u32[]{:S(2)}) async-start(f32[16,1,678]{2,1,0:T(1,128)} %all_to_all.14), calls=%async_computation.2 | async-start | bytes 98304 | tf_op jit(solution)/shard_map/all_to_all | solution.py:198
  186.3 5.6 %collective-permute-start.5 = (bf16[96,192]{1,0:T(8,128)(2,1)S(1)}, bf16[96,192]{1,0:T(8,128)(2,1)S(1)}, u32[]{:S(2)}, u32[]{:S(2)}) collective-permute-start(bf16[96,192]{1,0:T(8,128)(2,1)S(1)} %get-tuple-element.46), channel_id=1, source_target_pairs={{0,16},{16,0},{1,17},{17,1},{2,18},{18,2},{3,19},{19,3},{4,20},{20... | collective-permute-start | bytes 110600 | tf_op jit(solution)/shard_map/ppermute | solution.py:141
Sparse Core Ops, SparseCore 0:
  10.1 81.8 all-gather.2
  118.3 57.9 reduce-scatter.1

commit v8 on v7

--- a/solution.py
+++ b/solution.py
@@ -161,9 +161,9 @@
         ],
         axis=2,
     )
-    incoming = lax.all_to_all(outgoing, "col", 0, 0, tiled=True).astype(jnp.float32)
-    grad_norm = jnp.sum(incoming[:, :, :channels], axis=0)
-    totals = jnp.sum(incoming[:, :, channels:], axis=0)
+    incoming = lax.all_to_all(outgoing, "col", 0, 0, tiled=True)
+    grad_norm = jnp.sum(incoming[:, :, :channels].astype(jnp.float32), axis=0)
+    totals = jnp.sum(incoming[:, :, channels:].astype(jnp.float32), axis=0)
     first = (totals[:, 0] + totals[:, 1])[:, None] / width
     second = (totals[:, 2] + totals[:, 3])[:, None] / width
     dzhat = grad_norm * gain_own

time: 200 us -> 200 us (level)
    unnamed x25 -> x23, local copies, waits for them, and re-layouts: 5.85 us -> 4.13 us
  transfers between devices with their start and end apart: 10 -> 10, of which waited for: 5 -> 6; matrix products, arithmetic and copies ran while one was open for 25% -> 25% of each run, Pallas kernels for 3% -> 3%
where the time goes in v8:
time: 200 us; the launch traced here: 199 us
  blocking collectives  46.5 us (23%)
  waiting for transfers between devices  42.3 us (21%)
  starting transfers between devices  34.6 us (17%)
  local copies, waits for them, and re-layouts  27.5 us (14%)
  other arithmetic  20 us (10%)
  between operations  14.4 us (7%)
  matrix products  7.51 us (4%)
  Pallas kernels  6.61 us (3%)
    all_to_all x1, blocking collectives, gather_blocks(): return lax.all_to_all(wide, axis_name, 0, 0, tiled=True)  46.5 us
    all_gather x1, waiting for transfers between devices, gather_blocks(): return lax.all_gather(x, axis_name, axis=0, tiled=False)  18.7 us
    all_to_all x1, waiting for transfers between devices, body(): lax.all_to_all(jnp.concatenate([kernel_chip, norm_chip], axis=1), 'z', 0,...  10.8 us
    all_to_all x1, waiting for transfers between devices, body(): incoming = lax.all_to_all(outgoing, 'col', 0, 0, tiled=True)  10.3 us
    all_to_all x1, starting transfers between devices, body(): lax.all_to_all(jnp.concatenate([kernel_chip, norm_chip], axis=1), 'z', 0,...  7.19 us
    pallas_call x1, Pallas kernels, conv_call(): pl.pallas_call(conv_body, out_shape=(jax.ShapeDtypeStruct((rows, span, ch...  6.61 us
    all_to_all x1, starting transfers between devices, body(): incoming = lax.all_to_all(outgoing, 'col', 0, 0, tiled=True)  6.59 us
    ppermute x1, starting transfers between devices, body(): lax.ppermute(lax.dynamic_index_in_dim(chip_rows, 1 - core, axis=0, keepdi...  5.85 us
  transfers between devices with their start and end apart: 10, of which 6 were waited for; matrix products, arithmetic and copies ran while one was open for 25% of the time, Pallas kernels for 3%

profile of v8, /device:TPU:1, one launch (start us, length us, event | category | flops | bytes accessed | tf_op | source)
XLA Modules:
  0.0 199.4 jit_solution(4870099844567667443)
XLA Ops:
  8.4 1.6 pad_maximum_fusion.2
  12.2 46.5 %all_to_all.19 = bf16[16,256,384]{1,2,0:T(8,128)(2,1)S(1)} all-to-all(bf16[16,256,384]{1,2,0:T(8,128)(2,1)S(1)} %broadcast_in_dim.6), channel_id=1, replica_groups=mesh['z'=16,'core'=2,'col'=16] {'col'}, dimensions={0} | all-to-all | bytes 6291456 | tf_op jit(solution)/shard_map/all_to_all | solution.py:27
  58.7 2.6 %slice_convert_fusion = (f32[16,256,192]{1,2,0:T(8,128)}, bf16[16,256,192]{1,2,0:T(8,128)(2,1)}) fusion(bf16[16,256,384]{1,2,0:T(8,128)(2,1)S(1)} %all_to_all.19), kind=kLoop, calls=%fused_computation.14 | loop fusion | flops 786432 | bytes 7864320 | tf_op jit(solution)/shard_map/convert_element_type | solution.py:116
  61.3 3.7 %copy.47 = f32[256,3072]{1,0:T(8,128)} copy(f32[256,3072]{0,1:T(8,128)} %bitcast.56) | data formatting | bytes 6291456 | tf_op jit(solution)/shard_map/convert_element_type | solution.py:116
  67.0 2.0 add_convert_fusion
  68.9 4.4 %collective-permute-start.3 = (bf16[256,3072]{1,0:T(8,128)(2,1)}, bf16[256,3072]{1,0:T(8,128)(2,1)}, u32[]{:S(2)}, u32[]{:S(2)}) collective-permute-start(bf16[256,3072]{1,0:T(8,128)(2,1)} %get-tuple-element.33), channel_id=1, source_target_pairs={{0,16},{16,0},{1,17},{17,1},{2,18},{18,2},{3,19},{19,3},{4,20},{20... | collective-permute-start | bytes 4718600 | tf_op jit(solution)/shard_map/ppermute | solution.py:129
  73.3 18.7 %all-gather.3.cloned.1.call-done = bf16[3072,778]{1,0:T(8,128)(2,1)} async-done(((bf16[96,778]{1,0:T(8,128)(2,1)}), bf16[3072,778]{1,0:T(8,128)(2,1)}) %all-gather.3.cloned.1.call-update) | async-done | bytes 4780048 | tf_op jit(solution)/shard_map/all_gather | solution.py:28
  92.0 3.0 %fusion.31 = (bf16[32,96,384]{2,1,0:T(8,128)(2,1)S(1)}, bf16[32,96,384]{2,1,0:T(8,128)(2,1)S(1)}) fusion(bf16[32,96,778]{2,1,0:T(8,128)(2,1)} %bitcast.59), kind=kLoop, calls=%fused_computation.78 | loop fusion | bytes 9437184 | tf_op jit(solution)/shard_map/slice | solution.py:114
  95.0 1.1 fusion.5
  96.1 2.3 %fusion.3 = (f32[256]{0:T(256)S(1)}, f32[256]{0:T(256)S(1)}, bf16[256,3072]{1,0:T(8,128)(2,1)}) fusion(f32[3072]{0:T(1024)S(1)} %copy-done.5, f32[256,3072]{1,0:T(8,128)S(1)} %get-tuple-element.34, bf16[256,384]{1,0:T(8,128)(2,1)S(1)} %fusion.5, bf16[3072,384]{1,0:T(8,128)(2,1)S(1)} %bitcast.57), kind=kOutput, calls=%fused_computation.11 | convolution fusion | flops 608697856 | bytes 7288832 | tf_op jit(solution)/shard_map/dot_general | solution.py:148
  98.4 2.6 %copy.46 = bf16[256,3072]{0,1:T(8,128)(2,1)} copy(bf16[256,3072]{1,0:T(8,128)(2,1)} %get-tuple-element.58) | data formatting | bytes 3145728 | tf_op jit(solution)/shard_map/convert_element_type | solution.py:150
  101.0 2.7 %pad_maximum_fusion = bf16[16,256,196]{1,2,0:T(8,128)(2,1)} fusion(bf16[16,256,4]{1,2,0:T(4,128)(2,1)S(1)} %broadcast_in_dim.7, bf16[16,256,192]{1,2,0:T(8,128)(2,1)} %bitcast.58), kind=kLoop, calls=%fused_computation.13 | loop fusion | flops 3211264 | bytes 3211264 | tf_op jit(solution)/shard_map/concatenate | solution.py:157
  103.8 6.6 %all-to-all-start.1 = ((bf16[16,256,196]{1,2,0:T(8,128)(2,1)}), bf16[16,256,196]{1,2,0:T(8,128)(2,1)}, u32[]{:S(2)}, u32[]{:S(2)}) async-start(bf16[16,256,196]{1,2,0:T(8,128)(2,1)} %pad_maximum_fusion), calls=%async_computation.1 | async-start | bytes 3276800 | tf_op jit(solution)/shard_map/all_to_all | solution.py:164
  110.6 2.5 %collective-permute-start.4 = (bf16[256,192]{0,1:T(8,128)(2,1)S(1)}, bf16[256,192]{0,1:T(8,128)(2,1)S(1)}, u32[]{:S(2)}, u32[]{:S(2)}) collective-permute-start(bf16[256,192]{0,1:T(8,128)(2,1)S(1)} %get-tuple-element.42), channel_id=1, source_target_pairs={{0,16},{16,0},{1,17},{17,1},{2,18},{18,2},{3,19},{19,3},{4,20},{20... | collective-permute-start | bytes 294920 | tf_op jit(solution)/shard_map/ppermute | solution.py:133
  114.0 4.1 %convolution_convert_fusion = bf16[3072,192]{1,0:T(8,128)(2,1)} fusion(bf16[256,3072]{1,0:T(8,128)(2,1)} %collective-permute-done.3, bf16[256,3072]{1,0:T(8,128)(2,1)} %get-tuple-element.33, bf16[256,192]{0,1:T(8,128)(2,1)S(1)} %collective-permute-done.4, bf16[256,192]{0,1:T(8,128)(2,1)S(1)} %get-tuple-element.41), kind=kOutput, calls=%fused_computation.2 | convolution fusion | flops 611254272 | bytes 4521984 | tf_op jit(solution)/shard_map/dot_general | solution.py:134
  120.3 2.1 %slice.127 = bf16[32,96,10]{2,1,0:T(8,128)(2,1)} slice(bf16[32,96,778]{2,1,0:T(8,128)(2,1)} %bitcast.60), slice={[0:32], [0:96], [768:778]} | slice | bytes 122880 | tf_op jit(solution)/shard_map/slice | solution.py:107
  122.4 2.2 %reshape.175 = bf16[32,960]{1,0:T(8,128)(2,1)S(1)} reshape(bf16[32,96,10]{2,1,0:T(8,128)(2,1)} %slice.127) | data formatting | bytes 122880 | tf_op jit(solution)/shard_map/reshape | solution.py:107
  125.6 10.3 %all-to-all-done.1 = bf16[16,256,196]{1,2,0:T(8,128)(2,1)} async-done(((bf16[16,256,196]{1,2,0:T(8,128)(2,1)}), bf16[16,256,196]{1,2,0:T(8,128)(2,1)}, u32[]{:S(2)}, u32[]{:S(2)}) %all-to-all-start.1) | async-done | bytes 1605664 | tf_op jit(solution)/shard_map/all_to_all | solution.py:164
  135.9 2.5 %convert_reduce_fusion = (f32[192]{0:T(256)S(1)}, f32[256,192]{0,1:T(8,128)}) fusion(bf16[16,256,196]{1,2,0:T(8,128)(2,1)} %all-to-all-done.1), kind=kLoop, calls=%fused_computation | loop fusion | flops 2309952 | bytes 1770240 | tf_op jit(solution)/shard_map/reduce_sum | solution.py:172
  138.4 1.1 copy.48
  140.6 3.3 %collective-permute-start.1 = (bf16[3,64,192]{2,1,0:T(8,128)(2,1)S(1)}, bf16[3,64,192]{2,1,0:T(8,128)(2,1)S(1)}, u32[]{:S(2)}, u32[]{:S(2)}) collective-permute-start(bf16[3,64,192]{2,1,0:T(8,128)(2,1)S(1)} %bitcast.72), channel_id=1, source_target_pairs={{16,0},{32,16},{48,32},{64,48},{80,64},{96,80},{112,96},{128,112},... | collective-permute-start | bytes 221192 | tf_op jit(solution)/shard_map/ppermute | solution.py:179
  143.9 2.9 %collective-permute-start = (bf16[3,64,192]{2,1,0:T(8,128)(2,1)S(1)}, bf16[3,64,192]{2,1,0:T(8,128)(2,1)S(1)}, u32[]{:S(2)}, u32[]{:S(2)}) collective-permute-start(bf16[3,64,192]{2,1,0:T(8,128)(2,1)S(1)} %bitcast.71), channel_id=1, source_target_pairs={{0,16},{16,32},{32,48},{48,64},{64,80},{80,96},{96,112},{112,128},... | collective-permute-start | bytes 221192 | tf_op jit(solution)/shard_map/ppermute | solution.py:178
  146.8 1.2 fusion.18
  150.1 6.6 %shard_map.137 = (bf16[4,64,192]{2,1,0:T(8,128)(2,1)}, f32[49,8,192]{2,1,0:T(8,128)}) custom-call(bf16[10,70,192]{2,1,0:T(8,128)(2,1)} %fusion.17.tall_ref, bf16[4,64,192]{2,1,0:T(8,128)(2,1)} %bitcast.67, bf16[4,64,192]{2,1,0:T(8,128)(2,1)} %bitcast.66, f32[49,192]{1,0:T(8,128)} %copy.53.kernel_ref), custom_call_target="tpu_custom_call" | custom-call | tf_op jit(solution)/shard_map/pallas_call | solution.py:57
  156.7 1.1 reduce_sum.102
  158.0 1.9 collective-permute-start.2
  159.9 1.2 collective-permute-done.2
  161.2 1.2 slice.110
  162.8 1.2 copy.61
  164.8 7.2 %all-to-all-start.2 = ((f32[16,1,678]{2,1,0:T(1,128)}), f32[16,1,678]{2,1,0:T(1,128)S(1)}, u32[]{:S(2)}, u32[]{:S(2)}) async-start(f32[16,1,678]{2,1,0:T(1,128)} %all_to_all.14), calls=%async_computation.2 | async-start | bytes 98304 | tf_op jit(solution)/shard_map/all_to_all | solution.py:198
  172.8 10.8 %all-to-all-done.2 = f32[16,1,678]{2,1,0:T(1,128)S(1)} async-done(((f32[16,1,678]{2,1,0:T(1,128)}), f32[16,1,678]{2,1,0:T(1,128)S(1)}, u32[]{:S(2)}, u32[]{:S(2)}) %all-to-all-start.2) | async-done | bytes 43424 | tf_op jit(solution)/shard_map/all_to_all | solution.py:198
  184.6 5.9 %collective-permute-start.5 = (bf16[96,192]{1,0:T(8,128)(2,1)S(1)}, bf16[96,192]{1,0:T(8,128)(2,1)S(1)}, u32[]{:S(2)}, u32[]{:S(2)}) collective-permute-start(bf16[96,192]{1,0:T(8,128)(2,1)S(1)} %get-tuple-element.46), channel_id=1, source_target_pairs={{0,16},{16,0},{1,17},{17,1},{2,18},{18,2},{3,19},{19,3},{4,20},{20... | collective-permute-start | bytes 110600 | tf_op jit(solution)/shard_map/ppermute | solution.py:141
  (78 shorter events, 18.3 us)
Async XLA Ops:
  7.2 84.8 %all-gather.3.cloned.1.call-start = ((), (), s32[]{:S(2)}) async-start(), calls=%async_computation.5 | async-start | bytes 5677056 | tf_op jit(solution)/shard_map/all_gather | solution.py:28
  61.3 4.6 %copy-start.5 = (f32[3072]{0:T(1024)S(1)}, f32[3072]{0:T(1024)}, u32[]{:S(2)}) copy-start(f32[3072]{0:T(1024)} %param.15) | copy-start | bytes 36868
  61.3 4.6 %copy-start.6 = (f32[3072]{0:T(1024)S(1)}, f32[3072]{0:T(1024)}, u32[]{:S(2)}) copy-start(f32[3072]{0:T(1024)} %param.16) | copy-start | bytes 36868
  65.0 1.9 copy-start
  68.9 44.1 %collective-permute-start.3 = (bf16[256,3072]{1,0:T(8,128)(2,1)}, bf16[256,3072]{1,0:T(8,128)(2,1)}, u32[]{:S(2)}, u32[]{:S(2)}) collective-permute-start(bf16[256,3072]{1,0:T(8,128)(2,1)} %get-tuple-element.33), channel_id=1, source_target_pairs={{0,16},{16,0},{1,17},{17,1},{2,18},{18,2},{3,19},{19,3},{4,20},{20... | collective-permute-start | bytes 4718600 | tf_op jit(solution)/shard_map/ppermute | solution.py:129
  92.0 3.0 %copy-start.1 = (bf16[16,256,192]{1,2,0:T(8,128)(2,1)S(1)}, bf16[16,256,192]{1,2,0:T(8,128)(2,1)}, u32[]{:S(2)}) copy-start(bf16[16,256,192]{1,2,0:T(8,128)(2,1)} %get-tuple-element.40) | copy-start | bytes 4718596
  92.0 3.0 %copy-start.8 = (bf16[256,384]{1,0:T(8,128)(2,1)S(1)}, bf16[256,384]{1,0:T(8,128)(2,1)}, u32[]{:S(2)}) copy-start(bf16[256,384]{1,0:T(8,128)(2,1)} %param.12) | copy-start | bytes 589828
  103.8 32.2 %all-to-all-start.1 = ((bf16[16,256,196]{1,2,0:T(8,128)(2,1)}), bf16[16,256,196]{1,2,0:T(8,128)(2,1)}, u32[]{:S(2)}, u32[]{:S(2)}) async-start(bf16[16,256,196]{1,2,0:T(8,128)(2,1)} %pad_maximum_fusion), calls=%async_computation.1 | async-start | bytes 3276800 | tf_op jit(solution)/shard_map/all_to_all | solution.py:164
  110.4 73.3 %reduce-scatter.2.cloned.1.call-start = ((), (), s32[]{:S(2)}) async-start(), calls=%async_computation.4 | async-start | bytes 1671168 | tf_op jit(solution)/shard_map/reduce_scatter | solution.py:138
  110.6 3.4 %collective-permute-start.4 = (bf16[256,192]{0,1:T(8,128)(2,1)S(1)}, bf16[256,192]{0,1:T(8,128)(2,1)S(1)}, u32[]{:S(2)}, u32[]{:S(2)}) collective-permute-start(bf16[256,192]{0,1:T(8,128)(2,1)S(1)} %get-tuple-element.42), channel_id=1, source_target_pairs={{0,16},{16,0},{1,17},{17,1},{2,18},{18,2},{3,19},{19,3},{4,20},{20... | collective-permute-start | bytes 294920 | tf_op jit(solution)/shard_map/ppermute | solution.py:133
  114.0 4.2 %copy-start.2 = (bf16[256,192]{0,1:T(8,128)(2,1)S(1)}, bf16[256,192]{0,1:T(8,128)(2,1)}, u32[]{:S(2)}) copy-start(bf16[256,192]{0,1:T(8,128)(2,1)} %param.13) | copy-start | bytes 294916
  114.0 5.6 %copy-start.4 = (bf16[256,192]{0,1:T(8,128)(2,1)S(1)}, bf16[256,192]{0,1:T(8,128)(2,1)}, u32[]{:S(2)}) copy-start(bf16[256,192]{0,1:T(8,128)(2,1)} %param.10) | copy-start | bytes 294916
  119.5 20.8 %copy-start.7 = (f32[192]{0:T(256)S(1)}, f32[192]{0:T(256)}, u32[]{:S(2)}) copy-start(f32[192]{0:T(256)} %dynamic_slice.24) | copy-start | bytes 2308
  140.6 8.3 %collective-permute-start.1 = (bf16[3,64,192]{2,1,0:T(8,128)(2,1)S(1)}, bf16[3,64,192]{2,1,0:T(8,128)(2,1)S(1)}, u32[]{:S(2)}, u32[]{:S(2)}) collective-permute-start(bf16[3,64,192]{2,1,0:T(8,128)(2,1)S(1)} %bitcast.72), channel_id=1, source_target_pairs={{16,0},{32,16},{48,32},{64,48},{80,64},{96,80},{112,96},{128,112},... | collective-permute-start | bytes 221192 | tf_op jit(solution)/shard_map/ppermute | solution.py:179
  143.9 5.3 %collective-permute-start = (bf16[3,64,192]{2,1,0:T(8,128)(2,1)S(1)}, bf16[3,64,192]{2,1,0:T(8,128)(2,1)S(1)}, u32[]{:S(2)}, u32[]{:S(2)}) collective-permute-start(bf16[3,64,192]{2,1,0:T(8,128)(2,1)S(1)} %bitcast.71), channel_id=1, source_target_pairs={{0,16},{16,32},{32,48},{48,64},{64,80},{80,96},{96,112},{112,128},... | collective-permute-start | bytes 221192 | tf_op jit(solution)/shard_map/ppermute | solution.py:178
  156.7 15.4 %copy-start.3 = (bf16[4,64,192]{2,1,0:T(8,128)(2,1)S(1)}, bf16[4,64,192]{2,1,0:T(8,128)(2,1)}, u32[]{:S(2)}) copy-start(bf16[4,64,192]{2,1,0:T(8,128)(2,1)} %get-tuple-element.7) | copy-start | bytes 294916
  158.0 3.1 %collective-permute-start.2 = (f32[9792]{0:T(1024)S(1)}, f32[9792]{0:T(1024)S(1)}, u32[]{:S(2)}, u32[]{:S(2)}) collective-permute-start(f32[9792]{0:T(1024)S(1)} %concatenate.34), channel_id=1, source_target_pairs={{0,16},{16,0},{1,17},{17,1},{2,18},{18,2},{3,19},{19,3},{4,20},{20... | collective-permute-start | bytes 117512 | tf_op jit(solution)/shard_map/ppermute | solution.py:192
  164.8 18.8 %all-to-all-start.2 = ((f32[16,1,678]{2,1,0:T(1,128)}), f32[16,1,678]{2,1,0:T(1,128)S(1)}, u32[]{:S(2)}, u32[]{:S(2)}) async-start(f32[16,1,678]{2,1,0:T(1,128)} %all_to_all.14), calls=%async_computation.2 | async-start | bytes 98304 | tf_op jit(solution)/shard_map/all_to_all | solution.py:198
  184.6 7.3 %collective-permute-start.5 = (bf16[96,192]{1,0:T(8,128)(2,1)S(1)}, bf16[96,192]{1,0:T(8,128)(2,1)S(1)}, u32[]{:S(2)}, u32[]{:S(2)}) collective-permute-start(bf16[96,192]{1,0:T(8,128)(2,1)S(1)} %get-tuple-element.46), channel_id=1, source_target_pairs={{0,16},{16,0},{1,17},{17,1},{2,18},{18,2},{3,19},{19,3},{4,20},{20... | collective-permute-start | bytes 110600 | tf_op jit(solution)/shard_map/ppermute | solution.py:141
Sparse Core Ops, SparseCore 0:
  10.1 81.8 all-gather.2
  118.3 58.2 reduce-scatter.1

commit v9 on v8

--- a/solution.py
+++ b/solution.py
@@ -146,24 +146,22 @@
     )
 
     block_n = lax.dot_general(
-        grad_pre, w_in_full, (((1,), (1,)), ((), ())), preferred_element_type=jnp.float32
+        w_in_full.reshape(n_col, channels, hidden),
+        grad_pre,
+        (((2,), (1,)), ((), ())),
+        preferred_element_type=jnp.float32,
     ).astype(jnp.bfloat16)
-    weighted = block_n.astype(jnp.float32) * norm_gain
-    first_part = jnp.sum(weighted, axis=1)
-    second_part = jnp.sum(weighted * zhat_full, axis=1)
+    zhat_by_owner = jnp.transpose(zhat_full.reshape(tokens, n_col, channels), (1, 2, 0))
+    weighted = block_n.astype(jnp.float32) * norm_gain.reshape(n_col, channels, 1)
+    first_part = jnp.sum(weighted, axis=(0, 1))
+    second_part = jnp.sum(weighted * zhat_by_owner, axis=(0, 1))
     f_hi, f_lo = split_hi_lo(first_part)
     s_hi, s_lo = split_hi_lo(second_part)
-    sums = jnp.stack([f_hi, f_lo, s_hi, s_lo], axis=1)
-    outgoing = jnp.concatenate(
-        [
-            jnp.transpose(block_n.reshape(tokens, n_col, channels), (1, 0, 2)),
-            jnp.broadcast_to(sums[None], (n_col, tokens, 4)),
-        ],
-        axis=2,
-    )
+    sums = jnp.stack([f_hi, f_lo, s_hi, s_lo], axis=0)
+    outgoing = jnp.concatenate([block_n, jnp.broadcast_to(sums[None], (n_col, 4, tokens))], axis=1)
     incoming = lax.all_to_all(outgoing, "col", 0, 0, tiled=True)
-    grad_norm = jnp.sum(incoming[:, :, :channels].astype(jnp.float32), axis=0)
-    totals = jnp.sum(incoming[:, :, channels:].astype(jnp.float32), axis=0)
+    grad_norm = jnp.sum(incoming[:, :channels].astype(jnp.float32), axis=0).T
+    totals = jnp.sum(incoming[:, channels:].astype(jnp.float32), axis=0).T
     first = (totals[:, 0] + totals[:, 1])[:, None] / width
     second = (totals[:, 2] + totals[:, 3])[:, None] / width
     dzhat = grad_norm * gain_own

time: 200 us -> 196 us (0.980)
  blocking collectives: 46.5 us -> 0 us
  waiting for transfers between devices: 42.3 us -> 87.8 us
  starting transfers between devices: 34.6 us -> 47 us
  local copies, waits for them, and re-layouts: 27.5 us -> 18.9 us
  other arithmetic: 20 us -> 13.9 us
    all_to_all x1 -> x0, blocking collectives: 46.5 us -> none  [gather_blocks(): return lax.all_to_all(wide, axis_name, 0, 0, tiled=True)]
    all_to_all x0 -> x1, waiting for transfers between devices: none -> 39.7 us  [gather_blocks(): return lax.all_to_all(wide, axis_name, 0, 0, tiled=True)]
    all_to_all x0 -> x1, starting transfers between devices: none -> 7.72 us  [gather_blocks(): return lax.all_to_all(wide, axis_name, 0, 0, tiled=True)]
    convert_element_type x2 -> x1, local copies, waits for them, and re-layouts: 6.28 us -> 0.1 us  [body(): (rstd * (dzhat - first - zhat_own * second)).astype(jnp.bfloat16)]
    all_to_all x1, waiting for transfers between devices: 10.3 us -> 13.5 us  [body(): incoming = lax.all_to_all(outgoing, 'col', 0, 0, tiled=True)]
    convert_element_type x1 -> x0, other arithmetic: 2.62 us -> none  [body(): values = inputs_full.astype(jnp.float32)]
    ppermute x1, starting transfers between devices: 4.38 us -> 6.57 us  [body(): lax.ppermute(normed_full, 'core', SWAP)]
    reduce_sum x1, other arithmetic: 2.46 us -> 0.36 us  [body(): bias_part = jnp.sum(grad_norm, axis=0)]
  transfers between devices with their start and end apart: 10 -> 11, of which waited for: 6 -> 7; matrix products, arithmetic and copies ran while one was open for 25% -> 17% of each run, Pallas kernels for 3% -> 3%
where the time goes in v9:
time: 196 us; the launch traced here: 195 us
  waiting for transfers between devices  87.8 us (45%)
  starting transfers between devices  47 us (24%)
  local copies, waits for them, and re-layouts  18.9 us (10%)
  between operations  14.4 us (7%)
  other arithmetic  13.9 us (7%)
  Pallas kernels  6.62 us (3%)
  matrix products  6.46 us (3%)
    all_to_all x1, waiting for transfers between devices, gather_blocks(): return lax.all_to_all(wide, axis_name, 0, 0, tiled=True)  39.7 us
    all_gather x1, waiting for transfers between devices, gather_blocks(): return lax.all_gather(x, axis_name, axis=0, tiled=False)  20 us
    all_to_all x1, waiting for transfers between devices, body(): incoming = lax.all_to_all(outgoing, 'col', 0, 0, tiled=True)  13.5 us
    all_to_all x1, waiting for transfers between devices, body(): lax.all_to_all(jnp.concatenate([kernel_chip, norm_chip], axis=1), 'z', 0,...  11.3 us
    ppermute x1, starting transfers between devices, body(): lax.ppermute(lax.dynamic_index_in_dim(chip_rows, 1 - core, axis=0, keepdi...  7.88 us
    all_to_all x1, starting transfers between devices, gather_blocks(): return lax.all_to_all(wide, axis_name, 0, 0, tiled=True)  7.72 us
    all_to_all x1, starting transfers between devices, body(): lax.all_to_all(jnp.concatenate([kernel_chip, norm_chip], axis=1), 'z', 0,...  7.42 us
    pallas_call x1, Pallas kernels, conv_call(): pl.pallas_call(conv_body, out_shape=(jax.ShapeDtypeStruct((rows, span, ch...  6.62 us
  transfers between devices with their start and end apart: 11, of which 7 were waited for; matrix products, arithmetic and copies ran while one was open for 17% of the time, Pallas kernels for 3%

profile of v9, /device:TPU:1, one launch (start us, length us, event | category | flops | bytes accessed | tf_op | source)
XLA Modules:
  0.0 195.0 jit_solution(14801985395276886160)
XLA Ops:
  8.4 1.6 pad_maximum_fusion.2
  10.0 1.0 multiply_convert_fusion
  11.9 2.0 %broadcast_in_dim.6 = bf16[16,256,384]{1,2,0:T(8,128)(2,1)} broadcast(bf16[256,384]{0,1:T(8,128)(2,1)S(1)} %pad_maximum_fusion.1), dimensions={1,2} | broadcast | bytes 3342336 | tf_op jit(solution)/shard_map/broadcast_in_dim | solution.py:26
  13.9 7.7 %all-to-all-start = ((bf16[16,256,384]{1,2,0:T(8,128)(2,1)}), bf16[16,256,384]{1,2,0:T(8,128)(2,1)S(1)}, u32[]{:S(2)}, u32[]{:S(2)}) async-start(bf16[16,256,384]{1,2,0:T(8,128)(2,1)} %broadcast_in_dim.6), calls=%async_computation | async-start | bytes 6291456 | tf_op jit(solution)/shard_map/all_to_all | solution.py:27
  21.7 39.7 %all-to-all-done = bf16[16,256,384]{1,2,0:T(8,128)(2,1)S(1)} async-done(((bf16[16,256,384]{1,2,0:T(8,128)(2,1)}), bf16[16,256,384]{1,2,0:T(8,128)(2,1)S(1)}, u32[]{:S(2)}, u32[]{:S(2)}) %all-to-all-start) | async-done | bytes 3145760 | tf_op jit(solution)/shard_map/all_to_all | solution.py:27
  62.3 3.1 %add_convert_fusion = (bf16[256,3072]{0,1:T(8,128)(2,1)}, f32[256,3072]{0,1:T(8,128)}) fusion(f32[3072]{0:T(1024)S(1)} %copy-done.6, f32[3072]{0:T(1024)S(1)} %copy-done.5, f32[256]{0:T(256)S(1)} %add_rsqrt_fusion, f32[256]{0:T(256)S(1)} %broadcast_multiply_fusion, bf16[16,256,384]{1,2,0:T(8,128)(2,1)S(1)} %all-to-all-done), kind=kLoop, calls=%fused_computation.10 | loop fusion | flops 4718592 | bytes 6318080 | tf_op jit(solution)/shard_map/convert_element_type | solution.py:121
  65.4 6.6 %collective-permute-start.3 = (bf16[256,3072]{0,1:T(8,128)(2,1)}, bf16[256,3072]{0,1:T(8,128)(2,1)}, u32[]{:S(2)}, u32[]{:S(2)}) collective-permute-start(bf16[256,3072]{0,1:T(8,128)(2,1)} %get-tuple-element.37), channel_id=1, source_target_pairs={{0,16},{16,0},{1,17},{17,1},{2,18},{18,2},{3,19},{19,3},{4,20},{20... | collective-permute-start | bytes 4718600 | tf_op jit(solution)/shard_map/ppermute | solution.py:129
  72.0 20.0 %all-gather.3.cloned.1.call-done = bf16[3072,778]{1,0:T(8,128)(2,1)} async-done(((bf16[96,778]{1,0:T(8,128)(2,1)}), bf16[3072,778]{1,0:T(8,128)(2,1)}) %all-gather.3.cloned.1.call-update) | async-done | bytes 4780048 | tf_op jit(solution)/shard_map/all_gather | solution.py:28
  92.0 3.0 %fusion.38 = (bf16[32,96,384]{2,1,0:T(8,128)(2,1)S(1)}, bf16[32,96,384]{2,1,0:T(8,128)(2,1)S(1)}) fusion(bf16[32,96,778]{2,1,0:T(8,128)(2,1)} %bitcast.81), kind=kLoop, calls=%fused_computation.85 | loop fusion | bytes 9437184 | tf_op jit(solution)/shard_map/slice | solution.py:113
  95.0 1.1 fusion.6
  96.9 1.3 fusion.5
  98.3 1.3 pad_maximum_fusion
  99.6 6.6 %all-to-all-start.1 = ((bf16[16,196,256]{2,1,0:T(8,128)(2,1)}), bf16[16,196,256]{2,1,0:T(8,128)(2,1)S(1)}, u32[]{:S(2)}, u32[]{:S(2)}) async-start(bf16[16,196,256]{2,1,0:T(8,128)(2,1)} %pad_maximum_fusion), calls=%async_computation.1 | async-start | bytes 3276800 | tf_op jit(solution)/shard_map/all_to_all | solution.py:162
  106.5 2.5 %collective-permute-start.4 = (bf16[256,192]{0,1:T(8,128)(2,1)S(1)}, bf16[256,192]{0,1:T(8,128)(2,1)S(1)}, u32[]{:S(2)}, u32[]{:S(2)}) collective-permute-start(bf16[256,192]{0,1:T(8,128)(2,1)S(1)} %get-tuple-element.40), channel_id=1, source_target_pairs={{0,16},{16,0},{1,17},{17,1},{2,18},{18,2},{3,19},{19,3},{4,20},{20... | collective-permute-start | bytes 294920 | tf_op jit(solution)/shard_map/ppermute | solution.py:133
  109.0 0.9 collective-permute-done.4
  109.9 4.1 %convolution_convert_fusion = bf16[3072,192]{1,0:T(8,128)(2,1)} fusion(bf16[256,3072]{0,1:T(8,128)(2,1)} %collective-permute-done.3, bf16[256,3072]{0,1:T(8,128)(2,1)} %get-tuple-element.37, bf16[256,192]{0,1:T(8,128)(2,1)S(1)} %collective-permute-done.4, bf16[256,192]{0,1:T(8,128)(2,1)S(1)} %get-tuple-element.39), kind=kOutput, calls=%fused_computation.2 | convolution fusion | flops 611254272 | bytes 4521984 | tf_op jit(solution)/shard_map/dot_general | solution.py:134
  115.6 1.2 slice.127
  116.8 1.2 reshape.181
  118.2 13.5 %all-to-all-done.1 = bf16[16,196,256]{2,1,0:T(8,128)(2,1)S(1)} async-done(((bf16[16,196,256]{2,1,0:T(8,128)(2,1)}), bf16[16,196,256]{2,1,0:T(8,128)(2,1)S(1)}, u32[]{:S(2)}, u32[]{:S(2)}) %all-to-all-start.1) | async-done | bytes 1605664 | tf_op jit(solution)/shard_map/all_to_all | solution.py:162
  132.1 1.1 fusion.27
  133.5 3.3 %collective-permute-start.1 = (bf16[3,64,192]{2,1,0:T(8,128)(2,1)S(1)}, bf16[3,64,192]{2,1,0:T(8,128)(2,1)S(1)}, u32[]{:S(2)}, u32[]{:S(2)}) collective-permute-start(bf16[3,64,192]{2,1,0:T(8,128)(2,1)S(1)} %bitcast.94), channel_id=1, source_target_pairs={{16,0},{32,16},{48,32},{64,48},{80,64},{96,80},{112,96},{128,112},... | collective-permute-start | bytes 221192 | tf_op jit(solution)/shard_map/ppermute | solution.py:177
  136.8 3.0 %collective-permute-start = (bf16[3,64,192]{2,1,0:T(8,128)(2,1)S(1)}, bf16[3,64,192]{2,1,0:T(8,128)(2,1)S(1)}, u32[]{:S(2)}, u32[]{:S(2)}) collective-permute-start(bf16[3,64,192]{2,1,0:T(8,128)(2,1)S(1)} %bitcast.93), channel_id=1, source_target_pairs={{0,16},{16,32},{32,48},{48,64},{64,80},{80,96},{96,112},{112,128},... | collective-permute-start | bytes 221192 | tf_op jit(solution)/shard_map/ppermute | solution.py:176
  140.9 1.2 collective-permute-done
  142.9 6.6 %shard_map.137 = (bf16[4,64,192]{2,1,0:T(8,128)(2,1)}, f32[49,8,192]{2,1,0:T(8,128)}) custom-call(bf16[10,70,192]{2,1,0:T(8,128)(2,1)} %fusion.18.tall_ref, bf16[4,64,192]{2,1,0:T(8,128)(2,1)} %bitcast.88, bf16[4,64,192]{2,1,0:T(8,128)(2,1)} %bitcast.87, f32[49,192]{1,0:T(8,128)} %copy.51.kernel_ref), custom_call_target="tpu_custom_call" | custom-call | tf_op jit(solution)/shard_map/pallas_call | solution.py:57
  149.6 1.1 reduce_sum.102
  150.9 1.9 collective-permute-start.2
  152.8 1.2 collective-permute-done.2
  154.1 1.2 slice.110
  155.7 1.2 copy.58
  157.7 7.4 %all-to-all-start.2 = ((f32[16,1,678]{2,1,0:T(1,128)}), f32[16,1,678]{2,1,0:T(1,128)S(1)}, u32[]{:S(2)}, u32[]{:S(2)}) async-start(f32[16,1,678]{2,1,0:T(1,128)} %all_to_all.14), calls=%async_computation.2 | async-start | bytes 98304 | tf_op jit(solution)/shard_map/all_to_all | solution.py:196
  165.9 11.3 %all-to-all-done.2 = f32[16,1,678]{2,1,0:T(1,128)S(1)} async-done(((f32[16,1,678]{2,1,0:T(1,128)}), f32[16,1,678]{2,1,0:T(1,128)S(1)}, u32[]{:S(2)}, u32[]{:S(2)}) %all-to-all-start.2) | async-done | bytes 43424 | tf_op jit(solution)/shard_map/all_to_all | solution.py:196
  178.1 7.9 %collective-permute-start.5 = (bf16[96,192]{1,0:T(8,128)(2,1)S(1)}, bf16[96,192]{1,0:T(8,128)(2,1)S(1)}, u32[]{:S(2)}, u32[]{:S(2)}) collective-permute-start(bf16[96,192]{1,0:T(8,128)(2,1)S(1)} %get-tuple-element.42), channel_id=1, source_target_pairs={{0,16},{16,0},{1,17},{17,1},{2,18},{18,2},{3,19},{19,3},{4,20},{20... | collective-permute-start | bytes 110600 | tf_op jit(solution)/shard_map/ppermute | solution.py:141
  (79 shorter events, 13.9 us)
Async XLA Ops:
  7.2 84.8 %all-gather.3.cloned.1.call-start = ((), (), s32[]{:S(2)}) async-start(), calls=%async_computation.5 | async-start | bytes 5677056 | tf_op jit(solution)/shard_map/all_gather | solution.py:28
  13.9 7.7 %copy-start.5 = (f32[3072]{0:T(1024)S(1)}, f32[3072]{0:T(1024)}, u32[]{:S(2)}) copy-start(f32[3072]{0:T(1024)} %param.15) | copy-start | bytes 36868
  13.9 47.5 %all-to-all-start = ((bf16[16,256,384]{1,2,0:T(8,128)(2,1)}), bf16[16,256,384]{1,2,0:T(8,128)(2,1)S(1)}, u32[]{:S(2)}, u32[]{:S(2)}) async-start(bf16[16,256,384]{1,2,0:T(8,128)(2,1)} %broadcast_in_dim.6), calls=%async_computation | async-start | bytes 6291456 | tf_op jit(solution)/shard_map/all_to_all | solution.py:27
  21.6 40.7 %copy-start.6 = (f32[3072]{0:T(1024)S(1)}, f32[3072]{0:T(1024)}, u32[]{:S(2)}) copy-start(f32[3072]{0:T(1024)} %param.16) | copy-start | bytes 36868
  61.4 10.6 %copy-start = (bf16[16,256,384]{1,2,0:T(8,128)(2,1)}, bf16[16,256,384]{1,2,0:T(8,128)(2,1)S(1)}, u32[]{:S(2)}) copy-start(bf16[16,256,384]{1,2,0:T(8,128)(2,1)S(1)} %all-to-all-done) | copy-start | bytes 9437188
  65.4 43.6 %collective-permute-start.3 = (bf16[256,3072]{0,1:T(8,128)(2,1)}, bf16[256,3072]{0,1:T(8,128)(2,1)}, u32[]{:S(2)}, u32[]{:S(2)}) collective-permute-start(bf16[256,3072]{0,1:T(8,128)(2,1)} %get-tuple-element.37), channel_id=1, source_target_pairs={{0,16},{16,0},{1,17},{17,1},{2,18},{18,2},{3,19},{19,3},{4,20},{20... | collective-permute-start | bytes 4718600 | tf_op jit(solution)/shard_map/ppermute | solution.py:129
  92.0 3.0 %slice-start = ((bf16[16,256,384]{1,2,0:T(8,128)(2,1)}), bf16[16,256,192]{1,2,0:T(8,128)(2,1)S(1)}, s32[]{:S(2)}) async-start(bf16[16,256,384]{1,2,0:T(8,128)(2,1)} %copy-done), calls=%async_computation.6 | async-start | bytes 3145728 | tf_op jit(solution)/shard_map/slice | solution.py:111
  92.0 3.0 %copy-start.7 = (bf16[256,384]{1,0:T(8,128)(2,1)S(1)}, bf16[256,384]{1,0:T(8,128)(2,1)}, u32[]{:S(2)}) copy-start(bf16[256,384]{1,0:T(8,128)(2,1)} %param.12) | copy-start | bytes 589828
  95.0 1.9 copy-start.1
  99.6 32.1 %all-to-all-start.1 = ((bf16[16,196,256]{2,1,0:T(8,128)(2,1)}), bf16[16,196,256]{2,1,0:T(8,128)(2,1)S(1)}, u32[]{:S(2)}, u32[]{:S(2)}) async-start(bf16[16,196,256]{2,1,0:T(8,128)(2,1)} %pad_maximum_fusion), calls=%async_computation.1 | async-start | bytes 3276800 | tf_op jit(solution)/shard_map/all_to_all | solution.py:162
  106.2 71.0 %reduce-scatter.2.cloned.1.call-start = ((), (), s32[]{:S(2)}) async-start(), calls=%async_computation.4 | async-start | bytes 1671168 | tf_op jit(solution)/shard_map/reduce_scatter | solution.py:138
  106.5 3.4 %collective-permute-start.4 = (bf16[256,192]{0,1:T(8,128)(2,1)S(1)}, bf16[256,192]{0,1:T(8,128)(2,1)S(1)}, u32[]{:S(2)}, u32[]{:S(2)}) collective-permute-start(bf16[256,192]{0,1:T(8,128)(2,1)S(1)} %get-tuple-element.40), channel_id=1, source_target_pairs={{0,16},{16,0},{1,17},{17,1},{2,18},{18,2},{3,19},{19,3},{4,20},{20... | collective-permute-start | bytes 294920 | tf_op jit(solution)/shard_map/ppermute | solution.py:133
  109.9 4.1 %copy-start.2 = (bf16[256,192]{0,1:T(8,128)(2,1)S(1)}, bf16[256,192]{0,1:T(8,128)(2,1)}, u32[]{:S(2)}) copy-start(bf16[256,192]{0,1:T(8,128)(2,1)} %param.13) | copy-start | bytes 294916
  109.9 4.9 %copy-start.4 = (bf16[256,192]{0,1:T(8,128)(2,1)S(1)}, bf16[256,192]{0,1:T(8,128)(2,1)}, u32[]{:S(2)}) copy-start(bf16[256,192]{0,1:T(8,128)(2,1)} %param.10) | copy-start | bytes 294916
  133.5 7.4 %collective-permute-start.1 = (bf16[3,64,192]{2,1,0:T(8,128)(2,1)S(1)}, bf16[3,64,192]{2,1,0:T(8,128)(2,1)S(1)}, u32[]{:S(2)}, u32[]{:S(2)}) collective-permute-start(bf16[3,64,192]{2,1,0:T(8,128)(2,1)S(1)} %bitcast.94), channel_id=1, source_target_pairs={{16,0},{32,16},{48,32},{64,48},{80,64},{96,80},{112,96},{128,112},... | collective-permute-start | bytes 221192 | tf_op jit(solution)/shard_map/ppermute | solution.py:177
  136.8 5.3 %collective-permute-start = (bf16[3,64,192]{2,1,0:T(8,128)(2,1)S(1)}, bf16[3,64,192]{2,1,0:T(8,128)(2,1)S(1)}, u32[]{:S(2)}, u32[]{:S(2)}) collective-permute-start(bf16[3,64,192]{2,1,0:T(8,128)(2,1)S(1)} %bitcast.93), channel_id=1, source_target_pairs={{0,16},{16,32},{32,48},{48,64},{64,80},{80,96},{96,112},{112,128},... | collective-permute-start | bytes 221192 | tf_op jit(solution)/shard_map/ppermute | solution.py:176
  149.6 15.6 %copy-start.3 = (bf16[4,64,192]{2,1,0:T(8,128)(2,1)S(1)}, bf16[4,64,192]{2,1,0:T(8,128)(2,1)}, u32[]{:S(2)}) copy-start(bf16[4,64,192]{2,1,0:T(8,128)(2,1)} %get-tuple-element.7) | copy-start | bytes 294916
  150.9 3.1 %collective-permute-start.2 = (f32[9792]{0:T(1024)S(1)}, f32[9792]{0:T(1024)S(1)}, u32[]{:S(2)}, u32[]{:S(2)}) collective-permute-start(f32[9792]{0:T(1024)S(1)} %concatenate.34), channel_id=1, source_target_pairs={{0,16},{16,0},{1,17},{17,1},{2,18},{18,2},{3,19},{19,3},{4,20},{20... | collective-permute-start | bytes 117512 | tf_op jit(solution)/shard_map/ppermute | solution.py:190
  157.7 19.5 %all-to-all-start.2 = ((f32[16,1,678]{2,1,0:T(1,128)}), f32[16,1,678]{2,1,0:T(1,128)S(1)}, u32[]{:S(2)}, u32[]{:S(2)}) async-start(f32[16,1,678]{2,1,0:T(1,128)} %all_to_all.14), calls=%async_computation.2 | async-start | bytes 98304 | tf_op jit(solution)/shard_map/all_to_all | solution.py:196
  178.1 9.3 %collective-permute-start.5 = (bf16[96,192]{1,0:T(8,128)(2,1)S(1)}, bf16[96,192]{1,0:T(8,128)(2,1)S(1)}, u32[]{:S(2)}, u32[]{:S(2)}) collective-permute-start(bf16[96,192]{1,0:T(8,128)(2,1)S(1)} %get-tuple-element.42), channel_id=1, source_target_pairs={{0,16},{16,0},{1,17},{17,1},{2,18},{18,2},{3,19},{19,3},{4,20},{20... | collective-permute-start | bytes 110600 | tf_op jit(solution)/shard_map/ppermute | solution.py:141
Sparse Core Ops, SparseCore 0:
  10.1 81.8 all-gather.2
  114.1 58.6 reduce-scatter.1

commit v10 on v9

--- a/solution.py
+++ b/solution.py
@@ -122,15 +122,17 @@
     zhat_own = lax.dynamic_slice_in_dim(zhat_full, col_rank * channels, channels, 1)
     gain_own = lax.dynamic_slice_in_dim(norm_gain, col_rank * channels, channels, 0)
 
-    grad_act = jnp.dot(scaled_full, w_out_full, preferred_element_type=jnp.float32)
-    grad_pre = (grad_act * gelu_slope(hidden_pre.astype(jnp.float32))).astype(jnp.bfloat16)
-
     core = lax.axis_index("core")
+    scaled_pair = jnp.concatenate([scaled_full, lax.ppermute(scaled_full, "core", SWAP)], axis=0)
+    hidden_pair = jnp.concatenate([hidden_pre, lax.ppermute(hidden_pre, "core", SWAP)], axis=0)
+    grad_act = jnp.dot(scaled_pair, w_out_full, preferred_element_type=jnp.float32)
+    grad_pair_full = (grad_act * gelu_slope(hidden_pair.astype(jnp.float32))).astype(jnp.bfloat16)
+    grad_pre = grad_pair_full[:tokens]
+
     normed_pair = jnp.concatenate([normed_full, lax.ppermute(normed_full, "core", SWAP)], axis=0)
-    grad_halves = grad_pre.reshape(tokens, 2, hidden // 2)
-    kept = lax.dynamic_index_in_dim(grad_halves, core, axis=1, keepdims=False)
-    given = lax.dynamic_index_in_dim(grad_halves, 1 - core, axis=1, keepdims=False)
-    grad_pair = jnp.concatenate([kept, lax.ppermute(given, "core", SWAP)], axis=0)
+    grad_pair = lax.dynamic_index_in_dim(
+        grad_pair_full.reshape(2 * tokens, 2, hidden // 2), core, axis=1, keepdims=False
+    )
     chip_sum = lax.dot_general(
         normed_pair, grad_pair, (((0,), (0,)), ((), ())), preferred_element_type=jnp.float32
     )

time: 196 us -> 194 us (0.990)
  waiting for transfers between devices: 87.8 us -> 81.3 us
  matrix products: 6.46 us -> 8.82 us
    ppermute x1 -> x2, starting transfers between devices: 2.47 us -> 11.5 us  [the longest x1 6.57 us: body(): lax.ppermute(scaled_full, 'core', SWAP)]
    all_to_all x1, waiting for transfers between devices: 39.7 us -> 34.6 us  [gather_blocks(): return lax.all_to_all(wide, axis_name, 0, 0, tiled=True)]
    ppermute x1, starting transfers between devices: 6.57 us -> 1.91 us  [body(): lax.ppermute(normed_full, 'core', SWAP)]
    all_to_all x1, waiting for transfers between devices: 13.5 us -> 17 us  [body(): incoming = lax.all_to_all(outgoing, 'col', 0, 0, tiled=True)]
    all_gather x1, waiting for transfers between devices: 20 us -> 16.8 us  [gather_blocks(): return lax.all_gather(x, axis_name, axis=0, tiled=False)]
    dot_general x1, matrix products: 1.07 us -> 3.49 us  [body(): jnp.dot(scaled_pair, w_out_full, preferred_element_type=jnp.float32)]
    ppermute x1, starting transfers between devices: 7.88 us -> 5.78 us  [body(): lax.ppermute(lax.dynamic_index_in_dim(chip_rows, 1 - core, axis=0, keepdi...]
    unnamed x21 -> x22, local copies, waits for them, and re-layouts: 3.93 us -> 3.3 us
  transfers between devices with their start and end apart: 11 -> 12, of which waited for: 7 -> 6; matrix products, arithmetic and copies ran while one was open for 17% -> 19% of each run, Pallas kernels for 3% -> 3%
where the time goes in v10:
time: 194 us; the launch traced here: 193 us
  waiting for transfers between devices  81.3 us (42%)
  starting transfers between devices  48.9 us (25%)
  local copies, waits for them, and re-layouts  19.3 us (10%)
  between operations  14.5 us (7%)
  other arithmetic  13.9 us (7%)
  matrix products  8.82 us (5%)
  Pallas kernels  6.63 us (3%)
    all_to_all x1, waiting for transfers between devices, gather_blocks(): return lax.all_to_all(wide, axis_name, 0, 0, tiled=True)  34.6 us
    all_to_all x1, waiting for transfers between devices, body(): incoming = lax.all_to_all(outgoing, 'col', 0, 0, tiled=True)  17 us
    all_gather x1, waiting for transfers between devices, gather_blocks(): return lax.all_gather(x, axis_name, axis=0, tiled=False)  16.8 us
    all_to_all x1, waiting for transfers between devices, body(): lax.all_to_all(jnp.concatenate([kernel_chip, norm_chip], axis=1), 'z', 0,...  10.6 us
    all_to_all x1, starting transfers between devices, gather_blocks(): return lax.all_to_all(wide, axis_name, 0, 0, tiled=True)  7.72 us
    all_to_all x1, starting transfers between devices, body(): lax.all_to_all(jnp.concatenate([kernel_chip, norm_chip], axis=1), 'z', 0,...  7.1 us
    pallas_call x1, Pallas kernels, conv_call(): pl.pallas_call(conv_body, out_shape=(jax.ShapeDtypeStruct((rows, span, ch...  6.63 us
    all_to_all x1, starting transfers between devices, body(): incoming = lax.all_to_all(outgoing, 'col', 0, 0, tiled=True)  6.62 us
  transfers between devices with their start and end apart: 12, of which 6 were waited for; matrix products, arithmetic and copies ran while one was open for 19% of the time, Pallas kernels for 3%

profile of v10, /device:TPU:1, one launch (start us, length us, event | category | flops | bytes accessed | tf_op | source)
XLA Modules:
  0.0 193.3 jit_solution(15847625273870831075)
XLA Ops:
  8.4 1.6 pad_maximum_fusion.2
  11.9 2.0 %broadcast_in_dim.6 = bf16[16,256,384]{1,2,0:T(8,128)(2,1)} broadcast(bf16[256,384]{0,1:T(8,128)(2,1)S(1)} %pad_maximum_fusion.1), dimensions={1,2} | broadcast | bytes 3342336 | tf_op jit(solution)/shard_map/broadcast_in_dim | solution.py:26
  13.9 7.7 %all-to-all-start = ((bf16[16,256,384]{1,2,0:T(8,128)(2,1)}), bf16[16,256,384]{1,2,0:T(8,128)(2,1)S(1)}, u32[]{:S(2)}, u32[]{:S(2)}) async-start(bf16[16,256,384]{1,2,0:T(8,128)(2,1)} %broadcast_in_dim.6), calls=%async_computation | async-start | bytes 6291456 | tf_op jit(solution)/shard_map/all_to_all | solution.py:27
  21.8 4.9 %collective-permute-start.1 = (bf16[256,384]{0,1:T(8,128)(2,1)S(1)}, bf16[256,384]{0,1:T(8,128)(2,1)}, u32[]{:S(2)}, u32[]{:S(2)}) collective-permute-start(bf16[256,384]{0,1:T(8,128)(2,1)S(1)} %copy.52), channel_id=1, source_target_pairs={{0,16},{16,0},{1,17},{17,1},{2,18},{18,2},{3,19},{19,3},{4,20},{20... | collective-permute-start | bytes 589832 | tf_op jit(solution)/shard_map/ppermute | solution.py:127
  26.8 34.6 %all-to-all-done = bf16[16,256,384]{1,2,0:T(8,128)(2,1)S(1)} async-done(((bf16[16,256,384]{1,2,0:T(8,128)(2,1)}), bf16[16,256,384]{1,2,0:T(8,128)(2,1)S(1)}, u32[]{:S(2)}, u32[]{:S(2)}) %all-to-all-start) | async-done | bytes 3145760 | tf_op jit(solution)/shard_map/all_to_all | solution.py:27
  61.4 1.3 slice.121
  62.7 6.6 %collective-permute-start = (bf16[256,3072]{0,1:T(8,128)(2,1)}, bf16[256,3072]{0,1:T(8,128)(2,1)}, u32[]{:S(2)}, u32[]{:S(2)}) collective-permute-start(bf16[256,3072]{0,1:T(8,128)(2,1)} %bitcast.6), channel_id=1, source_target_pairs={{0,16},{16,0},{1,17},{17,1},{2,18},{18,2},{3,19},{19,3},{4,20},{20... | collective-permute-start | bytes 4718600 | tf_op jit(solution)/shard_map/ppermute | solution.py:126
  70.2 3.0 %add_convert_fusion = (bf16[256,3072]{0,1:T(8,128)(2,1)}, f32[256,3072]{0,1:T(8,128)}) fusion(f32[3072]{0:T(1024)S(1)} %copy-done.5, f32[3072]{0:T(1024)S(1)} %copy-done.4, f32[256]{0:T(256)S(1)} %add_rsqrt_fusion, f32[256]{0:T(256)S(1)} %broadcast_multiply_fusion, bf16[16,256,384]{1,2,0:T(8,128)(2,1)S(1)} %all-to-all-done), kind=kLoop, calls=%fused_computation.14 | loop fusion | flops 4718592 | bytes 6318080 | tf_op jit(solution)/shard_map/convert_element_type | solution.py:121
  73.3 1.9 collective-permute-start.5
  75.2 16.8 %all-gather.3.cloned.1.call-done = bf16[3072,778]{1,0:T(8,128)(2,1)} async-done(((bf16[96,778]{1,0:T(8,128)(2,1)}), bf16[3072,778]{1,0:T(8,128)(2,1)}) %all-gather.3.cloned.1.call-update) | async-done | bytes 4780048 | tf_op jit(solution)/shard_map/all_gather | solution.py:28
  92.0 2.9 %fusion.47 = (bf16[32,96,384]{2,1,0:T(8,128)(2,1)S(1)}, bf16[32,96,384]{2,1,0:T(8,128)(2,1)S(1)}) fusion(bf16[32,96,778]{2,1,0:T(8,128)(2,1)} %bitcast.78), kind=kLoop, calls=%fused_computation.88 | loop fusion | bytes 9437184 | tf_op jit(solution)/shard_map/slice | solution.py:113
  94.9 3.5 %fusion.13 = bf16[512,384]{0,1:T(8,128)(2,1)S(1)} fusion(bf16[3072,384]{1,0:T(8,128)(2,1)S(1)} %bitcast.81, bf16[256,3072]{0,1:T(8,128)(2,1)} %collective-permute-done, bf16[256,3072]{0,1:T(8,128)(2,1)} %bitcast.6, bf16[256,384]{0,1:T(8,128)(2,1)} %collective-permute-done.1, bf16[256,384]{0,1:T(8,128)(2,1)S(1)} %copy.52), kind=kOutput, calls=%fused_computation.26 | convolution fusion | flops 1217003520 | bytes 6291456 | tf_op jit(solution)/shard_map/dot_general | solution.py:128
  98.4 1.2 fusion.9
  99.7 1.3 pad_maximum_fusion
  101.1 6.6 %all-to-all-start.1 = ((bf16[16,196,256]{2,1,0:T(8,128)(2,1)}), bf16[16,196,256]{2,1,0:T(8,128)(2,1)S(1)}, u32[]{:S(2)}, u32[]{:S(2)}) async-start(bf16[16,196,256]{2,1,0:T(8,128)(2,1)} %pad_maximum_fusion), calls=%async_computation.1 | async-start | bytes 3276800 | tf_op jit(solution)/shard_map/all_to_all | solution.py:164
  107.8 4.1 %convolution_convert_fusion = bf16[3072,192]{1,0:T(8,128)(2,1)} fusion(bf16[256,3072]{0,1:T(8,128)(2,1)} %collective-permute-done.5, bf16[256,3072]{0,1:T(8,128)(2,1)} %get-tuple-element.37, bf16[512,2,192]{0,2,1:T(8,128)(2,1)S(1)} %bitcast.96, s32[]{:T(128)S(6)} %select_n.24), kind=kOutput, calls=%fused_computation.2 | convolution fusion | flops 610861056 | bytes 4521988 | tf_op jit(solution)/shard_map/dot_general | solution.py:136
  113.5 1.2 slice.132
  114.7 1.2 reshape.181
  116.1 17.0 %all-to-all-done.1 = bf16[16,196,256]{2,1,0:T(8,128)(2,1)S(1)} async-done(((bf16[16,196,256]{2,1,0:T(8,128)(2,1)}), bf16[16,196,256]{2,1,0:T(8,128)(2,1)S(1)}, u32[]{:S(2)}, u32[]{:S(2)}) %all-to-all-start.1) | async-done | bytes 1605664 | tf_op jit(solution)/shard_map/all_to_all | solution.py:164
  133.6 1.1 fusion.34
  135.0 3.3 %collective-permute-start.3 = (bf16[3,64,192]{2,1,0:T(8,128)(2,1)S(1)}, bf16[3,64,192]{2,1,0:T(8,128)(2,1)S(1)}, u32[]{:S(2)}, u32[]{:S(2)}) collective-permute-start(bf16[3,64,192]{2,1,0:T(8,128)(2,1)S(1)} %bitcast.90), channel_id=1, source_target_pairs={{16,0},{32,16},{48,32},{64,48},{80,64},{96,80},{112,96},{128,112},... | collective-permute-start | bytes 221192 | tf_op jit(solution)/shard_map/ppermute | solution.py:179
  138.3 3.0 %collective-permute-start.2 = (bf16[3,64,192]{2,1,0:T(8,128)(2,1)S(1)}, bf16[3,64,192]{2,1,0:T(8,128)(2,1)S(1)}, u32[]{:S(2)}, u32[]{:S(2)}) collective-permute-start(bf16[3,64,192]{2,1,0:T(8,128)(2,1)S(1)} %bitcast.89), channel_id=1, source_target_pairs={{0,16},{16,32},{32,48},{48,64},{64,80},{80,96},{96,112},{112,128},... | collective-permute-start | bytes 221192 | tf_op jit(solution)/shard_map/ppermute | solution.py:178
  142.4 1.1 collective-permute-done.2
  144.3 6.6 %shard_map.137 = (bf16[4,64,192]{2,1,0:T(8,128)(2,1)}, f32[49,8,192]{2,1,0:T(8,128)}) custom-call(bf16[10,70,192]{2,1,0:T(8,128)(2,1)} %fusion.27.tall_ref, bf16[4,64,192]{2,1,0:T(8,128)(2,1)} %bitcast.84, bf16[4,64,192]{2,1,0:T(8,128)(2,1)} %bitcast.83, f32[49,192]{1,0:T(8,128)} %copy.61.kernel_ref), custom_call_target="tpu_custom_call" | custom-call | tf_op jit(solution)/shard_map/pallas_call | solution.py:57
  151.0 1.1 reduce_sum.102
  152.3 1.9 collective-permute-start.4
  154.2 1.2 collective-permute-done.4
  155.5 1.2 slice.114
  157.1 1.2 copy.69
  159.1 7.1 %all-to-all-start.2 = ((f32[16,1,678]{2,1,0:T(1,128)}), f32[16,1,678]{2,1,0:T(1,128)S(1)}, u32[]{:S(2)}, u32[]{:S(2)}) async-start(f32[16,1,678]{2,1,0:T(1,128)} %all_to_all.14), calls=%async_computation.2 | async-start | bytes 98304 | tf_op jit(solution)/shard_map/all_to_all | solution.py:198
  167.0 10.6 %all-to-all-done.2 = f32[16,1,678]{2,1,0:T(1,128)S(1)} async-done(((f32[16,1,678]{2,1,0:T(1,128)}), f32[16,1,678]{2,1,0:T(1,128)S(1)}, u32[]{:S(2)}, u32[]{:S(2)}) %all-to-all-start.2) | async-done | bytes 43424 | tf_op jit(solution)/shard_map/all_to_all | solution.py:198
  178.5 5.8 %collective-permute-start.6 = (bf16[96,192]{1,0:T(8,128)(2,1)S(1)}, bf16[96,192]{1,0:T(8,128)(2,1)S(1)}, u32[]{:S(2)}, u32[]{:S(2)}) collective-permute-start(bf16[96,192]{1,0:T(8,128)(2,1)S(1)} %get-tuple-element.40), channel_id=1, source_target_pairs={{0,16},{16,0},{1,17},{17,1},{2,18},{18,2},{3,19},{19,3},{4,20},{20... | collective-permute-start | bytes 110600 | tf_op jit(solution)/shard_map/ppermute | solution.py:143
  (79 shorter events, 14.2 us)
Async XLA Ops:
  7.2 84.8 %all-gather.3.cloned.1.call-start = ((), (), s32[]{:S(2)}) async-start(), calls=%async_computation.5 | async-start | bytes 5677056 | tf_op jit(solution)/shard_map/all_gather | solution.py:28
  13.9 7.7 %copy-start.1 = (bf16[256,384]{1,0:T(8,128)(2,1)S(1)}, bf16[256,384]{1,0:T(8,128)(2,1)}, u32[]{:S(2)}) copy-start(bf16[256,384]{1,0:T(8,128)(2,1)} %param.12) | copy-start | bytes 589828
  13.9 12.8 %copy-start.4 = (f32[3072]{0:T(1024)S(1)}, f32[3072]{0:T(1024)}, u32[]{:S(2)}) copy-start(f32[3072]{0:T(1024)} %param.15) | copy-start | bytes 36868
  13.9 47.5 %all-to-all-start = ((bf16[16,256,384]{1,2,0:T(8,128)(2,1)}), bf16[16,256,384]{1,2,0:T(8,128)(2,1)S(1)}, u32[]{:S(2)}, u32[]{:S(2)}) async-start(bf16[16,256,384]{1,2,0:T(8,128)(2,1)} %broadcast_in_dim.6), calls=%async_computation | async-start | bytes 6291456 | tf_op jit(solution)/shard_map/all_to_all | solution.py:27
  21.8 73.1 %collective-permute-start.1 = (bf16[256,384]{0,1:T(8,128)(2,1)S(1)}, bf16[256,384]{0,1:T(8,128)(2,1)}, u32[]{:S(2)}, u32[]{:S(2)}) collective-permute-start(bf16[256,384]{0,1:T(8,128)(2,1)S(1)} %copy.52), channel_id=1, source_target_pairs={{0,16},{16,0},{1,17},{17,1},{2,18},{18,2},{3,19},{19,3},{4,20},{20... | collective-permute-start | bytes 589832 | tf_op jit(solution)/shard_map/ppermute | solution.py:127
  26.8 43.4 %copy-start.5 = (f32[3072]{0:T(1024)S(1)}, f32[3072]{0:T(1024)}, u32[]{:S(2)}) copy-start(f32[3072]{0:T(1024)} %param.16) | copy-start | bytes 36868
  62.7 32.2 %collective-permute-start = (bf16[256,3072]{0,1:T(8,128)(2,1)}, bf16[256,3072]{0,1:T(8,128)(2,1)}, u32[]{:S(2)}, u32[]{:S(2)}) collective-permute-start(bf16[256,3072]{0,1:T(8,128)(2,1)} %bitcast.6), channel_id=1, source_target_pairs={{0,16},{16,0},{1,17},{17,1},{2,18},{18,2},{3,19},{19,3},{4,20},{20... | collective-permute-start | bytes 4718600 | tf_op jit(solution)/shard_map/ppermute | solution.py:126
  73.3 34.5 %collective-permute-start.5 = (bf16[256,3072]{0,1:T(8,128)(2,1)}, bf16[256,3072]{0,1:T(8,128)(2,1)}, u32[]{:S(2)}, u32[]{:S(2)}) collective-permute-start(bf16[256,3072]{0,1:T(8,128)(2,1)} %get-tuple-element.37), channel_id=1, source_target_pairs={{0,16},{16,0},{1,17},{17,1},{2,18},{18,2},{3,19},{19,3},{4,20},{20... | collective-permute-start | bytes 4718600 | tf_op jit(solution)/shard_map/ppermute | solution.py:132
  98.4 1.3 copy-start.6
  99.7 8.0 %copy-start.7 = (bf16[512,384]{0,1:T(8,128)(2,1)S(1)}, bf16[512,384]{0,1:T(8,128)(2,1)}, u32[]{:S(2)}) copy-start(bf16[512,384]{0,1:T(8,128)(2,1)} %copy-done.6) | copy-start | bytes 1179652
  101.1 32.1 %all-to-all-start.1 = ((bf16[16,196,256]{2,1,0:T(8,128)(2,1)}), bf16[16,196,256]{2,1,0:T(8,128)(2,1)S(1)}, u32[]{:S(2)}, u32[]{:S(2)}) async-start(bf16[16,196,256]{2,1,0:T(8,128)(2,1)} %pad_maximum_fusion), calls=%async_computation.1 | async-start | bytes 3276800 | tf_op jit(solution)/shard_map/all_to_all | solution.py:164
  107.7 70.0 %reduce-scatter.2.cloned.1.call-start = ((), (), s32[]{:S(2)}) async-start(), calls=%async_computation.4 | async-start | bytes 1671168 | tf_op jit(solution)/shard_map/reduce_scatter | solution.py:140
  107.8 4.1 %copy-start = (bf16[256,192]{0,1:T(8,128)(2,1)S(1)}, bf16[256,192]{0,1:T(8,128)(2,1)}, u32[]{:S(2)}) copy-start(bf16[256,192]{0,1:T(8,128)(2,1)} %param.13) | copy-start | bytes 294916
  107.8 5.0 %copy-start.3 = (bf16[256,192]{0,1:T(8,128)(2,1)S(1)}, bf16[256,192]{0,1:T(8,128)(2,1)}, u32[]{:S(2)}) copy-start(bf16[256,192]{0,1:T(8,128)(2,1)} %param.10) | copy-start | bytes 294916
  135.0 7.4 %collective-permute-start.3 = (bf16[3,64,192]{2,1,0:T(8,128)(2,1)S(1)}, bf16[3,64,192]{2,1,0:T(8,128)(2,1)S(1)}, u32[]{:S(2)}, u32[]{:S(2)}) collective-permute-start(bf16[3,64,192]{2,1,0:T(8,128)(2,1)S(1)} %bitcast.90), channel_id=1, source_target_pairs={{16,0},{32,16},{48,32},{64,48},{80,64},{96,80},{112,96},{128,112},... | collective-permute-start | bytes 221192 | tf_op jit(solution)/shard_map/ppermute | solution.py:179
  138.3 5.2 %collective-permute-start.2 = (bf16[3,64,192]{2,1,0:T(8,128)(2,1)S(1)}, bf16[3,64,192]{2,1,0:T(8,128)(2,1)S(1)}, u32[]{:S(2)}, u32[]{:S(2)}) collective-permute-start(bf16[3,64,192]{2,1,0:T(8,128)(2,1)S(1)} %bitcast.89), channel_id=1, source_target_pairs={{0,16},{16,32},{32,48},{48,64},{64,80},{80,96},{96,112},{112,128},... | collective-permute-start | bytes 221192 | tf_op jit(solution)/shard_map/ppermute | solution.py:178
  151.0 15.3 %copy-start.2 = (bf16[4,64,192]{2,1,0:T(8,128)(2,1)S(1)}, bf16[4,64,192]{2,1,0:T(8,128)(2,1)}, u32[]{:S(2)}) copy-start(bf16[4,64,192]{2,1,0:T(8,128)(2,1)} %get-tuple-element.7) | copy-start | bytes 294916
  152.3 3.1 %collective-permute-start.4 = (f32[9792]{0:T(1024)S(1)}, f32[9792]{0:T(1024)S(1)}, u32[]{:S(2)}, u32[]{:S(2)}) collective-permute-start(f32[9792]{0:T(1024)S(1)} %concatenate.39), channel_id=1, source_target_pairs={{0,16},{16,0},{1,17},{17,1},{2,18},{18,2},{3,19},{19,3},{4,20},{20... | collective-permute-start | bytes 117512 | tf_op jit(solution)/shard_map/ppermute | solution.py:192
  159.1 18.5 %all-to-all-start.2 = ((f32[16,1,678]{2,1,0:T(1,128)}), f32[16,1,678]{2,1,0:T(1,128)S(1)}, u32[]{:S(2)}, u32[]{:S(2)}) async-start(f32[16,1,678]{2,1,0:T(1,128)} %all_to_all.14), calls=%async_computation.2 | async-start | bytes 98304 | tf_op jit(solution)/shard_map/all_to_all | solution.py:198
  178.5 7.2 %collective-permute-start.6 = (bf16[96,192]{1,0:T(8,128)(2,1)S(1)}, bf16[96,192]{1,0:T(8,128)(2,1)S(1)}, u32[]{:S(2)}, u32[]{:S(2)}) collective-permute-start(bf16[96,192]{1,0:T(8,128)(2,1)S(1)} %get-tuple-element.40), channel_id=1, source_target_pairs={{0,16},{16,0},{1,17},{17,1},{2,18},{18,2},{3,19},{19,3},{4,20},{20... | collective-permute-start | bytes 110600 | tf_op jit(solution)/shard_map/ppermute | solution.py:143
Sparse Core Ops, SparseCore 0:
  10.1 81.8 all-gather.2
  112.0 58.2 reduce-scatter.1

commit v11 on v10

--- a/solution.py
+++ b/solution.py
@@ -96,22 +96,23 @@
     scaled = (cotangent.astype(jnp.float32) * layer_scale).astype(jnp.bfloat16)
     acts = gather_blocks(jnp.concatenate([scaled, conv_out], axis=1), "col", n_col, ACTS_VIA)
     kernel_bits = split_three(conv_kernel).reshape(-1)
-    lanes_extra = -(-kernel_bits.shape[0] // w_in.shape[0])
-    kernel_bits = jnp.pad(kernel_bits, (0, lanes_extra * w_in.shape[0] - kernel_bits.shape[0]))
+    rows_extra = -(-kernel_bits.shape[0] // hidden)
+    kernel_bits = jnp.pad(kernel_bits, (0, rows_extra * hidden - kernel_bits.shape[0]))
+    block_rows = w_in.shape[0]
     weights = gather_blocks(
-        jnp.concatenate([w_out, w_in, kernel_bits.reshape(w_in.shape[0], lanes_extra)], axis=1),
+        jnp.concatenate([w_out, w_in, kernel_bits.reshape(rows_extra, hidden)], axis=0),
         ROW,
         n_row,
         WEIGHTS_VIA,
     )
-    kernel_parts = weights[:, :, 2 * hidden :].reshape(n_row, -1)[:, : 3 * KS * KS * few]
+    kernel_parts = weights[:, 2 * block_rows :].reshape(n_row, -1)[:, : 3 * KS * KS * few]
     kernel_parts = kernel_parts.reshape(n_row, 3, KS * KS, few).astype(jnp.float32)
     kernel_sum = kernel_parts[:, 0] + kernel_parts[:, 1] + kernel_parts[:, 2]
     kernel_rows_full = jnp.transpose(kernel_sum, (1, 0, 2)).reshape(KS * KS, n_row * few)
     scaled_full = jnp.transpose(acts[:, :, :channels], (1, 0, 2)).reshape(tokens, width)
     inputs_full = jnp.transpose(acts[:, :, channels:], (1, 0, 2)).reshape(tokens, width)
-    w_out_full = weights[:, :, :hidden].reshape(width, hidden)
-    w_in_full = weights[:, :, hidden : 2 * hidden].reshape(width, hidden)
+    w_out_full = weights[:, :block_rows].reshape(width, hidden)
+    w_in_full = weights[:, block_rows : 2 * block_rows].reshape(width, hidden)
 
     values = inputs_full.astype(jnp.float32)
     mean = jnp.mean(values, axis=1, keepdims=True)

time: 194 us -> 194 us (level)
    slice x3 -> x2, local copies, waits for them, and re-layouts: 4.05 us -> 3.81 us  [the longest x1 2.85 us: body(): w_out_full = weights[:, :block_rows].reshape(width, hidden)]
  transfers between devices with their start and end apart: 12 -> 12, of which waited for: 6 -> 6; matrix products, arithmetic and copies ran while one was open for 19% -> 18% of each run, Pallas kernels for 3% -> 3%
where the time goes in v11:
time: 194 us; the launch traced here: 193 us
  waiting for transfers between devices  82.5 us (43%)
  starting transfers between devices  49 us (25%)
  local copies, waits for them, and re-layouts  17.7 us (9%)
  between operations  14.5 us (7%)
  other arithmetic  13.9 us (7%)
  matrix products  8.81 us (5%)
  Pallas kernels  6.63 us (3%)
    all_to_all x1, waiting for transfers between devices, gather_blocks(): return lax.all_to_all(wide, axis_name, 0, 0, tiled=True)  34.6 us
    all_to_all x1, waiting for transfers between devices, body(): incoming = lax.all_to_all(outgoing, 'col', 0, 0, tiled=True)  18.5 us
    all_gather x1, waiting for transfers between devices, gather_blocks(): return lax.all_gather(x, axis_name, axis=0, tiled=False)  16.1 us
    all_to_all x1, waiting for transfers between devices, body(): lax.all_to_all(jnp.concatenate([kernel_chip, norm_chip], axis=1), 'z', 0,...  10.8 us
    all_to_all x1, starting transfers between devices, gather_blocks(): return lax.all_to_all(wide, axis_name, 0, 0, tiled=True)  7.72 us
    all_to_all x1, starting transfers between devices, body(): lax.all_to_all(jnp.concatenate([kernel_chip, norm_chip], axis=1), 'z', 0,...  7.34 us
    pallas_call x1, Pallas kernels, conv_call(): pl.pallas_call(conv_body, out_shape=(jax.ShapeDtypeStruct((rows, span, ch...  6.63 us
    ppermute x1, starting transfers between devices, body(): lax.ppermute(scaled_full, 'core', SWAP)  6.57 us
  transfers between devices with their start and end apart: 12, of which 6 were waited for; matrix products, arithmetic and copies ran while one was open for 18% of the time, Pallas kernels for 3%

profile of v11, /device:TPU:1, one launch (start us, length us, event | category | flops | bytes accessed | tf_op | source)
XLA Modules:
  0.0 193.0 jit_solution(4479380934441253930)
XLA Ops:
  8.2 1.6 maximum_bitcast_fusion
  9.9 1.0 multiply_convert_fusion
  11.8 1.9 %broadcast_in_dim.6 = bf16[16,256,384]{1,2,0:T(8,128)(2,1)} broadcast(bf16[256,384]{0,1:T(8,128)(2,1)S(1)} %pad_maximum_fusion.1), dimensions={1,2} | broadcast | bytes 3342336 | tf_op jit(solution)/shard_map/broadcast_in_dim | solution.py:26
  13.7 7.7 %all-to-all-start = ((bf16[16,256,384]{1,2,0:T(8,128)(2,1)}), bf16[16,256,384]{1,2,0:T(8,128)(2,1)S(1)}, u32[]{:S(2)}, u32[]{:S(2)}) async-start(bf16[16,256,384]{1,2,0:T(8,128)(2,1)} %broadcast_in_dim.6), calls=%async_computation | async-start | bytes 6291456 | tf_op jit(solution)/shard_map/all_to_all | solution.py:27
  21.6 4.9 %collective-permute-start.1 = (bf16[256,384]{0,1:T(8,128)(2,1)S(1)}, bf16[256,384]{0,1:T(8,128)(2,1)}, u32[]{:S(2)}, u32[]{:S(2)}) collective-permute-start(bf16[256,384]{0,1:T(8,128)(2,1)S(1)} %copy.52), channel_id=1, source_target_pairs={{0,16},{16,0},{1,17},{17,1},{2,18},{18,2},{3,19},{19,3},{4,20},{20... | collective-permute-start | bytes 589832 | tf_op jit(solution)/shard_map/ppermute | solution.py:128
  26.6 34.6 %all-to-all-done = bf16[16,256,384]{1,2,0:T(8,128)(2,1)S(1)} async-done(((bf16[16,256,384]{1,2,0:T(8,128)(2,1)}), bf16[16,256,384]{1,2,0:T(8,128)(2,1)S(1)}, u32[]{:S(2)}, u32[]{:S(2)}) %all-to-all-start) | async-done | bytes 3145760 | tf_op jit(solution)/shard_map/all_to_all | solution.py:27
  61.2 1.3 slice.121
  62.5 6.6 %collective-permute-start = (bf16[256,3072]{0,1:T(8,128)(2,1)}, bf16[256,3072]{0,1:T(8,128)(2,1)}, u32[]{:S(2)}, u32[]{:S(2)}) collective-permute-start(bf16[256,3072]{0,1:T(8,128)(2,1)} %bitcast.6), channel_id=1, source_target_pairs={{0,16},{16,0},{1,17},{17,1},{2,18},{18,2},{3,19},{19,3},{4,20},{20... | collective-permute-start | bytes 4718600 | tf_op jit(solution)/shard_map/ppermute | solution.py:127
  70.0 3.0 %add_convert_fusion = (bf16[256,3072]{0,1:T(8,128)(2,1)}, f32[256,3072]{0,1:T(8,128)}) fusion(f32[3072]{0:T(1024)S(1)} %copy-done.5, f32[3072]{0:T(1024)S(1)} %copy-done.4, f32[256]{0:T(256)S(1)} %add_rsqrt_fusion, f32[256]{0:T(256)S(1)} %broadcast_multiply_fusion, bf16[16,256,384]{1,2,0:T(8,128)(2,1)S(1)} %all-to-all-done), kind=kLoop, calls=%fused_computation.14 | loop fusion | flops 4718592 | bytes 6318080 | tf_op jit(solution)/shard_map/convert_element_type | solution.py:122
  73.1 1.9 collective-permute-start.5
  75.0 16.1 %all-gather.4.cloned.1.call-done = bf16[32,195,384]{2,1,0:T(8,128)(2,1)} async-done(((bf16[1,195,384]{2,1,0:T(8,128)(2,1)}), bf16[32,195,384]{2,1,0:T(8,128)(2,1)}) %all-gather.4.cloned.1.call-update) | async-done | bytes 4792336 | tf_op jit(solution)/shard_map/all_gather | solution.py:28
  91.1 2.9 %fusion.47 = (bf16[32,96,384]{2,1,0:T(8,128)(2,1)S(1)}, bf16[32,96,384]{2,1,0:T(8,128)(2,1)S(1)}) fusion(bf16[32,195,384]{2,1,0:T(8,128)(2,1)} %all-gather.4.cloned.1.call-done), kind=kLoop, calls=%fused_computation.89 | loop fusion | bytes 9437184 | tf_op jit(solution)/shard_map/slice | solution.py:114
  94.0 3.5 %fusion.13 = bf16[512,384]{0,1:T(8,128)(2,1)S(1)} fusion(bf16[3072,384]{1,0:T(8,128)(2,1)S(1)} %bitcast.82, bf16[256,3072]{0,1:T(8,128)(2,1)} %collective-permute-done, bf16[256,3072]{0,1:T(8,128)(2,1)} %bitcast.6, bf16[256,384]{0,1:T(8,128)(2,1)} %collective-permute-done.1, bf16[256,384]{0,1:T(8,128)(2,1)S(1)} %copy.52), kind=kOutput, calls=%fused_computation.26 | convolution fusion | flops 1217003520 | bytes 6291456 | tf_op jit(solution)/shard_map/dot_general | solution.py:129
  97.5 1.2 fusion.9
  98.8 1.4 pad_maximum_fusion
  100.2 6.5 %all-to-all-start.1 = ((bf16[16,196,256]{2,1,0:T(8,128)(2,1)}), bf16[16,196,256]{2,1,0:T(8,128)(2,1)S(1)}, u32[]{:S(2)}, u32[]{:S(2)}) async-start(bf16[16,196,256]{2,1,0:T(8,128)(2,1)} %pad_maximum_fusion), calls=%async_computation.1 | async-start | bytes 3276800 | tf_op jit(solution)/shard_map/all_to_all | solution.py:165
  106.8 4.1 %convolution_convert_fusion = bf16[3072,192]{1,0:T(8,128)(2,1)} fusion(bf16[256,3072]{0,1:T(8,128)(2,1)} %collective-permute-done.5, bf16[256,3072]{0,1:T(8,128)(2,1)} %get-tuple-element.37, bf16[512,2,192]{0,2,1:T(8,128)(2,1)S(1)} %bitcast.99, s32[]{:T(128)S(6)} %select_n.24), kind=kOutput, calls=%fused_computation.2 | convolution fusion | flops 610861056 | bytes 4521988 | tf_op jit(solution)/shard_map/dot_general | solution.py:137
  112.5 1.0 slice.132
  113.7 18.5 %all-to-all-done.1 = bf16[16,196,256]{2,1,0:T(8,128)(2,1)S(1)} async-done(((bf16[16,196,256]{2,1,0:T(8,128)(2,1)}), bf16[16,196,256]{2,1,0:T(8,128)(2,1)S(1)}, u32[]{:S(2)}, u32[]{:S(2)}) %all-to-all-start.1) | async-done | bytes 1605664 | tf_op jit(solution)/shard_map/all_to_all | solution.py:165
  132.6 1.1 fusion.34
  134.0 3.3 %collective-permute-start.3 = (bf16[3,64,192]{2,1,0:T(8,128)(2,1)S(1)}, bf16[3,64,192]{2,1,0:T(8,128)(2,1)S(1)}, u32[]{:S(2)}, u32[]{:S(2)}) collective-permute-start(bf16[3,64,192]{2,1,0:T(8,128)(2,1)S(1)} %bitcast.93), channel_id=1, source_target_pairs={{16,0},{32,16},{48,32},{64,48},{80,64},{96,80},{112,96},{128,112},... | collective-permute-start | bytes 221192 | tf_op jit(solution)/shard_map/ppermute | solution.py:180
  137.3 3.2 %collective-permute-start.2 = (bf16[3,64,192]{2,1,0:T(8,128)(2,1)S(1)}, bf16[3,64,192]{2,1,0:T(8,128)(2,1)S(1)}, u32[]{:S(2)}, u32[]{:S(2)}) collective-permute-start(bf16[3,64,192]{2,1,0:T(8,128)(2,1)S(1)} %bitcast.92), channel_id=1, source_target_pairs={{0,16},{16,32},{32,48},{48,64},{64,80},{80,96},{96,112},{112,128},... | collective-permute-start | bytes 221192 | tf_op jit(solution)/shard_map/ppermute | solution.py:179
  141.6 1.3 collective-permute-done.2
  143.8 6.6 %shard_map.137 = (bf16[4,64,192]{2,1,0:T(8,128)(2,1)}, f32[49,8,192]{2,1,0:T(8,128)}) custom-call(bf16[10,70,192]{2,1,0:T(8,128)(2,1)} %fusion.27.tall_ref, bf16[4,64,192]{2,1,0:T(8,128)(2,1)} %bitcast.85, bf16[4,64,192]{2,1,0:T(8,128)(2,1)} %bitcast.84, f32[49,192]{1,0:T(8,128)} %copy.61.kernel_ref), custom_call_target="tpu_custom_call" | custom-call | tf_op jit(solution)/shard_map/pallas_call | solution.py:57
  150.4 1.1 reduce_sum.102
  151.7 1.9 collective-permute-start.4
  153.7 1.2 collective-permute-done.4
  154.9 1.2 slice.114
  156.6 1.2 copy.69
  158.6 7.3 %all-to-all-start.2 = ((f32[16,1,678]{2,1,0:T(1,128)}), f32[16,1,678]{2,1,0:T(1,128)S(1)}, u32[]{:S(2)}, u32[]{:S(2)}) async-start(f32[16,1,678]{2,1,0:T(1,128)} %all_to_all.14), calls=%async_computation.2 | async-start | bytes 98304 | tf_op jit(solution)/shard_map/all_to_all | solution.py:199
  166.7 10.8 %all-to-all-done.2 = f32[16,1,678]{2,1,0:T(1,128)S(1)} async-done(((f32[16,1,678]{2,1,0:T(1,128)}), f32[16,1,678]{2,1,0:T(1,128)S(1)}, u32[]{:S(2)}, u32[]{:S(2)}) %all-to-all-start.2) | async-done | bytes 43424 | tf_op jit(solution)/shard_map/all_to_all | solution.py:199
  178.4 5.6 %collective-permute-start.6 = (bf16[96,192]{1,0:T(8,128)(2,1)S(1)}, bf16[96,192]{1,0:T(8,128)(2,1)S(1)}, u32[]{:S(2)}, u32[]{:S(2)}) collective-permute-start(bf16[96,192]{1,0:T(8,128)(2,1)S(1)} %get-tuple-element.40), channel_id=1, source_target_pairs={{0,16},{16,0},{1,17},{17,1},{2,18},{18,2},{3,19},{19,3},{4,20},{20... | collective-permute-start | bytes 110600 | tf_op jit(solution)/shard_map/ppermute | solution.py:144
  (79 shorter events, 13.0 us)
Async XLA Ops:
  7.2 83.9 %all-gather.4.cloned.1.call-start = ((), (), s32[]{:S(2)}) async-start(), calls=%async_computation.5 | async-start | bytes 5068800 | tf_op jit(solution)/shard_map/all_gather | solution.py:28
  13.7 7.7 %copy-start.1 = (bf16[256,384]{1,0:T(8,128)(2,1)S(1)}, bf16[256,384]{1,0:T(8,128)(2,1)}, u32[]{:S(2)}) copy-start(bf16[256,384]{1,0:T(8,128)(2,1)} %param.12) | copy-start | bytes 589828
  13.7 12.8 %copy-start.4 = (f32[3072]{0:T(1024)S(1)}, f32[3072]{0:T(1024)}, u32[]{:S(2)}) copy-start(f32[3072]{0:T(1024)} %param.15) | copy-start | bytes 36868
  13.7 47.5 %all-to-all-start = ((bf16[16,256,384]{1,2,0:T(8,128)(2,1)}), bf16[16,256,384]{1,2,0:T(8,128)(2,1)S(1)}, u32[]{:S(2)}, u32[]{:S(2)}) async-start(bf16[16,256,384]{1,2,0:T(8,128)(2,1)} %broadcast_in_dim.6), calls=%async_computation | async-start | bytes 6291456 | tf_op jit(solution)/shard_map/all_to_all | solution.py:27
  21.6 72.3 %collective-permute-start.1 = (bf16[256,384]{0,1:T(8,128)(2,1)S(1)}, bf16[256,384]{0,1:T(8,128)(2,1)}, u32[]{:S(2)}, u32[]{:S(2)}) collective-permute-start(bf16[256,384]{0,1:T(8,128)(2,1)S(1)} %copy.52), channel_id=1, source_target_pairs={{0,16},{16,0},{1,17},{17,1},{2,18},{18,2},{3,19},{19,3},{4,20},{20... | collective-permute-start | bytes 589832 | tf_op jit(solution)/shard_map/ppermute | solution.py:128
  26.6 43.4 %copy-start.5 = (f32[3072]{0:T(1024)S(1)}, f32[3072]{0:T(1024)}, u32[]{:S(2)}) copy-start(f32[3072]{0:T(1024)} %param.16) | copy-start | bytes 36868
  62.5 31.4 %collective-permute-start = (bf16[256,3072]{0,1:T(8,128)(2,1)}, bf16[256,3072]{0,1:T(8,128)(2,1)}, u32[]{:S(2)}, u32[]{:S(2)}) collective-permute-start(bf16[256,3072]{0,1:T(8,128)(2,1)} %bitcast.6), channel_id=1, source_target_pairs={{0,16},{16,0},{1,17},{17,1},{2,18},{18,2},{3,19},{19,3},{4,20},{20... | collective-permute-start | bytes 4718600 | tf_op jit(solution)/shard_map/ppermute | solution.py:127
  73.1 33.7 %collective-permute-start.5 = (bf16[256,3072]{0,1:T(8,128)(2,1)}, bf16[256,3072]{0,1:T(8,128)(2,1)}, u32[]{:S(2)}, u32[]{:S(2)}) collective-permute-start(bf16[256,3072]{0,1:T(8,128)(2,1)} %get-tuple-element.37), channel_id=1, source_target_pairs={{0,16},{16,0},{1,17},{17,1},{2,18},{18,2},{3,19},{19,3},{4,20},{20... | collective-permute-start | bytes 4718600 | tf_op jit(solution)/shard_map/ppermute | solution.py:133
  97.5 1.3 copy-start.6
  98.8 8.0 %copy-start.7 = (bf16[512,384]{0,1:T(8,128)(2,1)S(1)}, bf16[512,384]{0,1:T(8,128)(2,1)}, u32[]{:S(2)}) copy-start(bf16[512,384]{0,1:T(8,128)(2,1)} %copy-done.6) | copy-start | bytes 1179652
  100.2 32.0 %all-to-all-start.1 = ((bf16[16,196,256]{2,1,0:T(8,128)(2,1)}), bf16[16,196,256]{2,1,0:T(8,128)(2,1)S(1)}, u32[]{:S(2)}, u32[]{:S(2)}) async-start(bf16[16,196,256]{2,1,0:T(8,128)(2,1)} %pad_maximum_fusion), calls=%async_computation.1 | async-start | bytes 3276800 | tf_op jit(solution)/shard_map/all_to_all | solution.py:165
  106.7 70.9 %reduce-scatter.2.cloned.1.call-start = ((), (), s32[]{:S(2)}) async-start(), calls=%async_computation.4 | async-start | bytes 1671168 | tf_op jit(solution)/shard_map/reduce_scatter | solution.py:141
  106.7 4.1 %copy-start = (bf16[256,192]{0,1:T(8,128)(2,1)S(1)}, bf16[256,192]{0,1:T(8,128)(2,1)}, u32[]{:S(2)}) copy-start(bf16[256,192]{0,1:T(8,128)(2,1)} %param.13) | copy-start | bytes 294916
  106.8 5.0 %copy-start.3 = (bf16[256,192]{0,1:T(8,128)(2,1)S(1)}, bf16[256,192]{0,1:T(8,128)(2,1)}, u32[]{:S(2)}) copy-start(bf16[256,192]{0,1:T(8,128)(2,1)} %param.10) | copy-start | bytes 294916
  134.0 7.6 %collective-permute-start.3 = (bf16[3,64,192]{2,1,0:T(8,128)(2,1)S(1)}, bf16[3,64,192]{2,1,0:T(8,128)(2,1)S(1)}, u32[]{:S(2)}, u32[]{:S(2)}) collective-permute-start(bf16[3,64,192]{2,1,0:T(8,128)(2,1)S(1)} %bitcast.93), channel_id=1, source_target_pairs={{16,0},{32,16},{48,32},{64,48},{80,64},{96,80},{112,96},{128,112},... | collective-permute-start | bytes 221192 | tf_op jit(solution)/shard_map/ppermute | solution.py:180
  137.3 5.7 %collective-permute-start.2 = (bf16[3,64,192]{2,1,0:T(8,128)(2,1)S(1)}, bf16[3,64,192]{2,1,0:T(8,128)(2,1)S(1)}, u32[]{:S(2)}, u32[]{:S(2)}) collective-permute-start(bf16[3,64,192]{2,1,0:T(8,128)(2,1)S(1)} %bitcast.92), channel_id=1, source_target_pairs={{0,16},{16,32},{32,48},{48,64},{64,80},{80,96},{96,112},{112,128},... | collective-permute-start | bytes 221192 | tf_op jit(solution)/shard_map/ppermute | solution.py:179
  150.4 15.5 %copy-start.2 = (bf16[4,64,192]{2,1,0:T(8,128)(2,1)S(1)}, bf16[4,64,192]{2,1,0:T(8,128)(2,1)}, u32[]{:S(2)}) copy-start(bf16[4,64,192]{2,1,0:T(8,128)(2,1)} %get-tuple-element.7) | copy-start | bytes 294916
  151.7 3.1 %collective-permute-start.4 = (f32[9792]{0:T(1024)S(1)}, f32[9792]{0:T(1024)S(1)}, u32[]{:S(2)}, u32[]{:S(2)}) collective-permute-start(f32[9792]{0:T(1024)S(1)} %concatenate.39), channel_id=1, source_target_pairs={{0,16},{16,0},{1,17},{17,1},{2,18},{18,2},{3,19},{19,3},{4,20},{20... | collective-permute-start | bytes 117512 | tf_op jit(solution)/shard_map/ppermute | solution.py:193
  158.6 18.9 %all-to-all-start.2 = ((f32[16,1,678]{2,1,0:T(1,128)}), f32[16,1,678]{2,1,0:T(1,128)S(1)}, u32[]{:S(2)}, u32[]{:S(2)}) async-start(f32[16,1,678]{2,1,0:T(1,128)} %all_to_all.14), calls=%async_computation.2 | async-start | bytes 98304 | tf_op jit(solution)/shard_map/all_to_all | solution.py:199
  178.4 7.0 %collective-permute-start.6 = (bf16[96,192]{1,0:T(8,128)(2,1)S(1)}, bf16[96,192]{1,0:T(8,128)(2,1)S(1)}, u32[]{:S(2)}, u32[]{:S(2)}) collective-permute-start(bf16[96,192]{1,0:T(8,128)(2,1)S(1)} %get-tuple-element.40), channel_id=1, source_target_pairs={{0,16},{16,0},{1,17},{17,1},{2,18},{18,2},{3,19},{19,3},{4,20},{20... | collective-permute-start | bytes 110600 | tf_op jit(solution)/shard_map/ppermute | solution.py:144
Sparse Core Ops, SparseCore 0:
  10.1 80.9 all-gather.3
  111.0 58.9 reduce-scatter.1

commit v12 on v11

--- a/solution.py
+++ b/solution.py
@@ -191,17 +191,14 @@
     n_chip = n_row // 2
     partials = jnp.concatenate([kernel_sums.reshape(-1), gain_part, bias_part])
     partials = partials + lax.ppermute(partials, "core", SWAP)
-    kernel_chip = partials[: KS * KS * channels].reshape(KS * KS, n_chip, 2, few)
-    kernel_chip = lax.dynamic_index_in_dim(kernel_chip, core, axis=2, keepdims=False)
-    kernel_chip = jnp.transpose(kernel_chip, (1, 0, 2)).reshape(n_chip, KS * KS * few)
-    norm_chip = jnp.broadcast_to(partials[None, KS * KS * channels :], (n_chip, 2 * channels))
-    reduced = jnp.sum(
-        lax.all_to_all(jnp.concatenate([kernel_chip, norm_chip], axis=1), "z", 0, 0, tiled=True),
-        axis=0,
-    )
-    d_kernel = reduced[: KS * KS * few].reshape(KS * KS, few)
-    d_gain = reduced[KS * KS * few : KS * KS * few + channels]
-    d_bias = reduced[KS * KS * few + channels :]
+    step = 1
+    while step < n_chip:
+        partials = partials + lax.ppermute(partials, "z", [(i, i ^ step) for i in range(n_chip)])
+        step *= 2
+    kernel_total = partials[: KS * KS * channels].reshape(KS * KS, channels)
+    d_kernel = lax.dynamic_slice_in_dim(kernel_total, row_rank * few, few, 1)
+    d_gain = partials[KS * KS * channels : KS * KS * channels + channels]
+    d_bias = partials[KS * KS * channels + channels :]
     return (d_input, d_kernel, d_gain, d_bias, d_w_in)
 
 

time: 194 us -> 207 us (1.067)
  starting transfers between devices: 49 us -> 62.4 us
  local copies, waits for them, and re-layouts: 17.7 us -> 14.9 us
  waiting for transfers between devices: 82.5 us -> 85.3 us
    ppermute x0 -> x4, starting transfers between devices: none -> 19.8 us  [body(): lax.ppermute(partials, 'z', [(i, i ^ step) for i in range(n_chip)])]
    ppermute x0 -> x4, waiting for transfers between devices: none -> 13.5 us  [body(): lax.ppermute(partials, 'z', [(i, i ^ step) for i in range(n_chip)])]
    all_to_all x1 -> x0, waiting for transfers between devices: 10.8 us -> none  [body(): lax.all_to_all(jnp.concatenate([kernel_chip, norm_chip], axis=1), 'z', 0,...]
    all_to_all x1 -> x0, starting transfers between devices: 7.34 us -> none  [body(): lax.all_to_all(jnp.concatenate([kernel_chip, norm_chip], axis=1), 'z', 0,...]
  transfers between devices with their start and end apart: 12 -> 15, of which waited for: 6 -> 10; matrix products, arithmetic and copies ran while one was open for 18% -> 16% of each run, Pallas kernels for 3% -> 3%
where the time goes in v12:
time: 207 us; the launch traced here: 206 us
  waiting for transfers between devices  85.3 us (41%)
  starting transfers between devices  62.4 us (30%)
  local copies, waits for them, and re-layouts  14.9 us (7%)
  between operations  14.5 us (7%)
  other arithmetic  13.8 us (7%)
  matrix products  8.81 us (4%)
  Pallas kernels  6.63 us (3%)
    all_to_all x1, waiting for transfers between devices, gather_blocks(): return lax.all_to_all(wide, axis_name, 0, 0, tiled=True)  34.6 us
    ppermute x4, starting transfers between devices, body(): lax.ppermute(partials, 'z', [(i, i ^ step) for i in range(n_chip)])  19.8 us
    all_to_all x1, waiting for transfers between devices, body(): incoming = lax.all_to_all(outgoing, 'col', 0, 0, tiled=True)  18.5 us
    all_gather x1, waiting for transfers between devices, gather_blocks(): return lax.all_gather(x, axis_name, axis=0, tiled=False)  16.1 us
    ppermute x4, waiting for transfers between devices, body(): lax.ppermute(partials, 'z', [(i, i ^ step) for i in range(n_chip)])  13.5 us
    all_to_all x1, starting transfers between devices, gather_blocks(): return lax.all_to_all(wide, axis_name, 0, 0, tiled=True)  7.72 us
    pallas_call x1, Pallas kernels, conv_call(): pl.pallas_call(conv_body, out_shape=(jax.ShapeDtypeStruct((rows, span, ch...  6.63 us
    ppermute x1, starting transfers between devices, body(): lax.ppermute(scaled_full, 'core', SWAP)  6.57 us
  transfers between devices with their start and end apart: 15, of which 10 were waited for; matrix products, arithmetic and copies ran while one was open for 16% of the time, Pallas kernels for 3%

profile of v12, /device:TPU:1, one launch (start us, length us, event | category | flops | bytes accessed | tf_op | source)
XLA Modules:
  0.0 206.3 jit_solution(2395291920941202900)
XLA Ops:
  8.2 1.6 maximum_bitcast_fusion
  11.8 2.0 broadcast_in_dim.4
  13.7 7.7 %all-to-all-start = ((bf16[16,256,384]{1,2,0:T(8,128)(2,1)}), bf16[16,256,384]{1,2,0:T(8,128)(2,1)S(1)}, u32[]{:S(2)}, u32[]{:S(2)}) async-start(bf16[16,256,384]{1,2,0:T(8,128)(2,1)} %broadcast_in_dim.4), calls=%async_computation | async-start | bytes 6291456 | tf_op jit(solution)/shard_map/all_to_all | solution.py:27
  21.6 4.9 %collective-permute-start.1 = (bf16[256,384]{0,1:T(8,128)(2,1)S(1)}, bf16[256,384]{0,1:T(8,128)(2,1)}, u32[]{:S(2)}, u32[]{:S(2)}) collective-permute-start(bf16[256,384]{0,1:T(8,128)(2,1)S(1)} %copy.36), channel_id=1, source_target_pairs={{0,16},{16,0},{1,17},{17,1},{2,18},{18,2},{3,19},{19,3},{4,20},{20... | collective-permute-start | bytes 589832 | tf_op jit(solution)/shard_map/ppermute | solution.py:128
  26.7 34.6 %all-to-all-done = bf16[16,256,384]{1,2,0:T(8,128)(2,1)S(1)} async-done(((bf16[16,256,384]{1,2,0:T(8,128)(2,1)}), bf16[16,256,384]{1,2,0:T(8,128)(2,1)S(1)}, u32[]{:S(2)}, u32[]{:S(2)}) %all-to-all-start) | async-done | bytes 3145760 | tf_op jit(solution)/shard_map/all_to_all | solution.py:27
  61.2 1.4 slice.105
  62.6 6.6 %collective-permute-start = (bf16[256,3072]{0,1:T(8,128)(2,1)}, bf16[256,3072]{0,1:T(8,128)(2,1)}, u32[]{:S(2)}, u32[]{:S(2)}) collective-permute-start(bf16[256,3072]{0,1:T(8,128)(2,1)} %bitcast.6), channel_id=1, source_target_pairs={{0,16},{16,0},{1,17},{17,1},{2,18},{18,2},{3,19},{19,3},{4,20},{20... | collective-permute-start | bytes 4718600 | tf_op jit(solution)/shard_map/ppermute | solution.py:127
  70.1 3.0 %add_convert_fusion = (bf16[256,3072]{0,1:T(8,128)(2,1)}, f32[256,3072]{0,1:T(8,128)}) fusion(f32[3072]{0:T(1024)S(1)} %copy-done.4, f32[3072]{0:T(1024)S(1)} %copy-done.3, f32[256]{0:T(256)S(1)} %add_rsqrt_fusion, f32[256]{0:T(256)S(1)} %broadcast_multiply_fusion, bf16[16,256,384]{1,2,0:T(8,128)(2,1)S(1)} %all-to-all-done), kind=kLoop, calls=%fused_computation.14 | loop fusion | flops 4718592 | bytes 6318080 | tf_op jit(solution)/shard_map/convert_element_type | solution.py:122
  73.1 1.9 collective-permute-start.9
  75.0 16.1 %all-gather.4.cloned.1.call-done = bf16[32,195,384]{2,1,0:T(8,128)(2,1)} async-done(((bf16[1,195,384]{2,1,0:T(8,128)(2,1)}), bf16[32,195,384]{2,1,0:T(8,128)(2,1)}) %all-gather.4.cloned.1.call-update) | async-done | bytes 4792336 | tf_op jit(solution)/shard_map/all_gather | solution.py:28
  91.1 2.9 %fusion.47 = (bf16[32,96,384]{2,1,0:T(8,128)(2,1)S(1)}, bf16[32,96,384]{2,1,0:T(8,128)(2,1)S(1)}) fusion(bf16[32,195,384]{2,1,0:T(8,128)(2,1)} %all-gather.4.cloned.1.call-done), kind=kLoop, calls=%fused_computation.88 | loop fusion | bytes 9437184 | tf_op jit(solution)/shard_map/slice | solution.py:114
  94.0 3.5 %fusion.13 = bf16[512,384]{0,1:T(8,128)(2,1)S(1)} fusion(bf16[3072,384]{1,0:T(8,128)(2,1)S(1)} %bitcast.77, bf16[256,3072]{0,1:T(8,128)(2,1)} %collective-permute-done, bf16[256,3072]{0,1:T(8,128)(2,1)} %bitcast.6, bf16[256,384]{0,1:T(8,128)(2,1)} %collective-permute-done.1, bf16[256,384]{0,1:T(8,128)(2,1)S(1)} %copy.36), kind=kOutput, calls=%fused_computation.26 | convolution fusion | flops 1217003520 | bytes 6291456 | tf_op jit(solution)/shard_map/dot_general | solution.py:129
  97.5 1.2 fusion.9
  98.8 1.4 pad_maximum_fusion
  100.2 6.5 %all-to-all-start.1 = ((bf16[16,196,256]{2,1,0:T(8,128)(2,1)}), bf16[16,196,256]{2,1,0:T(8,128)(2,1)S(1)}, u32[]{:S(2)}, u32[]{:S(2)}) async-start(bf16[16,196,256]{2,1,0:T(8,128)(2,1)} %pad_maximum_fusion), calls=%async_computation.1 | async-start | bytes 3276800 | tf_op jit(solution)/shard_map/all_to_all | solution.py:165
  106.8 4.1 %convolution_convert_fusion = bf16[3072,192]{1,0:T(8,128)(2,1)} fusion(bf16[256,3072]{0,1:T(8,128)(2,1)} %collective-permute-done.9, bf16[256,3072]{0,1:T(8,128)(2,1)} %get-tuple-element.32, bf16[512,2,192]{0,2,1:T(8,128)(2,1)S(1)} %bitcast.93, s32[]{:T(128)S(6)} %select_n.27), kind=kOutput, calls=%fused_computation.2 | convolution fusion | flops 610861056 | bytes 4521988 | tf_op jit(solution)/shard_map/dot_general | solution.py:137
  113.8 18.5 %all-to-all-done.1 = bf16[16,196,256]{2,1,0:T(8,128)(2,1)S(1)} async-done(((bf16[16,196,256]{2,1,0:T(8,128)(2,1)}), bf16[16,196,256]{2,1,0:T(8,128)(2,1)S(1)}, u32[]{:S(2)}, u32[]{:S(2)}) %all-to-all-start.1) | async-done | bytes 1605664 | tf_op jit(solution)/shard_map/all_to_all | solution.py:165
  134.1 3.3 %collective-permute-start.3 = (bf16[3,64,192]{2,1,0:T(8,128)(2,1)S(1)}, bf16[3,64,192]{2,1,0:T(8,128)(2,1)S(1)}, u32[]{:S(2)}, u32[]{:S(2)}) collective-permute-start(bf16[3,64,192]{2,1,0:T(8,128)(2,1)S(1)} %bitcast.87), channel_id=1, source_target_pairs={{16,0},{32,16},{48,32},{64,48},{80,64},{96,80},{112,96},{128,112},... | collective-permute-start | bytes 221192 | tf_op jit(solution)/shard_map/ppermute | solution.py:180
  137.3 3.2 %collective-permute-start.2 = (bf16[3,64,192]{2,1,0:T(8,128)(2,1)S(1)}, bf16[3,64,192]{2,1,0:T(8,128)(2,1)S(1)}, u32[]{:S(2)}, u32[]{:S(2)}) collective-permute-start(bf16[3,64,192]{2,1,0:T(8,128)(2,1)S(1)} %bitcast.86), channel_id=1, source_target_pairs={{0,16},{16,32},{32,48},{48,64},{64,80},{80,96},{96,112},{112,128},... | collective-permute-start | bytes 221192 | tf_op jit(solution)/shard_map/ppermute | solution.py:179
  141.6 1.3 collective-permute-done.2
  143.8 6.6 %shard_map.137 = (bf16[4,64,192]{2,1,0:T(8,128)(2,1)}, f32[49,8,192]{2,1,0:T(8,128)}) custom-call(bf16[10,70,192]{2,1,0:T(8,128)(2,1)} %fusion.27.tall_ref, bf16[4,64,192]{2,1,0:T(8,128)(2,1)} %bitcast.79, bf16[4,64,192]{2,1,0:T(8,128)(2,1)} %bitcast.78, f32[49,192]{1,0:T(8,128)} %copy.45.kernel_ref), custom_call_target="tpu_custom_call" | custom-call | tf_op jit(solution)/shard_map/pallas_call | solution.py:57
  151.7 1.9 collective-permute-start.4
  154.8 4.1 %collective-permute-start.5 = (f32[9792]{0:T(1024)S(1)}, f32[9792]{0:T(1024)S(1)}, u32[]{:S(2)}, u32[]{:S(2)}) collective-permute-start(f32[9792]{0:T(1024)S(1)} %add.98), channel_id=1, source_target_pairs={{0,32},{32,0},{64,96},{96,64},{128,160},{160,128},{192,224},{224,1... | collective-permute-start | bytes 117512 | tf_op jit(solution)/shard_map/ppermute | solution.py:196
  159.0 2.7 %collective-permute-done.5 = f32[9792]{0:T(1024)S(1)} collective-permute-done((f32[9792]{0:T(1024)S(1)}, f32[9792]{0:T(1024)S(1)}, u32[]{:S(2)}, u32[]{:S(2)}) %collective-permute-start.5) | collective-permute-done | bytes 39200 | tf_op jit(solution)/shard_map/ppermute | solution.py:196
  161.6 2.3 %collective-permute-start.6 = (f32[9792]{0:T(1024)S(1)}, f32[9792]{0:T(1024)S(1)}, u32[]{:S(2)}, u32[]{:S(2)}) collective-permute-start(f32[9792]{0:T(1024)S(1)} %add.99), channel_id=1, source_target_pairs={{0,64},{32,96},{64,0},{96,32},{128,192},{160,224},{192,128},{224,1... | collective-permute-start | bytes 117512 | tf_op jit(solution)/shard_map/ppermute | solution.py:196
  163.9 3.3 %collective-permute-done.6 = f32[9792]{0:T(1024)S(1)} collective-permute-done((f32[9792]{0:T(1024)S(1)}, f32[9792]{0:T(1024)S(1)}, u32[]{:S(2)}, u32[]{:S(2)}) %collective-permute-start.6) | collective-permute-done | bytes 39200 | tf_op jit(solution)/shard_map/ppermute | solution.py:196
  167.3 6.9 %collective-permute-start.7 = (f32[9792]{0:T(1024)S(1)}, f32[9792]{0:T(1024)S(1)}, u32[]{:S(2)}, u32[]{:S(2)}) collective-permute-start(f32[9792]{0:T(1024)S(1)} %add.100), channel_id=1, source_target_pairs={{0,128},{32,160},{64,192},{96,224},{128,0},{160,32},{192,64},{224,... | collective-permute-start | bytes 117512 | tf_op jit(solution)/shard_map/ppermute | solution.py:196
  174.2 2.2 %collective-permute-done.7 = f32[9792]{0:T(1024)S(1)} collective-permute-done((f32[9792]{0:T(1024)S(1)}, f32[9792]{0:T(1024)S(1)}, u32[]{:S(2)}, u32[]{:S(2)}) %collective-permute-start.7) | collective-permute-done | bytes 39200 | tf_op jit(solution)/shard_map/ppermute | solution.py:196
  176.5 6.5 %collective-permute-start.8 = (f32[9792]{0:T(1024)S(1)}, f32[9792]{0:T(1024)S(1)}, u32[]{:S(2)}, u32[]{:S(2)}) collective-permute-start(f32[9792]{0:T(1024)S(1)} %add.101), channel_id=1, source_target_pairs={{0,256},{32,288},{64,320},{96,352},{128,384},{160,416},{192,448},{... | collective-permute-start | bytes 117512 | tf_op jit(solution)/shard_map/ppermute | solution.py:196
  182.9 1.6 copy.46
  184.6 5.3 %collective-permute-done.8 = f32[9792]{0:T(1024)S(1)} collective-permute-done((f32[9792]{0:T(1024)S(1)}, f32[9792]{0:T(1024)S(1)}, u32[]{:S(2)}, u32[]{:S(2)}) %collective-permute-start.8) | collective-permute-done | bytes 39200 | tf_op jit(solution)/shard_map/ppermute | solution.py:196
  191.5 6.4 %collective-permute-start.10 = (bf16[96,192]{1,0:T(8,128)(2,1)S(1)}, bf16[96,192]{1,0:T(8,128)(2,1)S(1)}, u32[]{:S(2)}, u32[]{:S(2)}) collective-permute-start(bf16[96,192]{1,0:T(8,128)(2,1)S(1)} %get-tuple-element.35), channel_id=1, source_target_pairs={{0,16},{16,0},{1,17},{17,1},{2,18},{18,2},{3,19},{19,3},{4,20},{20... | collective-permute-start | bytes 110600 | tf_op jit(solution)/shard_map/ppermute | solution.py:144
  (77 shorter events, 16.3 us)
Async XLA Ops:
  7.2 83.9 %all-gather.4.cloned.1.call-start = ((), (), s32[]{:S(2)}) async-start(), calls=%async_computation.4 | async-start | bytes 5068800 | tf_op jit(solution)/shard_map/all_gather | solution.py:28
  13.7 7.7 %copy-start.1 = (bf16[256,384]{1,0:T(8,128)(2,1)S(1)}, bf16[256,384]{1,0:T(8,128)(2,1)}, u32[]{:S(2)}) copy-start(bf16[256,384]{1,0:T(8,128)(2,1)} %param.12) | copy-start | bytes 589828
  13.7 12.8 %copy-start.3 = (f32[3072]{0:T(1024)S(1)}, f32[3072]{0:T(1024)}, u32[]{:S(2)}) copy-start(f32[3072]{0:T(1024)} %param.15) | copy-start | bytes 36868
  13.7 47.5 %all-to-all-start = ((bf16[16,256,384]{1,2,0:T(8,128)(2,1)}), bf16[16,256,384]{1,2,0:T(8,128)(2,1)S(1)}, u32[]{:S(2)}, u32[]{:S(2)}) async-start(bf16[16,256,384]{1,2,0:T(8,128)(2,1)} %broadcast_in_dim.4), calls=%async_computation | async-start | bytes 6291456 | tf_op jit(solution)/shard_map/all_to_all | solution.py:27
  21.6 72.3 %collective-permute-start.1 = (bf16[256,384]{0,1:T(8,128)(2,1)S(1)}, bf16[256,384]{0,1:T(8,128)(2,1)}, u32[]{:S(2)}, u32[]{:S(2)}) collective-permute-start(bf16[256,384]{0,1:T(8,128)(2,1)S(1)} %copy.36), channel_id=1, source_target_pairs={{0,16},{16,0},{1,17},{17,1},{2,18},{18,2},{3,19},{19,3},{4,20},{20... | collective-permute-start | bytes 589832 | tf_op jit(solution)/shard_map/ppermute | solution.py:128
  26.7 43.4 %copy-start.4 = (f32[3072]{0:T(1024)S(1)}, f32[3072]{0:T(1024)}, u32[]{:S(2)}) copy-start(f32[3072]{0:T(1024)} %param.16) | copy-start | bytes 36868
  62.6 31.4 %collective-permute-start = (bf16[256,3072]{0,1:T(8,128)(2,1)}, bf16[256,3072]{0,1:T(8,128)(2,1)}, u32[]{:S(2)}, u32[]{:S(2)}) collective-permute-start(bf16[256,3072]{0,1:T(8,128)(2,1)} %bitcast.6), channel_id=1, source_target_pairs={{0,16},{16,0},{1,17},{17,1},{2,18},{18,2},{3,19},{19,3},{4,20},{20... | collective-permute-start | bytes 4718600 | tf_op jit(solution)/shard_map/ppermute | solution.py:127
  73.1 33.7 %collective-permute-start.9 = (bf16[256,3072]{0,1:T(8,128)(2,1)}, bf16[256,3072]{0,1:T(8,128)(2,1)}, u32[]{:S(2)}, u32[]{:S(2)}) collective-permute-start(bf16[256,3072]{0,1:T(8,128)(2,1)} %get-tuple-element.32), channel_id=1, source_target_pairs={{0,16},{16,0},{1,17},{17,1},{2,18},{18,2},{3,19},{19,3},{4,20},{20... | collective-permute-start | bytes 4718600 | tf_op jit(solution)/shard_map/ppermute | solution.py:133
  97.5 1.3 copy-start.5
  98.8 8.0 %copy-start.6 = (bf16[512,384]{0,1:T(8,128)(2,1)S(1)}, bf16[512,384]{0,1:T(8,128)(2,1)}, u32[]{:S(2)}) copy-start(bf16[512,384]{0,1:T(8,128)(2,1)} %copy-done.5) | copy-start | bytes 1179652
  100.2 32.1 %all-to-all-start.1 = ((bf16[16,196,256]{2,1,0:T(8,128)(2,1)}), bf16[16,196,256]{2,1,0:T(8,128)(2,1)S(1)}, u32[]{:S(2)}, u32[]{:S(2)}) async-start(bf16[16,196,256]{2,1,0:T(8,128)(2,1)} %pad_maximum_fusion), calls=%async_computation.1 | async-start | bytes 3276800 | tf_op jit(solution)/shard_map/all_to_all | solution.py:165
  106.7 83.9 %reduce-scatter.2.cloned.1.call-start = ((), (), s32[]{:S(2)}) async-start(), calls=%async_computation.3 | async-start | bytes 1671168 | tf_op jit(solution)/shard_map/reduce_scatter | solution.py:141
  106.8 4.1 %copy-start = (bf16[256,192]{0,1:T(8,128)(2,1)S(1)}, bf16[256,192]{0,1:T(8,128)(2,1)}, u32[]{:S(2)}) copy-start(bf16[256,192]{0,1:T(8,128)(2,1)} %param.13) | copy-start | bytes 294916
  106.8 5.0 %copy-start.2 = (bf16[256,192]{0,1:T(8,128)(2,1)S(1)}, bf16[256,192]{0,1:T(8,128)(2,1)}, u32[]{:S(2)}) copy-start(bf16[256,192]{0,1:T(8,128)(2,1)} %param.10) | copy-start | bytes 294916
  134.1 7.5 %collective-permute-start.3 = (bf16[3,64,192]{2,1,0:T(8,128)(2,1)S(1)}, bf16[3,64,192]{2,1,0:T(8,128)(2,1)S(1)}, u32[]{:S(2)}, u32[]{:S(2)}) collective-permute-start(bf16[3,64,192]{2,1,0:T(8,128)(2,1)S(1)} %bitcast.87), channel_id=1, source_target_pairs={{16,0},{32,16},{48,32},{64,48},{80,64},{96,80},{112,96},{128,112},... | collective-permute-start | bytes 221192 | tf_op jit(solution)/shard_map/ppermute | solution.py:180
  137.3 5.6 %collective-permute-start.2 = (bf16[3,64,192]{2,1,0:T(8,128)(2,1)S(1)}, bf16[3,64,192]{2,1,0:T(8,128)(2,1)S(1)}, u32[]{:S(2)}, u32[]{:S(2)}) collective-permute-start(bf16[3,64,192]{2,1,0:T(8,128)(2,1)S(1)} %bitcast.86), channel_id=1, source_target_pairs={{0,16},{16,32},{32,48},{48,64},{64,80},{80,96},{96,112},{112,128},... | collective-permute-start | bytes 221192 | tf_op jit(solution)/shard_map/ppermute | solution.py:179
  151.7 3.1 %collective-permute-start.4 = (f32[9792]{0:T(1024)S(1)}, f32[9792]{0:T(1024)S(1)}, u32[]{:S(2)}, u32[]{:S(2)}) collective-permute-start(f32[9792]{0:T(1024)S(1)} %concatenate.36), channel_id=1, source_target_pairs={{0,16},{16,0},{1,17},{17,1},{2,18},{18,2},{3,19},{19,3},{4,20},{20... | collective-permute-start | bytes 117512 | tf_op jit(solution)/shard_map/ppermute | solution.py:193
  154.8 6.8 %collective-permute-start.5 = (f32[9792]{0:T(1024)S(1)}, f32[9792]{0:T(1024)S(1)}, u32[]{:S(2)}, u32[]{:S(2)}) collective-permute-start(f32[9792]{0:T(1024)S(1)} %add.98), channel_id=1, source_target_pairs={{0,32},{32,0},{64,96},{96,64},{128,160},{160,128},{192,224},{224,1... | collective-permute-start | bytes 117512 | tf_op jit(solution)/shard_map/ppermute | solution.py:196
  161.6 5.7 %collective-permute-start.6 = (f32[9792]{0:T(1024)S(1)}, f32[9792]{0:T(1024)S(1)}, u32[]{:S(2)}, u32[]{:S(2)}) collective-permute-start(f32[9792]{0:T(1024)S(1)} %add.99), channel_id=1, source_target_pairs={{0,64},{32,96},{64,0},{96,32},{128,192},{160,224},{192,128},{224,1... | collective-permute-start | bytes 117512 | tf_op jit(solution)/shard_map/ppermute | solution.py:196
  167.3 9.2 %collective-permute-start.7 = (f32[9792]{0:T(1024)S(1)}, f32[9792]{0:T(1024)S(1)}, u32[]{:S(2)}, u32[]{:S(2)}) collective-permute-start(f32[9792]{0:T(1024)S(1)} %add.100), channel_id=1, source_target_pairs={{0,128},{32,160},{64,192},{96,224},{128,0},{160,32},{192,64},{224,... | collective-permute-start | bytes 117512 | tf_op jit(solution)/shard_map/ppermute | solution.py:196
  176.5 13.4 %collective-permute-start.8 = (f32[9792]{0:T(1024)S(1)}, f32[9792]{0:T(1024)S(1)}, u32[]{:S(2)}, u32[]{:S(2)}) collective-permute-start(f32[9792]{0:T(1024)S(1)} %add.101), channel_id=1, source_target_pairs={{0,256},{32,288},{64,320},{96,352},{128,384},{160,416},{192,448},{... | collective-permute-start | bytes 117512 | tf_op jit(solution)/shard_map/ppermute | solution.py:196
  191.5 7.3 %collective-permute-start.10 = (bf16[96,192]{1,0:T(8,128)(2,1)S(1)}, bf16[96,192]{1,0:T(8,128)(2,1)S(1)}, u32[]{:S(2)}, u32[]{:S(2)}) collective-permute-start(bf16[96,192]{1,0:T(8,128)(2,1)S(1)} %get-tuple-element.35), channel_id=1, source_target_pairs={{0,16},{16,0},{1,17},{17,1},{2,18},{18,2},{3,19},{19,3},{4,20},{20... | collective-permute-start | bytes 110600 | tf_op jit(solution)/shard_map/ppermute | solution.py:144
Sparse Core Ops, SparseCore 0:
  10.1 80.9 all-gather.3
  111.1 59.0 reduce-scatter.1
